TPU v7x, 32 devices: a whole 2x2x4 slice. The times are simulated.
32 devices in a mesh: surf: 8 (over z, y), vol: 4 (over x, core).
Axes of the slice: x: 2, y: 2, z: 4, core: 2. Of those that a mesh axis runs over, the one named last changes fastest.
Arguments:
- casting: bfloat16 [32768, 128], P(('surf', 'vol')), may hold values from -5 to 5, as said below
- owner: int32 [32768, 1], P(('surf', 'vol')), may hold values from 0 to 31; in each aligned block of 1024 rows (0 to 1023, 1024 to 2047, ...) at most 128 rows name the same one
- face_id: int32 [32768], P(('surf', 'vol')), may hold values from 0 to 2047
- mold_faces: bfloat16 [65536, 128], P(('surf', 'vol')), may hold values from -5 to 5, as said below
- mortar_d: bfloat16 [64, 64], replicated, may hold values from -0.75 to 0.75
- mortar_m: bfloat16 [64, 64], replicated, may hold values from -0.75 to 0.75
- conduct: bfloat16 [128, 128], replicated, may hold values from -0.5 to 0.5
- volume: bfloat16 [65536, 128], P(('surf', 'vol')), may hold values from -6 to 6
Outputs:
- casting_out: bfloat16 [32768, 128], P(('surf', 'vol'))
- mold_out: bfloat16 [65536, 128], P(('surf', 'vol'))
Inputs may be any that keep to these rules, and one draw needn't show every extreme that they name: Among the 1024 rows of one device no owner is named more than 128 times, a bound that some block reaches. `casting`: temperatures lie within -5 to 5; conductances lie within 0.3 to 3. `mold_faces`: temperatures lie within -5 to 5; area weights lie within 0.3 to 3.
All inputs are finite; a program needn't handle non-finite values.
Results may differ from a plain program's by a relative error of at most 0.0055.
Values may be sent and summed in bfloat16 or wider, within the bound.
No kernel may reach another device: no remote copies, remote signals or barrier semaphores. Data moves between devices by JAX's collectives and lax.ppermute only.
A program may use at most 64 MiB of HBM per device.

v0:
```python
import math

import jax
import jax.numpy as jnp
from jax import lax
from jax.sharding import PartitionSpec as P

relax = 0.5


def contact(rows, mold_rows, stacked, joined, node_count):
    pair_rows = jnp.concatenate([rows[:, :node_count], mold_rows[:, :node_count]], axis=1)
    gap_jump = jnp.dot(pair_rows, stacked, preferred_element_type=jnp.float32)
    heat_flux = (
        rows[:, node_count:].astype(jnp.float32)
        * mold_rows[:, node_count:].astype(jnp.float32)
        * gap_jump
    ).astype(jnp.bfloat16)
    projected = jnp.dot(heat_flux, joined, preferred_element_type=jnp.float32)
    answer = jnp.concatenate([projected[:, :node_count], gap_jump], axis=1).astype(jnp.bfloat16)
    gained = projected[:, node_count:].astype(jnp.bfloat16)
    return (answer, gained)


def local(casting, owner, face_id, mold_faces, mortar_d, mortar_m, conduct, volume):
    seg_rows, row_width = casting.shape
    node_count = mortar_d.shape[0]
    face_rows = mold_faces.shape[0]
    surf_count = lax.axis_size("surf")
    vol_count = lax.axis_size("vol")
    devices = surf_count * vol_count
    capacity = 4 * seg_rows // devices
    slots = devices * capacity
    target = owner[:, 0]
    hits = (target[:, None] == jnp.arange(devices, dtype=jnp.int32)[None, :]).astype(jnp.int32)
    position = jnp.sum((jnp.cumsum(hits, axis=0) - 1) * hits, axis=1)
    slot_index = target * capacity + position
    send_ids = jnp.full((slots,), -1, jnp.int32).at[slot_index].set(face_id)
    block_rows = math.gcd(512, slots)
    turns = slots // block_rows
    stacked = jnp.concatenate([mortar_d.T, -mortar_m.T], axis=0)
    joined = jnp.concatenate([mortar_d, mortar_m], axis=1)
    face_range = jnp.arange(face_rows, dtype=jnp.int32)
    send_rows = jnp.zeros((slots, row_width), jnp.bfloat16).at[slot_index].set(casting)
    got_rows, got_ids = (
        lax.all_to_all(
            send_rows.reshape(devices, capacity, row_width),
            ("surf", "vol"),
            split_axis=0,
            concat_axis=0,
            tiled=True,
        ),
        lax.all_to_all(
            send_ids.reshape(devices, capacity),
            ("surf", "vol"),
            split_axis=0,
            concat_axis=0,
            tiled=True,
        ),
    )
    flat_rows = got_rows.reshape(turns, block_rows, row_width)
    flat_ids = got_ids.reshape(turns, block_rows)

    def settle(totals, pieces):
        rows, row_ids = pieces
        selector = (row_ids[:, None] == face_range[None, :]).astype(jnp.bfloat16)
        mold_rows = jnp.dot(selector, mold_faces, preferred_element_type=jnp.float32).astype(
            jnp.bfloat16
        )
        answer, gained = contact(rows, mold_rows, stacked, joined, node_count)
        totals = totals + lax.dot_general(
            selector, gained, (((0,), (0,)), ((), ())), preferred_element_type=jnp.float32
        )
        return (totals, answer)

    totals, answers = lax.scan(
        settle, jnp.zeros((face_rows, node_count), jnp.float32), (flat_rows, flat_ids)
    )
    returned = lax.all_to_all(
        answers.reshape(devices, capacity, row_width),
        ("surf", "vol"),
        split_axis=0,
        concat_axis=0,
        tiled=True,
    )
    casting_out = returned.reshape(slots, row_width)[slot_index]
    face_totals = totals.astype(jnp.bfloat16)
    quarter = face_rows // vol_count
    relaid = lax.all_to_all(
        face_totals.reshape(vol_count, quarter * node_count // row_width, row_width),
        "vol",
        split_axis=0,
        concat_axis=0,
        tiled=True,
    )
    heat = jnp.dot(volume, conduct, preferred_element_type=jnp.float32)
    placed = relaid.reshape(face_rows, node_count).astype(jnp.float32)
    inject = jnp.concatenate([placed, jnp.zeros((face_rows, node_count), jnp.float32)], axis=1)
    mold_out = (volume.astype(jnp.float32) + relax * (inject - heat)).astype(jnp.bfloat16)
    return (casting_out, mold_out)


def solution(mesh):
    return jax.shard_map(
        local,
        mesh=mesh,
        in_specs=(
            P(("surf", "vol"), None),
            P(("surf", "vol"), None),
            P(("surf", "vol")),
            P(("surf", "vol"), None),
            P(),
            P(),
            P(),
            P(("surf", "vol"), None),
        ),
        out_specs=(P(("surf", "vol"), None), P(("surf", "vol"), None)),
        check_vma=False,
    )
```

profile of v0, /device:TPU:0, one launch (start us, length us, event | category | flops | bytes accessed | tf_op | source)
XLA Modules:
  0.0 131.0 jit_solution(7700214398383684304)
XLA Ops:
  0.7 0.8 fusion.23
  1.4 9.0 %reduce-window.6 = s32[32,8,128]{2,1,0:T(8,128)S(1)} reduce-window(s32[32,8,128]{2,1,0:T(8,128)S(1)} %fusion.23, s32[]{:T(128)} %constant.13.clone.1), window={size=1x1x128 pad=0_0x0_0x127_0}, to_apply=%region_0.0 | reduce-window | flops 4161536 | bytes 262148 | tf_op jit(solution)/shard_map/reduce-window
  11.0 5.1 %scatter_custom_fusion = s32[4096]{0:T(1024)} fusion(s32[1024]{0:T(1024)S(1)} %bitcast.65, s32[1024]{0:T(1024)} %param.12, s32[]{:T(128)} %constant.20.clone.1), kind=kCustom, calls=%fused_computation.44 | custom fusion | bytes 16896 | tf_op jit(solution)/shard_map/scatter | solution.py:38
  16.0 7.3 %all-to-all-start = ((s32[32,1,128]{2,1,0:T(1,128)}), s32[32,1,128]{2,1,0:T(1,128)S(1)}, u32[]{:S(2)}, u32[]{:S(2)}) async-start(s32[32,1,128]{2,1,0:T(1,128)} %bitcast.6), calls=%async_computation | async-start | bytes 32768 | tf_op jit(solution)/shard_map/all_to_all | solution.py:53
  23.3 4.7 %scatter_custom_fusion.1 = bf16[4096,128]{1,0:T(8,128)(2,1)} fusion(s32[1024]{0:T(1024)S(1)} %bitcast.66, bf16[1024,128]{1,0:T(8,128)(2,1)} %param.10, bf16[]{:T(256)} %constant.15.clone.1), kind=kCustom, calls=%fused_computation.31 | custom fusion | bytes 1049088 | tf_op jit(solution)/shard_map/scatter | solution.py:44
  28.0 2.4 %all-to-all-done = s32[32,1,128]{2,1,0:T(1,128)S(1)} async-done(((s32[32,1,128]{2,1,0:T(1,128)}), s32[32,1,128]{2,1,0:T(1,128)S(1)}, u32[]{:S(2)}, u32[]{:S(2)}) %all-to-all-start) | async-done | bytes 16416 | tf_op jit(solution)/shard_map/all_to_all | solution.py:53
  30.5 3.4 %all-to-all-start.1 = ((bf16[32,128,128]{2,1,0:T(8,128)(2,1)}), bf16[32,128,128]{2,1,0:T(8,128)(2,1)S(1)}, u32[]{:S(2)}, u32[]{:S(2)}) async-start(bf16[32,128,128]{2,1,0:T(8,128)(2,1)} %bitcast.7), calls=%async_computation.1 | async-start | bytes 2097152 | tf_op jit(solution)/shard_map/all_to_all | solution.py:46
  34.2 0.5 broadcast.60
  34.8 0.7 reduce.3
  35.5 24.6 %all-to-all-done.1 = bf16[32,128,128]{2,1,0:T(8,128)(2,1)S(1)} async-done(((bf16[32,128,128]{2,1,0:T(8,128)(2,1)}), bf16[32,128,128]{2,1,0:T(8,128)(2,1)S(1)}, u32[]{:S(2)}, u32[]{:S(2)}) %all-to-all-start.1) | async-done | bytes 1048608 | tf_op jit(solution)/shard_map/all_to_all | solution.py:46
  60.1 28.5 %while.13 = (s32[]{:T(128)}, f32[2048,64]{0,1:T(8,128)S(1)}, bf16[8,512,128]{2,1,0:T(8,128)(2,1)}, s32[8,512]{1,0:T(8,128)S(1)}, bf16[8,512,128]{2,1,0:T(8,128)(...) while((s32[]{:T(128)}, f32[2048,64]{0,1:T(8,128)S(1)}, ...), condition=%wide.region_6.7_spmd.clone, body=%wide.region_5.6_spmd.clone.sunk | while | flops 422641664 | bytes 4366467 | solution.py:76
  60.1 1.1 fusion.44
  62.0 1.0 fusion.46
  63.0 0.7 constant_dynamic-update-slice_fusion.2
  63.7 1.1 fusion.44
  65.5 1.0 fusion.46
  66.6 0.7 constant_dynamic-update-slice_fusion.2
  67.2 1.1 fusion.44
  68.7 0.2 convolution_convert_fusion.2
  69.1 1.0 fusion.46
  70.1 0.7 constant_dynamic-update-slice_fusion.2
  70.8 1.1 fusion.44
  72.3 0.2 convolution_convert_fusion.2
  72.7 1.0 fusion.46
  73.7 0.7 constant_dynamic-update-slice_fusion.2
  74.4 1.1 fusion.44
  75.8 0.2 convolution_convert_fusion.2
  76.3 1.0 fusion.46
  77.3 0.7 constant_dynamic-update-slice_fusion.2
  77.9 1.1 fusion.44
  79.4 0.2 convolution_convert_fusion.2
  79.8 1.0 fusion.46
  80.8 0.7 constant_dynamic-update-slice_fusion.2
  81.5 1.1 fusion.44
  83.0 0.2 convolution_convert_fusion.2
  83.4 1.0 fusion.46
  84.4 0.7 constant_dynamic-update-slice_fusion.2
  85.1 1.1 fusion.44
  86.9 1.0 fusion.46
  88.0 0.7 constant_dynamic-update-slice_fusion.2
  88.7 0.3 copy.25
  89.0 0.3 reshape.89
  89.2 8.5 %all_to_all.24 = bf16[4,256,128]{2,1,0:T(8,128)(2,1)S(1)} all-to-all(bf16[4,256,128]{2,1,0:T(8,128)(2,1)S(1)} %reshape.89), channel_id=1, replica_groups=mesh['surf'=8,'vol'=4] {'vol'}, dimensions={0} | all-to-all | bytes 524288 | tf_op jit(solution)/shard_map/all_to_all | solution.py:89
  97.8 2.8 %all-to-all-start.2 = ((bf16[32,128,128]{2,1,0:T(8,128)(2,1)}), bf16[32,128,128]{2,1,0:T(8,128)(2,1)S(1)}, u32[]{:S(2)}, u32[]{:S(2)}) async-start(bf16[32,128,128]{2,1,0:T(8,128)(2,1)} %bitcast.11), calls=%async_computation.2 | async-start | bytes 2097152 | tf_op jit(solution)/shard_map/all_to_all | solution.py:79
  100.6 0.2 convert_element_type.43
  100.8 1.1 fusion.18
  102.0 24.8 %all-to-all-done.2 = bf16[32,128,128]{2,1,0:T(8,128)(2,1)S(1)} async-done(((bf16[32,128,128]{2,1,0:T(8,128)(2,1)}), bf16[32,128,128]{2,1,0:T(8,128)(2,1)S(1)}, u32[]{:S(2)}, u32[]{:S(2)}) %all-to-all-start.2) | async-done | bytes 1048608 | tf_op jit(solution)/shard_map/all_to_all | solution.py:79
  126.7 4.3 %gather_fusion = bf16[1024,128]{1,0:T(8,128)(2,1)} fusion(bf16[4096,128]{1,0:T(8,128)(2,1)S(1)} %bitcast.55, s32[1024]{0:T(1024)S(1)} %broadcast_clamp_fusion), kind=kCustom, calls=%fused_computation | custom fusion | bytes 528384 | tf_op jit(solution)/shard_map/gather | solution.py:86
  (113 shorter events, 5.5 us)
Async XLA Ops:
  0.6 100.2 %copy-start = (bf16[128,128]{1,0:T(8,128)(2,1)S(1)}, bf16[128,128]{1,0:T(8,128)(2,1)}, u32[]{:S(2)}) copy-start(bf16[128,128]{1,0:T(8,128)(2,1)} %param.16) | copy-start | bytes 98308
  0.6 10.2 %copy-start.4 = (s32[1024,1]{0,1:T(1,128)S(1)}, s32[1024,1]{0,1:T(1,128)}, u32[]{:S(2)}) copy-start(s32[1024,1]{0,1:T(1,128)} %param.11) | copy-start | bytes 12292
  16.0 14.4 %all-to-all-start = ((s32[32,1,128]{2,1,0:T(1,128)}), s32[32,1,128]{2,1,0:T(1,128)S(1)}, u32[]{:S(2)}, u32[]{:S(2)}) async-start(s32[32,1,128]{2,1,0:T(1,128)} %bitcast.6), calls=%async_computation | async-start | bytes 32768 | tf_op jit(solution)/shard_map/all_to_all | solution.py:53
  30.5 3.5 %copy-start.3 = (bf16[64,64]{1,0:T(8,128)(2,1)S(1)}, bf16[64,64]{1,0:T(8,128)(2,1)}, u32[]{:S(2)}) copy-start(bf16[64,64]{1,0:T(8,128)(2,1)} %param.14) | copy-start | bytes 24580
  30.5 3.6 %copy-start.2 = (bf16[64,64]{1,0:T(8,128)(2,1)S(1)}, bf16[64,64]{1,0:T(8,128)(2,1)}, u32[]{:S(2)}) copy-start(bf16[64,64]{1,0:T(8,128)(2,1)} %param.15) | copy-start | bytes 24580
  30.5 29.6 %copy-start.5 = (bf16[2048,128]{1,0:T(8,128)(2,1)S(1)}, bf16[2048,128]{1,0:T(8,128)(2,1)}, u32[]{:S(2)}) copy-start(bf16[2048,128]{1,0:T(8,128)(2,1)} %param.13) | copy-start | bytes 1572868
  30.5 29.6 %all-to-all-start.1 = ((bf16[32,128,128]{2,1,0:T(8,128)(2,1)}), bf16[32,128,128]{2,1,0:T(8,128)(2,1)S(1)}, u32[]{:S(2)}, u32[]{:S(2)}) async-start(bf16[32,128,128]{2,1,0:T(8,128)(2,1)} %bitcast.7), calls=%async_computation.1 | async-start | bytes 2097152 | tf_op jit(solution)/shard_map/all_to_all | solution.py:46
  97.8 3.1 %copy-start.1 = (bf16[2048,128]{1,0:T(8,128)(2,1)S(1)}, bf16[2048,128]{1,0:T(8,128)(2,1)}, u32[]{:S(2)}) copy-start(bf16[2048,128]{1,0:T(8,128)(2,1)} %param.17) | copy-start | bytes 1572868
  97.8 29.0 %all-to-all-start.2 = ((bf16[32,128,128]{2,1,0:T(8,128)(2,1)}), bf16[32,128,128]{2,1,0:T(8,128)(2,1)S(1)}, u32[]{:S(2)}, u32[]{:S(2)}) async-start(bf16[32,128,128]{2,1,0:T(8,128)(2,1)} %bitcast.11), calls=%async_computation.2 | async-start | bytes 2097152 | tf_op jit(solution)/shard_map/all_to_all | solution.py:79
where the time goes:
time: 131 us
  waiting for transfers between devices  51.8 us (40%)
  local copies, waits for them, and re-layouts  23.3 us (18%)
  matrix products  21.3 us (16%)
  starting transfers between devices  13.5 us (10%)
  other arithmetic  11 us (8%)
  blocking collectives  8.54 us (7%)
    all_to_all x1, waiting for transfers between devices, local(): lax.all_to_all(answers.reshape(devices, capacity, row_width), ('surf', 'v...  24.8 us
    all_to_all x1, waiting for transfers between devices, local(): lax.all_to_all(send_rows.reshape(devices, capacity, row_width), ('surf',...  24.6 us
    another operation x2, other arithmetic  9.04 us
    dot_general x8, matrix products, settle(): jnp.dot(selector, mold_faces, preferred_element_type=jnp.float32)  8.6 us
    all_to_all x1, blocking collectives, local(): lax.all_to_all(face_totals.reshape(vol_count, quarter * node_count // row...  8.54 us
    dot_general x8, matrix products, settle(): lax.dot_general(selector, gained, (((0,), (0,)), ((), ())), preferred_ele...  8.09 us
    all_to_all x1, starting transfers between devices, local(): lax.all_to_all(send_ids.reshape(devices, capacity), ('surf', 'vol'), spli...  7.33 us
    dynamic_update_slice x16, local copies, waits for them, and re-layouts, local(): lax.scan(settle, jnp.zeros((face_rows, node_count), jnp.float32), (flat_r...  6.25 us
  transfers between devices with their start and end apart: 3, of which 3 were waited for; matrix products, arithmetic and copies ran while one was open for 6% of the time, Pallas kernels for 0%

commit v1 on v0

v1 whole, which is shorter than its diff:
```python
import jax
import jax.numpy as jnp
from jax import lax
from jax.sharding import PartitionSpec as P

relax = 0.5


def contact(rows, mold_rows, stacked, joined, node_count):
    pair_rows = jnp.concatenate([rows[:, :node_count], mold_rows[:, :node_count]], axis=1)
    gap_jump = jnp.dot(pair_rows, stacked, preferred_element_type=jnp.float32)
    heat_flux = (
        rows[:, node_count:].astype(jnp.float32)
        * mold_rows[:, node_count:].astype(jnp.float32)
        * gap_jump
    ).astype(jnp.bfloat16)
    projected = jnp.dot(heat_flux, joined, preferred_element_type=jnp.float32)
    answer = jnp.concatenate([projected[:, :node_count], gap_jump], axis=1).astype(jnp.bfloat16)
    gained = projected[:, node_count:].astype(jnp.bfloat16)
    return (answer, gained)


def local(casting, owner, face_id, mold_faces, mortar_d, mortar_m, conduct, volume):
    seg_rows, row_width = casting.shape
    node_count = mortar_d.shape[0]
    face_rows = mold_faces.shape[0]
    surf_count = lax.axis_size("surf")
    vol_count = lax.axis_size("vol")
    devices = surf_count * vol_count
    capacity = 4 * seg_rows // devices
    slots = devices * capacity
    axes = ("surf", "vol")
    f32, bf16 = jnp.float32, jnp.bfloat16

    target = owner[:, 0]
    hits = (target[:, None] == jnp.arange(devices, dtype=jnp.int32)[None, :]).astype(bf16)
    row_i = lax.broadcasted_iota(jnp.int32, (seg_rows, seg_rows), 0)
    row_j = lax.broadcasted_iota(jnp.int32, (seg_rows, seg_rows), 1)
    earlier = (row_j < row_i).astype(bf16)
    before = jnp.dot(earlier, hits, preferred_element_type=f32)
    position = jnp.sum(before * hits.astype(f32), axis=1).astype(jnp.int32)
    slot_index = target * capacity + position

    code = face_id + 1
    pos_hot = (position[:, None] == jnp.arange(capacity, dtype=jnp.int32)[None, :]).astype(bf16)
    hi = (code // 64).astype(bf16)[:, None]
    lo = (code % 64).astype(bf16)[:, None]
    placed_hi = lax.dot_general(hits, pos_hot * hi, (((0,), (0,)), ((), ())), preferred_element_type=f32)
    placed_lo = lax.dot_general(hits, pos_hot * lo, (((0,), (0,)), ((), ())), preferred_element_type=f32)
    send_ids = (placed_hi * 64.0 + placed_lo).astype(jnp.int32) - 1

    got_ids = lax.all_to_all(send_ids, axes, 0, 0, tiled=True).reshape(slots)

    face_range = jnp.arange(face_rows, dtype=jnp.int32)
    selector = (got_ids[:, None] == face_range[None, :]).astype(bf16)
    ask_rows = jnp.dot(selector, mold_faces, preferred_element_type=f32).astype(bf16)
    back_rows = lax.all_to_all(
        ask_rows.reshape(devices, capacity, row_width), axes, 0, 0, tiled=True
    ).reshape(slots, row_width)
    mold_rows = jnp.take(back_rows, slot_index, axis=0)

    stacked = jnp.concatenate([mortar_d.T, -mortar_m.T], axis=0)
    joined = jnp.concatenate([mortar_d, mortar_m], axis=1)
    casting_out, gained = contact(casting, mold_rows, stacked, joined, node_count)

    send_gain = jnp.zeros((slots, node_count), bf16).at[slot_index].set(gained)
    got_gain = lax.all_to_all(
        send_gain.reshape(devices, capacity, node_count), axes, 0, 0, tiled=True
    ).reshape(slots, node_count)
    totals = lax.dot_general(
        selector, got_gain, (((0,), (0,)), ((), ())), preferred_element_type=f32
    )

    face_totals = totals.astype(bf16)
    quarter = face_rows // vol_count
    relaid = lax.all_to_all(
        face_totals.reshape(vol_count, quarter * node_count // row_width, row_width),
        "vol",
        split_axis=0,
        concat_axis=0,
        tiled=True,
    )
    heat = jnp.dot(volume, conduct, preferred_element_type=f32)
    placed = relaid.reshape(face_rows, node_count).astype(f32)
    inject = jnp.concatenate([placed, jnp.zeros((face_rows, node_count), f32)], axis=1)
    mold_out = (volume.astype(f32) + relax * (inject - heat)).astype(bf16)
    return (casting_out, mold_out)


def solution(mesh):
    return jax.shard_map(
        local,
        mesh=mesh,
        in_specs=(
            P(("surf", "vol"), None),
            P(("surf", "vol"), None),
            P(("surf", "vol")),
            P(("surf", "vol"), None),
            P(),
            P(),
            P(),
            P(("surf", "vol"), None),
        ),
        out_specs=(P(("surf", "vol"), None), P(("surf", "vol"), None)),
        check_vma=False,
    )
```

time: 131 us -> 100 us (0.76)
  blocking collectives: 8.54 us -> 33.3 us
  waiting for transfers between devices: 51.8 us -> 30.5 us
  local copies, waits for them, and re-layouts: 23.3 us -> 11 us
  other arithmetic: 11 us -> 0.11 us
  starting transfers between devices: 13.5 us -> 6.18 us
  matrix products: 21.3 us -> 17.6 us
    all_to_all x1 -> x2, blocking collectives: 8.54 us -> 33.3 us  [the longest x1 19 us: local(): lax.all_to_all(send_gain.reshape(devices, capacity, node_count), axes, 0,...]
    all_to_all x3 -> x2, waiting for transfers between devices: 51.8 us -> 30.5 us  [the longest x1 25.5 us: local(): lax.all_to_all(ask_rows.reshape(devices, capacity, row_width), axes, 0, 0...]
    another operation x2 -> x0, other arithmetic: 9.04 us -> none
    all_to_all x3 -> x2, starting transfers between devices: 13.5 us -> 6.18 us  [the longest x1 3.41 us: local(): lax.all_to_all(face_totals.reshape(vol_count, quarter * node_count // row...]
    dynamic_update_slice x16 -> x0, local copies, waits for them, and re-layouts: 6.25 us -> none  [local(): lax.scan(settle, jnp.zeros((face_rows, node_count), jnp.float32), (flat_r...]
    scatter x2 -> x1, local copies, waits for them, and re-layouts: 9.74 us -> 3.54 us  [local(): send_gain = jnp.zeros((slots, node_count), bf16).at[slot_index].set(gained)]
    unnamed x14 -> x19, local copies, waits for them, and re-layouts: 0.21 us -> 1.89 us
    dot_general x8 -> x1, matrix products: 1.84 us -> 0.34 us  [contact(): projected = jnp.dot(heat_flux, joined, preferred_element_type=jnp.float32)]
  transfers between devices with their start and end apart: 3 -> 2, of which waited for: 3 -> 2; matrix products, arithmetic and copies ran while one was open for 6% -> 1% of each run, Pallas kernels for 0% -> 0%
where the time goes in v1:
time: 100 us; the launch traced here: 99.6 us
  blocking collectives  33.3 us (33%)
  waiting for transfers between devices  30.5 us (30%)
  matrix products  17.6 us (18%)
  local copies, waits for them, and re-layouts  11 us (11%)
  starting transfers between devices  6.18 us (6%)
    all_to_all x1, waiting for transfers between devices, local(): lax.all_to_all(ask_rows.reshape(devices, capacity, row_width), axes, 0, 0...  25.5 us
    all_to_all x1, blocking collectives, local(): lax.all_to_all(send_gain.reshape(devices, capacity, node_count), axes, 0,...  19 us
    all_to_all x1, blocking collectives, local(): got_ids = lax.all_to_all(send_ids, axes, 0, 0, tiled=True).reshape(slots)  14.3 us
    dot_general x1, matrix products, local(): jnp.dot(selector, mold_faces, preferred_element_type=f32).astype(bf16)  7.14 us
    dot_general x1, matrix products, local(): lax.dot_general(selector, got_gain, (((0,), (0,)), ((), ())), preferred_e...  6.52 us
    all_to_all x1, waiting for transfers between devices, local(): lax.all_to_all(face_totals.reshape(vol_count, quarter * node_count // row...  5.08 us
    scatter x1, local copies, waits for them, and re-layouts, local(): send_gain = jnp.zeros((slots, node_count), bf16).at[slot_index].set(gained)  3.54 us
    all_to_all x1, starting transfers between devices, local(): lax.all_to_all(face_totals.reshape(vol_count, quarter * node_count // row...  3.41 us
  transfers between devices with their start and end apart: 2, of which 2 were waited for; matrix products, arithmetic and copies ran while one was open for 1% of the time, Pallas kernels for 0%

profile of v1, /device:TPU:0, one launch (start us, length us, event | category | flops | bytes accessed | tf_op | source)
XLA Modules:
  0.0 99.6 jit_solution(4462265533365780487)
XLA Ops:
  0.6 0.0 copy-start
  0.6 0.0 copy-start.7
  0.7 0.0 copy-start.6
  0.7 1.3 %fusion.11 = f32[1024]{0:T(1024)S(1)} fusion(s32[1024]{0:T(1024)} %bitcast.32), kind=kOutput, calls=%fused_computation.17 | convolution fusion | flops 68353024 | bytes 8192 | tf_op jit(solution)/shard_map/dot_general | solution.py:40
  2.0 0.0 copy-done.6
  2.0 0.0 copy-done.7
  2.0 0.5 convolution_multiply_fusion
  2.5 0.5 fusion.13
  3.0 14.3 %all_to_all.24 = s32[32,1,128]{2,1,0:T(1,128)S(1)} all-to-all(s32[32,1,128]{2,1,0:T(1,128)S(1)} %bitcast.28), channel_id=1, replica_groups=mesh['surf'=8,'vol'=4] {'surf','vol'}, dimensions={0} | all-to-all | bytes 32768 | tf_op jit(solution)/shard_map/all_to_all | solution.py:52
  17.3 0.0 copy-done
  17.3 7.1 %fusion.4 = bf16[4096,128]{1,0:T(8,128)(2,1)} fusion(bf16[2048,128]{1,0:T(8,128)(2,1)S(1)} %copy-done, s32[4096]{0:T(1024)S(1)} %bitcast.26), kind=kOutput, calls=%fused_computation.7 | convolution fusion | flops 2156396544 | bytes 1589248 | tf_op jit(solution)/shard_map/dot_general | solution.py:56
  24.4 0.0 copy-start.1
  24.4 2.8 %all-to-all-start.1 = ((bf16[32,128,128]{2,1,0:T(8,128)(2,1)}), bf16[32,128,128]{2,1,0:T(8,128)(2,1)S(1)}, u32[]{:S(2)}, u32[]{:S(2)}) async-start(bf16[32,128,128]{2,1,0:T(8,128)(2,1)} %bitcast.5), calls=%async_computation.1 | async-start | bytes 2097152 | tf_op jit(solution)/shard_map/all_to_all | solution.py:57
  27.2 0.0 copy-done.1
  27.2 0.0 copy-start.4
  27.2 0.1 fusion.52
  27.4 0.1 copy.38
  27.5 0.1 copy.37
  27.7 0.2 copy-done.4
  27.9 25.5 %all-to-all-done.1 = bf16[32,128,128]{2,1,0:T(8,128)(2,1)S(1)} async-done(((bf16[32,128,128]{2,1,0:T(8,128)(2,1)}), bf16[32,128,128]{2,1,0:T(8,128)(2,1)S(1)}, u32[]{:S(2)}, u32[]{:S(2)}) %all-to-all-start.1) | async-done | bytes 1048608 | tf_op jit(solution)/shard_map/all_to_all | solution.py:57
  53.4 3.2 %gather_fusion = bf16[1024,128]{1,0:T(8,128)(2,1)S(1)} fusion(bf16[4096,128]{1,0:T(8,128)(2,1)S(1)} %bitcast.23, s32[1024]{0:T(1024)S(1)} %broadcast_clamp_fusion), kind=kCustom, calls=%fused_computation | custom fusion | bytes 528384 | tf_op jit(solution)/shard_map/jit(_take)/gather | solution.py:60
  56.6 0.0 copy-start.3
  56.6 0.1 copy.30
  56.8 0.5 copy-done.3
  57.3 0.2 fusion.53
  57.6 0.3 convolution_convert_fusion
  57.9 0.2 copy.32
  58.1 3.5 %scatter_custom_fusion = bf16[4096,64]{1,0:T(8,128)(2,1)S(1)} fusion(s32[1024]{0:T(1024)S(1)} %bitcast.30, bf16[1024,64]{1,0:T(8,128)(2,1)S(1)} %copy.32, bf16[]{:T(256)} %constant.57.clone.1), kind=kCustom, calls=%fused_computation.24 | custom fusion | bytes 524290 | tf_op jit(solution)/shard_map/scatter | solution.py:66
  61.6 0.4 copy.33
  62.0 19.0 %all_to_all.25 = bf16[32,128,64]{1,2,0:T(8,128)(2,1)S(1)} all-to-all(bf16[32,128,64]{1,2,0:T(8,128)(2,1)S(1)} %copy.33), channel_id=1, replica_groups=mesh['surf'=8,'vol'=4] {'surf','vol'}, dimensions={0} | all-to-all | bytes 1048576 | tf_op jit(solution)/shard_map/all_to_all | solution.py:67
  81.0 6.5 %fusion.9 = bf16[2048,64]{0,1:T(8,128)(2,1)S(1)} fusion(s32[4096]{0:T(1024)S(1)} %bitcast.27, bf16[32,128,64]{1,2,0:T(8,128)(2,1)S(1)} %all_to_all.25), kind=kOutput, calls=%fused_computation.14 | convolution fusion | flops 1082261504 | bytes 802816 | tf_op jit(solution)/shard_map/dot_general | solution.py:70
  87.5 0.3 copy.35
  87.8 1.0 reshape.46
  88.8 3.4 %all-to-all-start.3 = ((bf16[4,256,128]{2,1,0:T(8,128)(2,1)}), bf16[4,256,128]{2,1,0:T(8,128)(2,1)S(1)}, u32[]{:S(2)}, u32[]{:S(2)}) async-start(bf16[4,256,128]{2,1,0:T(8,128)(2,1)} %reshape.46), calls=%async_computation.3 | async-start | bytes 524288 | tf_op jit(solution)/shard_map/all_to_all | solution.py:76
  92.2 0.0 copy-start.2
  92.2 0.0 copy-start.5
  92.2 0.8 copy.36
  93.1 5.1 %all-to-all-done.3 = bf16[4,256,128]{2,1,0:T(8,128)(2,1)S(1)} async-done(((bf16[4,256,128]{2,1,0:T(8,128)(2,1)}), bf16[4,256,128]{2,1,0:T(8,128)(2,1)S(1)}, u32[]{:S(2)}, u32[]{:S(2)}) %all-to-all-start.3) | async-done | bytes 262176 | tf_op jit(solution)/shard_map/all_to_all | solution.py:76
  98.1 0.2 convert_element_type.74
  98.4 0.0 copy-done.2
  98.4 0.0 copy-done.5
  98.4 1.2 %fusion.8 = bf16[2048,128]{1,0:T(8,128)(2,1)} fusion(bf16[2048,128]{1,0:T(8,128)(2,1)S(1)} %copy-done.2, bf16[128,128]{1,0:T(8,128)(2,1)S(1)} %copy-done.5, bf16[2048,64]{1,0:T(8,128)(2,1)S(1)} %convert_element_type.74), kind=kOutput, calls=%fused_computation.13 | convolution fusion | flops 68681728 | bytes 1343488 | tf_op jit(solution)/shard_map/dot_general | solution.py:83
  (9 shorter events, 0.1 us)
Async XLA Ops:
  0.6 16.6 %copy-start = (bf16[2048,128]{1,0:T(8,128)(2,1)S(1)}, bf16[2048,128]{1,0:T(8,128)(2,1)}, u32[]{:S(2)}) copy-start(bf16[2048,128]{1,0:T(8,128)(2,1)} %param.11) | copy-start | bytes 1572868
  0.6 1.4 %copy-start.7 = (s32[1024,1]{0,1:T(1,128)S(1)}, s32[1024,1]{0,1:T(1,128)}, u32[]{:S(2)}) copy-start(s32[1024,1]{0,1:T(1,128)} %param.9) | copy-start | bytes 12292
  0.7 1.3 %copy-start.6 = (s32[1024]{0:T(1024)S(1)}, s32[1024]{0:T(1024)}, u32[]{:S(2)}) copy-start(s32[1024]{0:T(1024)} %param.10) | copy-start | bytes 12292
  24.4 2.8 %copy-start.1 = (bf16[1024,128]{1,0:T(8,128)(2,1)S(1)}, bf16[1024,128]{1,0:T(8,128)(2,1)}, u32[]{:S(2)}) copy-start(bf16[1024,128]{1,0:T(8,128)(2,1)} %param.8) | copy-start | bytes 786436
  24.4 29.0 %all-to-all-start.1 = ((bf16[32,128,128]{2,1,0:T(8,128)(2,1)}), bf16[32,128,128]{2,1,0:T(8,128)(2,1)S(1)}, u32[]{:S(2)}, u32[]{:S(2)}) async-start(bf16[32,128,128]{2,1,0:T(8,128)(2,1)} %bitcast.5), calls=%async_computation.1 | async-start | bytes 2097152 | tf_op jit(solution)/shard_map/all_to_all | solution.py:57
  27.2 0.7 copy-start.4
  56.6 0.7 copy-start.3
  88.8 9.4 %all-to-all-start.3 = ((bf16[4,256,128]{2,1,0:T(8,128)(2,1)}), bf16[4,256,128]{2,1,0:T(8,128)(2,1)S(1)}, u32[]{:S(2)}, u32[]{:S(2)}) async-start(bf16[4,256,128]{2,1,0:T(8,128)(2,1)} %reshape.46), calls=%async_computation.3 | async-start | bytes 524288 | tf_op jit(solution)/shard_map/all_to_all | solution.py:76
  92.2 6.2 %copy-start.2 = (bf16[2048,128]{1,0:T(8,128)(2,1)S(1)}, bf16[2048,128]{1,0:T(8,128)(2,1)}, u32[]{:S(2)}) copy-start(bf16[2048,128]{1,0:T(8,128)(2,1)} %param.15) | copy-start | bytes 1572868
  92.2 6.2 %copy-start.5 = (bf16[128,128]{1,0:T(8,128)(2,1)S(1)}, bf16[128,128]{1,0:T(8,128)(2,1)}, u32[]{:S(2)}) copy-start(bf16[128,128]{1,0:T(8,128)(2,1)} %param.14) | copy-start | bytes 98308

commit v2 on v1

--- a/solution.py
+++ b/solution.py
@@ -65,7 +65,8 @@
 
     send_gain = jnp.zeros((slots, node_count), bf16).at[slot_index].set(gained)
     got_gain = lax.all_to_all(
-        send_gain.reshape(devices, capacity, node_count), axes, 0, 0, tiled=True
+        send_gain.reshape(devices, capacity * node_count // row_width, row_width),
+        axes, 0, 0, tiled=True,
     ).reshape(slots, node_count)
     totals = lax.dot_general(
         selector, got_gain, (((0,), (0,)), ((), ())), preferred_element_type=f32

time: 100 us -> 101 us (1.010)
  no operation moved by 1% of the time
where the time goes in v2:
time: 101 us; the launch traced here: 100 us
  blocking collectives  33.3 us (33%)
  waiting for transfers between devices  30.5 us (30%)
  matrix products  17.9 us (18%)
  local copies, waits for them, and re-layouts  11.5 us (11%)
  starting transfers between devices  6.18 us (6%)
    all_to_all x1, waiting for transfers between devices, local(): lax.all_to_all(ask_rows.reshape(devices, capacity, row_width), axes, 0, 0...  25.5 us
    all_to_all x1, blocking collectives, local(): lax.all_to_all(send_gain.reshape(devices, capacity * node_count // row_wi...  19 us
    all_to_all x1, blocking collectives, local(): got_ids = lax.all_to_all(send_ids, axes, 0, 0, tiled=True).reshape(slots)  14.3 us
    dot_general x1, matrix products, local(): jnp.dot(selector, mold_faces, preferred_element_type=f32).astype(bf16)  7.14 us
    dot_general x1, matrix products, local(): lax.dot_general(selector, got_gain, (((0,), (0,)), ((), ())), preferred_e...  6.83 us
    all_to_all x1, waiting for transfers between devices, local(): lax.all_to_all(face_totals.reshape(vol_count, quarter * node_count // row...  5.08 us
    scatter x1, local copies, waits for them, and re-layouts, local(): send_gain = jnp.zeros((slots, node_count), bf16).at[slot_index].set(gained)  3.54 us
    all_to_all x1, starting transfers between devices, local(): lax.all_to_all(face_totals.reshape(vol_count, quarter * node_count // row...  3.41 us
  transfers between devices with their start and end apart: 2, of which 2 were waited for; matrix products, arithmetic and copies ran while one was open for 1% of the time, Pallas kernels for 0%

profile of v2, /device:TPU:0, one launch (start us, length us, event | category | flops | bytes accessed | tf_op | source)
XLA Modules:
  0.0 100.4 jit_solution(14187768760243407959)
XLA Ops:
  0.6 0.0 copy-start
  0.6 0.0 copy-start.7
  0.7 0.0 copy-start.6
  0.7 1.3 %fusion.11 = f32[1024]{0:T(1024)S(1)} fusion(s32[1024]{0:T(1024)} %bitcast.24), kind=kOutput, calls=%fused_computation.17 | convolution fusion | flops 68353024 | bytes 8192 | tf_op jit(solution)/shard_map/dot_general | solution.py:40
  2.0 0.0 copy-done.6
  2.0 0.0 copy-done.7
  2.0 0.5 convolution_multiply_fusion
  2.5 0.5 fusion.13
  3.0 14.3 %all_to_all.24 = s32[32,1,128]{2,1,0:T(1,128)S(1)} all-to-all(s32[32,1,128]{2,1,0:T(1,128)S(1)} %bitcast.20), channel_id=1, replica_groups=mesh['surf'=8,'vol'=4] {'surf','vol'}, dimensions={0} | all-to-all | bytes 32768 | tf_op jit(solution)/shard_map/all_to_all | solution.py:52
  17.3 0.0 copy-done
  17.3 7.1 %fusion.4 = bf16[4096,128]{1,0:T(8,128)(2,1)} fusion(bf16[2048,128]{1,0:T(8,128)(2,1)S(1)} %copy-done, s32[4096]{0:T(1024)S(1)} %bitcast.18), kind=kOutput, calls=%fused_computation.7 | convolution fusion | flops 2156396544 | bytes 1589248 | tf_op jit(solution)/shard_map/dot_general | solution.py:56
  24.4 0.0 copy-start.1
  24.4 2.8 %all-to-all-start.1 = ((bf16[32,128,128]{2,1,0:T(8,128)(2,1)}), bf16[32,128,128]{2,1,0:T(8,128)(2,1)S(1)}, u32[]{:S(2)}, u32[]{:S(2)}) async-start(bf16[32,128,128]{2,1,0:T(8,128)(2,1)} %bitcast.5), calls=%async_computation.1 | async-start | bytes 2097152 | tf_op jit(solution)/shard_map/all_to_all | solution.py:57
  27.2 0.0 copy-done.1
  27.2 0.0 copy-start.4
  27.2 0.1 fusion.50
  27.4 0.1 copy.28
  27.5 0.1 copy.27
  27.7 0.2 copy-done.4
  27.9 25.5 %all-to-all-done.1 = bf16[32,128,128]{2,1,0:T(8,128)(2,1)S(1)} async-done(((bf16[32,128,128]{2,1,0:T(8,128)(2,1)}), bf16[32,128,128]{2,1,0:T(8,128)(2,1)S(1)}, u32[]{:S(2)}, u32[]{:S(2)}) %all-to-all-start.1) | async-done | bytes 1048608 | tf_op jit(solution)/shard_map/all_to_all | solution.py:57
  53.4 3.2 %gather_fusion = bf16[1024,128]{1,0:T(8,128)(2,1)S(1)} fusion(bf16[4096,128]{1,0:T(8,128)(2,1)S(1)} %bitcast.16, s32[1024]{0:T(1024)S(1)} %broadcast_clamp_fusion), kind=kCustom, calls=%fused_computation | custom fusion | bytes 528384 | tf_op jit(solution)/shard_map/jit(_take)/gather | solution.py:60
  56.6 0.0 copy-start.3
  56.6 0.1 copy.22
  56.8 0.5 copy-done.3
  57.3 0.2 fusion.51
  57.6 0.3 convolution_convert_fusion
  57.9 0.2 copy.24
  58.1 3.5 %scatter_custom_fusion = bf16[4096,64]{1,0:T(8,128)(2,1)S(1)} fusion(s32[1024]{0:T(1024)S(1)} %bitcast.22, bf16[1024,64]{1,0:T(8,128)(2,1)S(1)} %copy.24, bf16[]{:T(256)} %constant.57.clone.1), kind=kCustom, calls=%fused_computation.22 | custom fusion | bytes 524290 | tf_op jit(solution)/shard_map/scatter | solution.py:66
  61.6 0.5 reshape.44
  62.1 19.0 %all_to_all.25 = bf16[32,64,128]{2,1,0:T(8,128)(2,1)S(1)} all-to-all(bf16[32,64,128]{2,1,0:T(8,128)(2,1)S(1)} %reshape.44), channel_id=1, replica_groups=mesh['surf'=8,'vol'=4] {'surf','vol'}, dimensions={0} | all-to-all | bytes 1048576 | tf_op jit(solution)/shard_map/all_to_all | solution.py:67
  81.1 0.4 reshape.45
  81.5 6.8 %fusion.9 = bf16[2048,64]{0,1:T(8,128)(2,1)S(1)} fusion(bf16[4096,64]{1,0:T(8,128)(2,1)S(1)} %reshape.45, s32[4096]{0:T(1024)S(1)} %bitcast.19), kind=kOutput, calls=%fused_computation.14 | convolution fusion | flops 1082261504 | bytes 802816 | tf_op jit(solution)/shard_map/dot_general | solution.py:71
  88.3 0.3 copy.25
  88.6 1.0 reshape.46
  89.6 3.4 %all-to-all-start.3 = ((bf16[4,256,128]{2,1,0:T(8,128)(2,1)}), bf16[4,256,128]{2,1,0:T(8,128)(2,1)S(1)}, u32[]{:S(2)}, u32[]{:S(2)}) async-start(bf16[4,256,128]{2,1,0:T(8,128)(2,1)} %reshape.46), calls=%async_computation.3 | async-start | bytes 524288 | tf_op jit(solution)/shard_map/all_to_all | solution.py:77
  93.0 0.0 copy-start.2
  93.0 0.0 copy-start.5
  93.0 0.8 copy.26
  93.9 5.1 %all-to-all-done.3 = bf16[4,256,128]{2,1,0:T(8,128)(2,1)S(1)} async-done(((bf16[4,256,128]{2,1,0:T(8,128)(2,1)}), bf16[4,256,128]{2,1,0:T(8,128)(2,1)S(1)}, u32[]{:S(2)}, u32[]{:S(2)}) %all-to-all-start.3) | async-done | bytes 262176 | tf_op jit(solution)/shard_map/all_to_all | solution.py:77
  99.0 0.2 convert_element_type.74
  99.2 0.0 copy-done.2
  99.2 0.0 copy-done.5
  99.2 1.2 %fusion.8 = bf16[2048,128]{1,0:T(8,128)(2,1)} fusion(bf16[2048,128]{1,0:T(8,128)(2,1)S(1)} %copy-done.2, bf16[128,128]{1,0:T(8,128)(2,1)S(1)} %copy-done.5, bf16[2048,64]{1,0:T(8,128)(2,1)S(1)} %convert_element_type.74), kind=kOutput, calls=%fused_computation.13 | convolution fusion | flops 68681728 | bytes 1343488 | tf_op jit(solution)/shard_map/dot_general | solution.py:84
  (9 shorter events, 0.1 us)
Async XLA Ops:
  0.6 16.6 %copy-start = (bf16[2048,128]{1,0:T(8,128)(2,1)S(1)}, bf16[2048,128]{1,0:T(8,128)(2,1)}, u32[]{:S(2)}) copy-start(bf16[2048,128]{1,0:T(8,128)(2,1)} %param.11) | copy-start | bytes 1572868
  0.6 1.4 %copy-start.7 = (s32[1024,1]{0,1:T(1,128)S(1)}, s32[1024,1]{0,1:T(1,128)}, u32[]{:S(2)}) copy-start(s32[1024,1]{0,1:T(1,128)} %param.9) | copy-start | bytes 12292
  0.7 1.3 %copy-start.6 = (s32[1024]{0:T(1024)S(1)}, s32[1024]{0:T(1024)}, u32[]{:S(2)}) copy-start(s32[1024]{0:T(1024)} %param.10) | copy-start | bytes 12292
  24.4 2.8 %copy-start.1 = (bf16[1024,128]{1,0:T(8,128)(2,1)S(1)}, bf16[1024,128]{1,0:T(8,128)(2,1)}, u32[]{:S(2)}) copy-start(bf16[1024,128]{1,0:T(8,128)(2,1)} %param.8) | copy-start | bytes 786436
  24.4 29.0 %all-to-all-start.1 = ((bf16[32,128,128]{2,1,0:T(8,128)(2,1)}), bf16[32,128,128]{2,1,0:T(8,128)(2,1)S(1)}, u32[]{:S(2)}, u32[]{:S(2)}) async-start(bf16[32,128,128]{2,1,0:T(8,128)(2,1)} %bitcast.5), calls=%async_computation.1 | async-start | bytes 2097152 | tf_op jit(solution)/shard_map/all_to_all | solution.py:57
  27.2 0.7 copy-start.4
  56.6 0.7 copy-start.3
  89.6 9.4 %all-to-all-start.3 = ((bf16[4,256,128]{2,1,0:T(8,128)(2,1)}), bf16[4,256,128]{2,1,0:T(8,128)(2,1)S(1)}, u32[]{:S(2)}, u32[]{:S(2)}) async-start(bf16[4,256,128]{2,1,0:T(8,128)(2,1)} %reshape.46), calls=%async_computation.3 | async-start | bytes 524288 | tf_op jit(solution)/shard_map/all_to_all | solution.py:77
  93.0 6.2 %copy-start.2 = (bf16[2048,128]{1,0:T(8,128)(2,1)S(1)}, bf16[2048,128]{1,0:T(8,128)(2,1)}, u32[]{:S(2)}) copy-start(bf16[2048,128]{1,0:T(8,128)(2,1)} %param.15) | copy-start | bytes 1572868
  93.0 6.2 %copy-start.5 = (bf16[128,128]{1,0:T(8,128)(2,1)S(1)}, bf16[128,128]{1,0:T(8,128)(2,1)}, u32[]{:S(2)}) copy-start(bf16[128,128]{1,0:T(8,128)(2,1)} %param.14) | copy-start | bytes 98308

commit v3 on v1

--- a/solution.py
+++ b/solution.py
@@ -31,6 +31,7 @@
     slots = devices * capacity
     axes = ("surf", "vol")
     f32, bf16 = jnp.float32, jnp.bfloat16
+    contract0 = (((0,), (0,)), ((), ()))
 
     target = owner[:, 0]
     hits = (target[:, None] == jnp.arange(devices, dtype=jnp.int32)[None, :]).astype(bf16)
@@ -45,32 +46,38 @@
     pos_hot = (position[:, None] == jnp.arange(capacity, dtype=jnp.int32)[None, :]).astype(bf16)
     hi = (code // 64).astype(bf16)[:, None]
     lo = (code % 64).astype(bf16)[:, None]
-    placed_hi = lax.dot_general(hits, pos_hot * hi, (((0,), (0,)), ((), ())), preferred_element_type=f32)
-    placed_lo = lax.dot_general(hits, pos_hot * lo, (((0,), (0,)), ((), ())), preferred_element_type=f32)
-    send_ids = (placed_hi * 64.0 + placed_lo).astype(jnp.int32) - 1
+    id_hi = lax.dot_general(hits, pos_hot * hi, contract0, preferred_element_type=f32)
+    id_lo = lax.dot_general(hits, pos_hot * lo, contract0, preferred_element_type=f32)
+    id_count = 2 * capacity
+    id_height = -(-id_count // row_width)
+    id_flat = jnp.stack([id_hi, id_lo], axis=1).reshape(devices, id_count)
+    id_flat = jnp.pad(id_flat, ((0, 0), (0, id_height * row_width - id_count)))
+    id_rows = id_flat.reshape(devices, id_height, row_width)
 
-    got_ids = lax.all_to_all(send_ids, axes, 0, 0, tiled=True).reshape(slots)
+    send_rows = jnp.zeros((slots, row_width), bf16).at[slot_index].set(casting)
+    send = jnp.concatenate(
+        [send_rows.reshape(devices, capacity, row_width), id_rows.astype(bf16)], axis=1
+    )
+    got = lax.all_to_all(send, axes, 0, 0, tiled=True)
+    got_rows = got[:, :capacity, :].reshape(slots, row_width)
+    got_code = got[:, capacity:, :].astype(f32).reshape(devices, id_height * row_width)
+    got_code = got_code[:, :id_count].reshape(devices, 2, capacity)
+    got_ids = (got_code[:, 0, :] * 64.0 + got_code[:, 1, :]).astype(jnp.int32).reshape(slots) - 1
 
     face_range = jnp.arange(face_rows, dtype=jnp.int32)
     selector = (got_ids[:, None] == face_range[None, :]).astype(bf16)
-    ask_rows = jnp.dot(selector, mold_faces, preferred_element_type=f32).astype(bf16)
-    back_rows = lax.all_to_all(
-        ask_rows.reshape(devices, capacity, row_width), axes, 0, 0, tiled=True
-    ).reshape(slots, row_width)
-    mold_rows = jnp.take(back_rows, slot_index, axis=0)
+    mold_rows = jnp.dot(selector, mold_faces, preferred_element_type=f32).astype(bf16)
 
     stacked = jnp.concatenate([mortar_d.T, -mortar_m.T], axis=0)
     joined = jnp.concatenate([mortar_d, mortar_m], axis=1)
-    casting_out, gained = contact(casting, mold_rows, stacked, joined, node_count)
+    answers, gained = contact(got_rows, mold_rows, stacked, joined, node_count)
 
-    send_gain = jnp.zeros((slots, node_count), bf16).at[slot_index].set(gained)
-    got_gain = lax.all_to_all(
-        send_gain.reshape(devices, capacity, node_count), axes, 0, 0, tiled=True
-    ).reshape(slots, node_count)
-    totals = lax.dot_general(
-        selector, got_gain, (((0,), (0,)), ((), ())), preferred_element_type=f32
-    )
+    returned = lax.all_to_all(
+        answers.reshape(devices, capacity, row_width), axes, 0, 0, tiled=True
+    ).reshape(slots, row_width)
+    casting_out = jnp.take(returned, slot_index, axis=0)
 
+    totals = lax.dot_general(selector, gained, contract0, preferred_element_type=f32)
     face_totals = totals.astype(bf16)
     quarter = face_rows // vol_count
     relaid = lax.all_to_all(

time: 100 us -> 107 us (1.070)
  blocking collectives: 33.3 us -> 0 us
  waiting for transfers between devices: 30.5 us -> 56.9 us
  starting transfers between devices: 6.18 us -> 13.7 us
  other arithmetic: 0.11 us -> 3.27 us
  local copies, waits for them, and re-layouts: 11 us -> 13.2 us
    all_to_all x2 -> x0, blocking collectives: 33.3 us -> none  [the longest x1 19 us: local(): lax.all_to_all(send_gain.reshape(devices, capacity, node_count), axes, 0,...]
    all_to_all x1 -> x2, waiting for transfers between devices: 25.5 us -> 52.2 us  [the longest x1 27.4 us: local(): got = lax.all_to_all(send, axes, 0, 0, tiled=True)]
    all_to_all x1 -> x2, starting transfers between devices: 2.78 us -> 10.3 us  [the longest x1 7.5 us: local(): got = lax.all_to_all(send, axes, 0, 0, tiled=True)]
    concatenate x1 -> x2, other arithmetic: 0.02 us -> 1.19 us  [contact(): jnp.concatenate([projected[:, :node_count], gap_jump], axis=1)]
    concatenate x0 -> x1, other arithmetic: none -> 1.1 us  [local(): jnp.concatenate([send_rows.reshape(devices, capacity, row_width), id_rows...]
    unnamed x19 -> x20, local copies, waits for them, and re-layouts: 1.89 us -> 2.63 us
    gather x2 -> x1, local copies, waits for them, and re-layouts: 3.35 us -> 3.21 us  [local(): casting_out = jnp.take(returned, slot_index, axis=0)]
  transfers between devices with their start and end apart: 2 -> 3, of which waited for: 2 -> 3; matrix products, arithmetic and copies ran while one was open for 1% -> 2% of each run, Pallas kernels for 0% -> 0%
where the time goes in v3:
time: 107 us; the launch traced here: 106 us
  waiting for transfers between devices  56.9 us (53%)
  matrix products  18.3 us (17%)
  starting transfers between devices  13.7 us (13%)
  local copies, waits for them, and re-layouts  13.2 us (12%)
  other arithmetic  3.27 us (3%)
    all_to_all x1, waiting for transfers between devices, local(): got = lax.all_to_all(send, axes, 0, 0, tiled=True)  27.4 us
    all_to_all x1, waiting for transfers between devices, local(): lax.all_to_all(answers.reshape(devices, capacity, row_width), axes, 0, 0,...  24.8 us
    all_to_all x1, starting transfers between devices, local(): got = lax.all_to_all(send, axes, 0, 0, tiled=True)  7.5 us
    dot_general x1, matrix products, local(): jnp.dot(selector, mold_faces, preferred_element_type=f32).astype(bf16)  7.5 us
    dot_general x1, matrix products, local(): lax.dot_general(selector, gained, contract0, preferred_element_type=f32)  6.51 us
    all_to_all x1, waiting for transfers between devices, local(): lax.all_to_all(face_totals.reshape(vol_count, quarter * node_count // row...  4.75 us
    scatter x1, local copies, waits for them, and re-layouts, local(): send_rows = jnp.zeros((slots, row_width), bf16).at[slot_index].set(casting)  3.89 us
    all_to_all x1, starting transfers between devices, local(): lax.all_to_all(face_totals.reshape(vol_count, quarter * node_count // row...  3.41 us
  transfers between devices with their start and end apart: 3, of which 3 were waited for; matrix products, arithmetic and copies ran while one was open for 2% of the time, Pallas kernels for 0%

profile of v3, /device:TPU:0, one launch (start us, length us, event | category | flops | bytes accessed | tf_op | source)
XLA Modules:
  0.0 106.3 jit_solution(2157373865272049659)
XLA Ops:
  0.6 0.0 copy-start
  0.6 0.0 copy-start.8
  0.7 0.0 copy-start.7
  0.7 1.3 %fusion.11 = f32[1024]{0:T(1024)S(1)} fusion(s32[1024]{0:T(1024)} %bitcast.35), kind=kOutput, calls=%fused_computation.17 | convolution fusion | flops 68353024 | bytes 8192 | tf_op jit(solution)/shard_map/dot_general | solution.py:41
  2.0 0.0 copy-done.7
  2.0 0.0 copy-done.8
  2.0 0.5 fusion.12
  2.5 0.5 fusion.13
  3.0 3.9 %scatter_custom_fusion = bf16[4096,128]{1,0:T(8,128)(2,1)S(1)} fusion(s32[1024]{0:T(1024)S(1)} %bitcast.32, bf16[1024,128]{1,0:T(8,128)(2,1)} %param.8, bf16[]{:T(256)} %constant.54.clone.1), kind=kCustom, calls=%fused_computation.38 | custom fusion | bytes 1049088 | tf_op jit(solution)/shard_map/scatter | solution.py:57
  6.9 1.1 %pad_maximum_fusion = bf16[32,130,128]{2,1,0:T(8,128)(2,1)} fusion(bf16[32,1,128]{2,1,0:T(2,128)(2,1)S(1)} %copy.18, bf16[32,1,128]{2,1,0:T(2,128)(2,1)S(1)} %copy.17, bf16[32,128,128]{2,1,0:T(8,128)(2,1)S(1)} %bitcast.30), kind=kLoop, calls=%fused_computation.18 | loop fusion | flops 3194880 | bytes 2129920 | tf_op jit(solution)/shard_map/concatenate | solution.py:58
  8.0 0.0 copy-start.5
  8.0 7.5 %all-to-all-start = ((bf16[32,130,128]{2,1,0:T(8,128)(2,1)}), bf16[32,130,128]{2,1,0:T(8,128)(2,1)S(1)}, u32[]{:S(2)}, u32[]{:S(2)}) async-start(bf16[32,130,128]{2,1,0:T(8,128)(2,1)} %pad_maximum_fusion), calls=%async_computation | async-start | bytes 2228224 | tf_op jit(solution)/shard_map/all_to_all | solution.py:61
  15.6 0.0 copy-done.5
  15.6 27.4 %all-to-all-done = bf16[32,130,128]{2,1,0:T(8,128)(2,1)S(1)} async-done(((bf16[32,130,128]{2,1,0:T(8,128)(2,1)}), bf16[32,130,128]{2,1,0:T(8,128)(2,1)S(1)}, u32[]{:S(2)}, u32[]{:S(2)}) %all-to-all-start) | async-done | bytes 1064992 | tf_op jit(solution)/shard_map/all_to_all | solution.py:61
  43.0 0.0 copy-done
  43.0 7.5 %fusion.4 = bf16[4096,128]{0,1:T(8,128)(2,1)S(1)} fusion(bf16[2048,128]{1,0:T(8,128)(2,1)S(1)} %copy-done, s32[4096]{0:T(1024)S(1)} %fusion.38), kind=kOutput, calls=%fused_computation.7 | convolution fusion | flops 2156396544 | bytes 1589248 | tf_op jit(solution)/shard_map/dot_general | solution.py:69
  50.5 0.0 copy-start.1
  50.6 0.1 slice.44
  50.7 0.8 copy-done.1
  51.5 0.4 fusion.53
  51.9 0.3 copy.28
  52.2 0.0 slice-start
  52.2 0.0 copy-start.4
  52.3 0.3 copy.26
  52.6 0.7 slice-done
  53.3 0.0 copy-done.4
  53.3 0.4 fusion.14
  53.6 0.0 copy-start.2
  53.6 0.1 copy_bitcast_fusion
  53.8 1.1 %copy-done.2 = bf16[4096,128]{0,1:T(8,128)(2,1)S(1)} copy-done((bf16[4096,128]{0,1:T(8,128)(2,1)S(1)}, bf16[4096,128]{0,1:T(8,128)(2,1)}, u32[]{:S(2)}) %copy-start.2) | copy-done | bytes 1048600
  54.9 0.6 convolution_convert_fusion
  55.4 6.5 %fusion.9 = bf16[2048,64]{0,1:T(8,128)(2,1)S(1)} fusion(s32[4096]{0:T(1024)S(1)} %fusion.38, bf16[4096,128]{0,1:T(8,128)(2,1)S(1)} %convolution_convert_fusion), kind=kOutput, calls=%fused_computation.15 | convolution fusion | flops 1082261504 | bytes 802816 | tf_op jit(solution)/shard_map/dot_general | solution.py:80
  61.9 0.3 copy.24
  62.2 1.0 reshape.66
  63.2 3.4 %all-to-all-start.2 = ((bf16[4,256,128]{2,1,0:T(8,128)(2,1)}), bf16[4,256,128]{2,1,0:T(8,128)(2,1)S(1)}, u32[]{:S(2)}, u32[]{:S(2)}) async-start(bf16[4,256,128]{2,1,0:T(8,128)(2,1)} %reshape.66), calls=%async_computation.2 | async-start | bytes 524288 | tf_op jit(solution)/shard_map/all_to_all | solution.py:83
  66.6 0.1 copy_bitcast_fusion.1
  66.7 1.1 %pad_maximum_fusion.1 = bf16[32,128,128]{1,2,0:T(8,128)(2,1)} fusion(bf16[32,128,64]{1,2,0:T(8,128)(2,1)S(1)} %copy_bitcast_fusion, bf16[32,128,64]{1,2,0:T(8,128)(2,1)S(1)} %copy_bitcast_fusion.1), kind=kLoop, calls=%fused_computation.27 | loop fusion | flops 2097152 | bytes 2097152 | tf_op jit(solution)/shard_map/concatenate | solution.py:18
  67.8 0.0 copy-start.3
  67.8 4.8 %all-to-all-done.2 = bf16[4,256,128]{2,1,0:T(8,128)(2,1)S(1)} async-done(((bf16[4,256,128]{2,1,0:T(8,128)(2,1)}), bf16[4,256,128]{2,1,0:T(8,128)(2,1)S(1)}, u32[]{:S(2)}, u32[]{:S(2)}) %all-to-all-start.2) | async-done | bytes 262176 | tf_op jit(solution)/shard_map/all_to_all | solution.py:83
  72.6 2.8 %all-to-all-start.1 = ((bf16[32,128,128]{1,2,0:T(8,128)(2,1)}), bf16[32,128,128]{1,2,0:T(8,128)(2,1)S(1)}, u32[]{:S(2)}, u32[]{:S(2)}) async-start(bf16[32,128,128]{1,2,0:T(8,128)(2,1)} %pad_maximum_fusion.1), calls=%async_computation.1 | async-start | bytes 2097152 | tf_op jit(solution)/shard_map/all_to_all | solution.py:75
  75.3 0.2 convert_element_type.86
  75.6 0.0 copy-done.3
  75.6 0.0 copy-done.6
  75.6 1.2 %fusion.8 = bf16[2048,128]{1,0:T(8,128)(2,1)} fusion(bf16[2048,128]{1,0:T(8,128)(2,1)S(1)} %copy-done.3, bf16[128,128]{1,0:T(8,128)(2,1)S(1)} %copy-done.6, bf16[2048,64]{1,0:T(8,128)(2,1)S(1)} %convert_element_type.86), kind=kOutput, calls=%fused_computation.14 | convolution fusion | flops 68681728 | bytes 1343488 | tf_op jit(solution)/shard_map/dot_general | solution.py:90
  76.8 24.8 %all-to-all-done.1 = bf16[32,128,128]{1,2,0:T(8,128)(2,1)S(1)} async-done(((bf16[32,128,128]{1,2,0:T(8,128)(2,1)}), bf16[32,128,128]{1,2,0:T(8,128)(2,1)S(1)}, u32[]{:S(2)}, u32[]{:S(2)}) %all-to-all-start.1) | async-done | bytes 1048608 | tf_op jit(solution)/shard_map/all_to_all | solution.py:75
  101.5 0.7 copy.23
  102.2 3.2 %gather_fusion = bf16[1024,128]{1,0:T(8,128)(2,1)S(1)} fusion(bf16[4096,128]{1,0:T(8,128)(2,1)S(1)} %bitcast.28, s32[1024]{0:T(1024)S(1)} %broadcast_clamp_fusion), kind=kCustom, calls=%fused_computation | custom fusion | bytes 528384 | tf_op jit(solution)/shard_map/jit(_take)/gather | solution.py:78
  105.4 0.9 broadcast_select_fusion
  (11 shorter events, 0.1 us)
Async XLA Ops:
  0.6 42.4 %copy-start = (bf16[2048,128]{1,0:T(8,128)(2,1)S(1)}, bf16[2048,128]{1,0:T(8,128)(2,1)}, u32[]{:S(2)}) copy-start(bf16[2048,128]{1,0:T(8,128)(2,1)} %param.11) | copy-start | bytes 1572868
  0.6 1.4 %copy-start.8 = (s32[1024,1]{0,1:T(1,128)S(1)}, s32[1024,1]{0,1:T(1,128)}, u32[]{:S(2)}) copy-start(s32[1024,1]{0,1:T(1,128)} %param.9) | copy-start | bytes 12292
  0.7 1.3 %copy-start.7 = (s32[1024]{0:T(1024)S(1)}, s32[1024]{0:T(1024)}, u32[]{:S(2)}) copy-start(s32[1024]{0:T(1024)} %param.10) | copy-start | bytes 12292
  8.0 7.5 %copy-start.5 = (bf16[64,64]{1,0:T(8,128)(2,1)S(1)}, bf16[64,64]{1,0:T(8,128)(2,1)}, u32[]{:S(2)}) copy-start(bf16[64,64]{1,0:T(8,128)(2,1)} %param.13) | copy-start | bytes 24580
  8.0 34.9 %all-to-all-start = ((bf16[32,130,128]{2,1,0:T(8,128)(2,1)}), bf16[32,130,128]{2,1,0:T(8,128)(2,1)S(1)}, u32[]{:S(2)}, u32[]{:S(2)}) async-start(bf16[32,130,128]{2,1,0:T(8,128)(2,1)} %pad_maximum_fusion), calls=%async_computation | async-start | bytes 2228224 | tf_op jit(solution)/shard_map/all_to_all | solution.py:61
  50.5 1.0 copy-start.1
  52.2 1.0 slice-start
  52.2 1.0 copy-start.4
  53.6 1.2 %copy-start.2 = (bf16[4096,128]{0,1:T(8,128)(2,1)S(1)}, bf16[4096,128]{0,1:T(8,128)(2,1)}, u32[]{:S(2)}) copy-start(bf16[4096,128]{0,1:T(8,128)(2,1)} %copy-done.1) | copy-start | bytes 3145732
  63.2 9.4 %all-to-all-start.2 = ((bf16[4,256,128]{2,1,0:T(8,128)(2,1)}), bf16[4,256,128]{2,1,0:T(8,128)(2,1)S(1)}, u32[]{:S(2)}, u32[]{:S(2)}) async-start(bf16[4,256,128]{2,1,0:T(8,128)(2,1)} %reshape.66), calls=%async_computation.2 | async-start | bytes 524288 | tf_op jit(solution)/shard_map/all_to_all | solution.py:83
  67.8 7.8 %copy-start.3 = (bf16[2048,128]{1,0:T(8,128)(2,1)S(1)}, bf16[2048,128]{1,0:T(8,128)(2,1)}, u32[]{:S(2)}) copy-start(bf16[2048,128]{1,0:T(8,128)(2,1)} %param.15) | copy-start | bytes 1572868
  67.8 7.8 %copy-start.6 = (bf16[128,128]{1,0:T(8,128)(2,1)S(1)}, bf16[128,128]{1,0:T(8,128)(2,1)}, u32[]{:S(2)}) copy-start(bf16[128,128]{1,0:T(8,128)(2,1)} %param.14) | copy-start | bytes 98308
  72.6 29.0 %all-to-all-start.1 = ((bf16[32,128,128]{1,2,0:T(8,128)(2,1)}), bf16[32,128,128]{1,2,0:T(8,128)(2,1)S(1)}, u32[]{:S(2)}, u32[]{:S(2)}) async-start(bf16[32,128,128]{1,2,0:T(8,128)(2,1)} %pad_maximum_fusion.1), calls=%async_computation.1 | async-start | bytes 2097152 | tf_op jit(solution)/shard_map/all_to_all | solution.py:75

commit v4 on v3

--- a/solution.py
+++ b/solution.py
@@ -75,10 +75,10 @@
     returned = lax.all_to_all(
         answers.reshape(devices, capacity, row_width), axes, 0, 0, tiled=True
     ).reshape(slots, row_width)
+    totals = lax.dot_general(selector, gained, contract0, preferred_element_type=f32)
+    face_totals, returned = lax.optimization_barrier((totals.astype(bf16), returned))
     casting_out = jnp.take(returned, slot_index, axis=0)
 
-    totals = lax.dot_general(selector, gained, contract0, preferred_element_type=f32)
-    face_totals = totals.astype(bf16)
     quarter = face_rows // vol_count
     relaid = lax.all_to_all(
         face_totals.reshape(vol_count, quarter * node_count // row_width, row_width),

time: 107 us -> 98.8 us (0.923)
  waiting for transfers between devices: 56.9 us -> 48.9 us
    all_to_all x1, waiting for transfers between devices: 24.8 us -> 19.5 us  [local(): lax.all_to_all(answers.reshape(devices, capacity, row_width), axes, 0, 0,...]
    all_to_all x1, waiting for transfers between devices: 4.75 us -> 1.82 us  [local(): lax.all_to_all(face_totals.reshape(vol_count, quarter * node_count // row...]
  transfers between devices with their start and end apart: 3 -> 3, of which waited for: 3 -> 3; matrix products, arithmetic and copies ran while one was open for 2% -> 11% of each run, Pallas kernels for 0% -> 0%
where the time goes in v4:
time: 98.8 us; the launch traced here: 98.3 us
  waiting for transfers between devices  48.9 us (49%)
  matrix products  18.3 us (19%)
  starting transfers between devices  14.5 us (15%)
  local copies, waits for them, and re-layouts  12.2 us (12%)
  other arithmetic  3.44 us (3%)
    all_to_all x1, waiting for transfers between devices, local(): got = lax.all_to_all(send, axes, 0, 0, tiled=True)  27.6 us
    all_to_all x1, waiting for transfers between devices, local(): lax.all_to_all(answers.reshape(devices, capacity, row_width), axes, 0, 0,...  19.5 us
    dot_general x1, matrix products, local(): jnp.dot(selector, mold_faces, preferred_element_type=f32).astype(bf16)  7.5 us
    all_to_all x1, starting transfers between devices, local(): got = lax.all_to_all(send, axes, 0, 0, tiled=True)  7.32 us
    dot_general x1, matrix products, local(): lax.dot_general(selector, gained, contract0, preferred_element_type=f32)  6.5 us
    scatter x1, local copies, waits for them, and re-layouts, local(): send_rows = jnp.zeros((slots, row_width), bf16).at[slot_index].set(casting)  3.89 us
    all_to_all x1, starting transfers between devices, local(): lax.all_to_all(answers.reshape(devices, capacity, row_width), axes, 0, 0,...  3.81 us
    all_to_all x1, starting transfers between devices, local(): lax.all_to_all(face_totals.reshape(vol_count, quarter * node_count // row...  3.41 us
  transfers between devices with their start and end apart: 3, of which 3 were waited for; matrix products, arithmetic and copies ran while one was open for 11% of the time, Pallas kernels for 0%

profile of v4, /device:TPU:0, one launch (start us, length us, event | category | flops | bytes accessed | tf_op | source)
XLA Modules:
  0.0 98.3 jit_solution(14745535889982945207)
XLA Ops:
  0.6 0.0 copy-start
  0.6 0.0 copy-start.8
  0.7 0.0 copy-start.7
  0.7 1.3 %fusion.11 = f32[1024]{0:T(1024)S(1)} fusion(s32[1024]{0:T(1024)} %bitcast.35), kind=kOutput, calls=%fused_computation.17 | convolution fusion | flops 68353024 | bytes 8192 | tf_op jit(solution)/shard_map/dot_general | solution.py:41
  2.0 0.0 copy-done.7
  2.0 0.0 copy-done.8
  2.0 0.5 fusion.12
  2.5 0.5 fusion.13
  3.0 3.9 %scatter_custom_fusion = bf16[4096,128]{1,0:T(8,128)(2,1)S(1)} fusion(s32[1024]{0:T(1024)S(1)} %bitcast.32, bf16[1024,128]{1,0:T(8,128)(2,1)} %param.8, bf16[]{:T(256)} %constant.54.clone.1), kind=kCustom, calls=%fused_computation.38 | custom fusion | bytes 1049088 | tf_op jit(solution)/shard_map/scatter | solution.py:57
  6.9 1.1 %pad_maximum_fusion = bf16[32,130,128]{2,1,0:T(8,128)(2,1)} fusion(bf16[32,1,128]{2,1,0:T(2,128)(2,1)S(1)} %copy.18, bf16[32,1,128]{2,1,0:T(2,128)(2,1)S(1)} %copy.17, bf16[32,128,128]{2,1,0:T(8,128)(2,1)S(1)} %bitcast.30), kind=kLoop, calls=%fused_computation.18 | loop fusion | flops 3194880 | bytes 2129920 | tf_op jit(solution)/shard_map/concatenate | solution.py:58
  8.0 0.0 copy-start.5
  8.1 7.3 %all-to-all-start = ((bf16[32,130,128]{2,1,0:T(8,128)(2,1)}), bf16[32,130,128]{2,1,0:T(8,128)(2,1)S(1)}, u32[]{:S(2)}, u32[]{:S(2)}) async-start(bf16[32,130,128]{2,1,0:T(8,128)(2,1)} %pad_maximum_fusion), calls=%async_computation | async-start | bytes 2228224 | tf_op jit(solution)/shard_map/all_to_all | solution.py:61
  15.4 0.0 copy-done.5
  15.4 27.6 %all-to-all-done = bf16[32,130,128]{2,1,0:T(8,128)(2,1)S(1)} async-done(((bf16[32,130,128]{2,1,0:T(8,128)(2,1)}), bf16[32,130,128]{2,1,0:T(8,128)(2,1)S(1)}, u32[]{:S(2)}, u32[]{:S(2)}) %all-to-all-start) | async-done | bytes 1064992 | tf_op jit(solution)/shard_map/all_to_all | solution.py:61
  43.0 0.0 copy-done
  43.0 7.5 %fusion.4 = bf16[4096,128]{0,1:T(8,128)(2,1)S(1)} fusion(bf16[2048,128]{1,0:T(8,128)(2,1)S(1)} %copy-done, s32[4096]{0:T(1024)S(1)} %fusion.38), kind=kOutput, calls=%fused_computation.7 | convolution fusion | flops 2156396544 | bytes 1589248 | tf_op jit(solution)/shard_map/dot_general | solution.py:69
  50.5 0.0 copy-start.1
  50.6 0.1 slice.47
  50.7 0.8 copy-done.1
  51.5 0.4 fusion.53
  51.9 0.3 copy.28
  52.2 0.0 slice-start
  52.3 0.0 copy-start.4
  52.3 0.3 copy.27
  52.6 0.0 copy-start.2
  52.6 0.7 slice-done
  53.3 0.0 copy-done.4
  53.3 0.4 fusion.14
  53.6 0.2 copy-done.2
  53.9 0.6 convolution_convert_fusion
  54.4 0.3 copy_bitcast_fusion
  54.7 1.1 %pad_maximum_fusion.1 = bf16[32,128,128]{1,2,0:T(8,128)(2,1)} fusion(bf16[32,128,64]{1,2,0:T(8,128)(2,1)S(1)} %get-tuple-element.12, bf16[32,128,64]{1,2,0:T(8,128)(2,1)S(1)} %get-tuple-element.13), kind=kLoop, calls=%fused_computation.27 | loop fusion | flops 2097152 | bytes 2097152 | tf_op jit(solution)/shard_map/concatenate | solution.py:18
  55.8 3.8 %all-to-all-start.1 = ((bf16[32,128,128]{1,2,0:T(8,128)(2,1)}), bf16[32,128,128]{1,2,0:T(8,128)(2,1)S(1)}, u32[]{:S(2)}, u32[]{:S(2)}) async-start(bf16[32,128,128]{1,2,0:T(8,128)(2,1)} %pad_maximum_fusion.1), calls=%async_computation.1 | async-start | bytes 2097152 | tf_op jit(solution)/shard_map/all_to_all | solution.py:75
  59.6 6.5 %fusion.9 = bf16[2048,64]{0,1:T(8,128)(2,1)S(1)} fusion(s32[4096]{0:T(1024)S(1)} %fusion.38, bf16[4096,128]{0,1:T(8,128)(2,1)S(1)} %convolution_convert_fusion), kind=kOutput, calls=%fused_computation.15 | convolution fusion | flops 1082261504 | bytes 802816 | tf_op jit(solution)/shard_map/dot_general | solution.py:78
  66.1 19.5 %all-to-all-done.1 = bf16[32,128,128]{1,2,0:T(8,128)(2,1)S(1)} async-done(((bf16[32,128,128]{1,2,0:T(8,128)(2,1)}), bf16[32,128,128]{1,2,0:T(8,128)(2,1)S(1)}, u32[]{:S(2)}, u32[]{:S(2)}) %all-to-all-start.1) | async-done | bytes 1048608 | tf_op jit(solution)/shard_map/all_to_all | solution.py:75
  85.6 0.7 copy.23
  86.3 0.3 copy.24
  86.6 1.0 reshape.66
  87.5 3.4 %all-to-all-start.2 = ((bf16[4,256,128]{2,1,0:T(8,128)(2,1)}), bf16[4,256,128]{2,1,0:T(8,128)(2,1)S(1)}, u32[]{:S(2)}, u32[]{:S(2)}) async-start(bf16[4,256,128]{2,1,0:T(8,128)(2,1)} %reshape.66), calls=%async_computation.2 | async-start | bytes 524288 | tf_op jit(solution)/shard_map/all_to_all | solution.py:83
  90.9 3.2 %gather_fusion = bf16[1024,128]{1,0:T(8,128)(2,1)S(1)} fusion(bf16[4096,128]{1,0:T(8,128)(2,1)S(1)} %bitcast.28, s32[1024]{0:T(1024)S(1)} %broadcast_clamp_fusion), kind=kCustom, calls=%fused_computation | custom fusion | bytes 528384 | tf_op jit(solution)/shard_map/jit(_take)/gather | solution.py:80
  94.2 0.0 copy-start.3
  94.2 0.0 copy-start.6
  94.2 0.9 broadcast_select_fusion
  95.1 1.8 %all-to-all-done.2 = bf16[4,256,128]{2,1,0:T(8,128)(2,1)S(1)} async-done(((bf16[4,256,128]{2,1,0:T(8,128)(2,1)}), bf16[4,256,128]{2,1,0:T(8,128)(2,1)S(1)}, u32[]{:S(2)}, u32[]{:S(2)}) %all-to-all-start.2) | async-done | bytes 262176 | tf_op jit(solution)/shard_map/all_to_all | solution.py:83
  96.9 0.2 convert_element_type.86
  97.2 0.0 copy-done.3
  97.2 0.0 copy-done.6
  97.2 1.1 %fusion.8 = bf16[2048,128]{1,0:T(8,128)(2,1)} fusion(bf16[2048,128]{1,0:T(8,128)(2,1)S(1)} %copy-done.3, bf16[128,128]{1,0:T(8,128)(2,1)S(1)} %copy-done.6, bf16[2048,64]{1,0:T(8,128)(2,1)S(1)} %convert_element_type.86), kind=kOutput, calls=%fused_computation.14 | convolution fusion | flops 68681728 | bytes 1343488 | tf_op jit(solution)/shard_map/dot_general | solution.py:90
  (10 shorter events, 0.1 us)
Async XLA Ops:
  0.6 42.4 %copy-start = (bf16[2048,128]{1,0:T(8,128)(2,1)S(1)}, bf16[2048,128]{1,0:T(8,128)(2,1)}, u32[]{:S(2)}) copy-start(bf16[2048,128]{1,0:T(8,128)(2,1)} %param.11) | copy-start | bytes 1572868
  0.6 1.4 %copy-start.8 = (s32[1024,1]{0,1:T(1,128)S(1)}, s32[1024,1]{0,1:T(1,128)}, u32[]{:S(2)}) copy-start(s32[1024,1]{0,1:T(1,128)} %param.9) | copy-start | bytes 12292
  0.7 1.3 %copy-start.7 = (s32[1024]{0:T(1024)S(1)}, s32[1024]{0:T(1024)}, u32[]{:S(2)}) copy-start(s32[1024]{0:T(1024)} %param.10) | copy-start | bytes 12292
  8.0 7.3 %copy-start.5 = (bf16[64,64]{1,0:T(8,128)(2,1)S(1)}, bf16[64,64]{1,0:T(8,128)(2,1)}, u32[]{:S(2)}) copy-start(bf16[64,64]{1,0:T(8,128)(2,1)} %param.13) | copy-start | bytes 24580
  8.1 34.9 %all-to-all-start = ((bf16[32,130,128]{2,1,0:T(8,128)(2,1)}), bf16[32,130,128]{2,1,0:T(8,128)(2,1)S(1)}, u32[]{:S(2)}, u32[]{:S(2)}) async-start(bf16[32,130,128]{2,1,0:T(8,128)(2,1)} %pad_maximum_fusion), calls=%async_computation | async-start | bytes 2228224 | tf_op jit(solution)/shard_map/all_to_all | solution.py:61
  50.5 1.0 copy-start.1
  52.2 1.0 %slice-start = ((bf16[4096,128]{0,1:T(8,128)(2,1)}), bf16[4096,64]{0,1:T(8,128)(2,1)S(1)}, s32[]{:S(2)}) async-start(bf16[4096,128]{0,1:T(8,128)(2,1)} %copy-done.1), calls=%async_computation.3 | async-start | bytes 1048576 | tf_op jit(solution)/shard_map/slice | solution.py:10
  52.3 1.0 %copy-start.4 = (bf16[64,64]{1,0:T(8,128)(2,1)S(1)}, bf16[64,64]{1,0:T(8,128)(2,1)}, u32[]{:S(2)}) copy-start(bf16[64,64]{1,0:T(8,128)(2,1)} %param.12) | copy-start | bytes 24580
  52.6 1.3 %copy-start.2 = (bf16[4096,128]{0,1:T(8,128)(2,1)S(1)}, bf16[4096,128]{0,1:T(8,128)(2,1)}, u32[]{:S(2)}) copy-start(bf16[4096,128]{0,1:T(8,128)(2,1)} %copy-done.1) | copy-start | bytes 3145732
  55.8 29.8 %all-to-all-start.1 = ((bf16[32,128,128]{1,2,0:T(8,128)(2,1)}), bf16[32,128,128]{1,2,0:T(8,128)(2,1)S(1)}, u32[]{:S(2)}, u32[]{:S(2)}) async-start(bf16[32,128,128]{1,2,0:T(8,128)(2,1)} %pad_maximum_fusion.1), calls=%async_computation.1 | async-start | bytes 2097152 | tf_op jit(solution)/shard_map/all_to_all | solution.py:75
  87.5 9.4 %all-to-all-start.2 = ((bf16[4,256,128]{2,1,0:T(8,128)(2,1)}), bf16[4,256,128]{2,1,0:T(8,128)(2,1)S(1)}, u32[]{:S(2)}, u32[]{:S(2)}) async-start(bf16[4,256,128]{2,1,0:T(8,128)(2,1)} %reshape.66), calls=%async_computation.2 | async-start | bytes 524288 | tf_op jit(solution)/shard_map/all_to_all | solution.py:83
  94.2 3.0 %copy-start.3 = (bf16[2048,128]{1,0:T(8,128)(2,1)S(1)}, bf16[2048,128]{1,0:T(8,128)(2,1)}, u32[]{:S(2)}) copy-start(bf16[2048,128]{1,0:T(8,128)(2,1)} %param.15) | copy-start | bytes 1572868
  94.2 3.0 %copy-start.6 = (bf16[128,128]{1,0:T(8,128)(2,1)S(1)}, bf16[128,128]{1,0:T(8,128)(2,1)}, u32[]{:S(2)}) copy-start(bf16[128,128]{1,0:T(8,128)(2,1)} %param.14) | copy-start | bytes 98308

commit v5 on v4

--- a/solution.py
+++ b/solution.py
@@ -54,10 +54,10 @@
     id_flat = jnp.pad(id_flat, ((0, 0), (0, id_height * row_width - id_count)))
     id_rows = id_flat.reshape(devices, id_height, row_width)
 
-    send_rows = jnp.zeros((slots, row_width), bf16).at[slot_index].set(casting)
-    send = jnp.concatenate(
-        [send_rows.reshape(devices, capacity, row_width), id_rows.astype(bf16)], axis=1
-    )
+    block = capacity + id_height
+    send = jnp.zeros((devices, block, row_width), bf16).at[:, capacity:, :].set(id_rows.astype(bf16))
+    send = send.reshape(devices * block, row_width).at[target * block + position].set(casting)
+    send = send.reshape(devices, block, row_width)
     got = lax.all_to_all(send, axes, 0, 0, tiled=True)
     got_rows = got[:, :capacity, :].reshape(slots, row_width)
     got_code = got[:, capacity:, :].astype(f32).reshape(devices, id_height * row_width)
@@ -76,12 +76,13 @@
         answers.reshape(devices, capacity, row_width), axes, 0, 0, tiled=True
     ).reshape(slots, row_width)
     totals = lax.dot_general(selector, gained, contract0, preferred_element_type=f32)
-    face_totals, returned = lax.optimization_barrier((totals.astype(bf16), returned))
+    quarter = face_rows // vol_count
+    face_totals = totals.astype(bf16).reshape(vol_count, quarter * node_count // row_width, row_width)
+    face_totals, returned = lax.optimization_barrier((face_totals, returned))
     casting_out = jnp.take(returned, slot_index, axis=0)
 
-    quarter = face_rows // vol_count
     relaid = lax.all_to_all(
-        face_totals.reshape(vol_count, quarter * node_count // row_width, row_width),
+        face_totals,
         "vol",
         split_axis=0,
         concat_axis=0,

time: 98.8 us -> 98.6 us (level)
  local copies, waits for them, and re-layouts: 12.2 us -> 14.3 us
  waiting for transfers between devices: 48.9 us -> 47.6 us
  other arithmetic: 3.44 us -> 2.4 us
    reshape x1 -> x3, local copies, waits for them, and re-layouts: 0.96 us -> 2.44 us  [the longest x1 1.16 us: local(): send = send.reshape(devices, block, row_width)]
    all_to_all x1, waiting for transfers between devices: 19.5 us -> 18.2 us  [local(): lax.all_to_all(answers.reshape(devices, capacity, row_width), axes, 0, 0,...]
    concatenate x1 -> x0, other arithmetic: 1.11 us -> none  [local(): jnp.concatenate([send_rows.reshape(devices, capacity, row_width), id_rows...]
    unnamed x20 -> x23, local copies, waits for them, and re-layouts: 1.77 us -> 2.39 us
    scatter x1 -> x2, local copies, waits for them, and re-layouts: 3.89 us -> 3.87 us  [the longest x1 3.73 us: local(): send.reshape(devices * block, row_width).at[target * block + position]]
  transfers between devices with their start and end apart: 3 -> 3, of which waited for: 3 -> 3; matrix products, arithmetic and copies ran while one was open for 11% -> 12% of each run, Pallas kernels for 0% -> 0%
where the time goes in v5:
time: 98.6 us; the launch traced here: 98.1 us
  waiting for transfers between devices  47.6 us (48%)
  matrix products  18.3 us (19%)
  starting transfers between devices  14.5 us (15%)
  local copies, waits for them, and re-layouts  14.3 us (15%)
  other arithmetic  2.4 us (2%)
    all_to_all x1, waiting for transfers between devices, local(): got = lax.all_to_all(send, axes, 0, 0, tiled=True)  27.6 us
    all_to_all x1, waiting for transfers between devices, local(): lax.all_to_all(answers.reshape(devices, capacity, row_width), axes, 0, 0,...  18.2 us
    dot_general x1, matrix products, local(): jnp.dot(selector, mold_faces, preferred_element_type=f32).astype(bf16)  7.5 us
    all_to_all x1, starting transfers between devices, local(): got = lax.all_to_all(send, axes, 0, 0, tiled=True)  7.32 us
    dot_general x1, matrix products, local(): lax.dot_general(selector, gained, contract0, preferred_element_type=f32)  6.51 us
    all_to_all x1, starting transfers between devices, local(): lax.all_to_all(answers.reshape(devices, capacity, row_width), axes, 0, 0,...  3.8 us
    scatter x1, local copies, waits for them, and re-layouts, local(): send.reshape(devices * block, row_width).at[target * block + position]  3.73 us
    all_to_all x1, starting transfers between devices, local(): lax.all_to_all(face_totals, 'vol', split_axis=0, concat_axis=0, tiled=True)  3.42 us
  transfers between devices with their start and end apart: 3, of which 3 were waited for; matrix products, arithmetic and copies ran while one was open for 12% of the time, Pallas kernels for 0%

profile of v5, /device:TPU:0, one launch (start us, length us, event | category | flops | bytes accessed | tf_op | source)
XLA Modules:
  0.0 98.1 jit_solution(17429744484916116036)
XLA Ops:
  0.6 0.0 copy-start
  0.6 0.0 copy-start.8
  0.7 0.0 copy-start.9
  0.7 1.3 %fusion.11 = f32[1024]{0:T(1024)S(1)} fusion(s32[1024]{0:T(1024)} %bitcast.35), kind=kOutput, calls=%fused_computation.17 | convolution fusion | flops 68353024 | bytes 8192 | tf_op jit(solution)/shard_map/dot_general | solution.py:41
  2.0 0.0 copy-done.9
  2.0 0.0 copy-done.8
  2.0 0.5 fusion.12
  2.5 0.5 fusion.13
  3.0 0.1 scatter.12.clone
  3.1 0.0 copy-start.4
  3.2 0.3 reshape.98
  3.5 0.6 copy-done.4
  4.1 3.7 %scatter_fusion = bf16[4160,128]{1,0:T(8,128)(2,1)S(1)} fusion(bf16[4160,128]{1,0:T(8,128)(2,1)S(1)} %reshape.98, s32[1024]{0:T(1024)S(1)} %bitcast.32, bf16[1024,128]{1,0:T(8,128)(2,1)S(1)} %copy-done.4), kind=kCustom, calls=%fused_computation.1 | custom fusion | bytes 790528 | tf_op jit(solution)/shard_map/scatter | solution.py:59
  7.8 1.2 %reshape.99 = bf16[32,130,128]{2,1,0:T(8,128)(2,1)} reshape(bf16[4160,128]{1,0:T(8,128)(2,1)S(1)} %scatter_fusion) | data formatting | bytes 2129920 | tf_op jit(solution)/shard_map/reshape | solution.py:60
  9.0 7.3 %all-to-all-start = ((bf16[32,130,128]{2,1,0:T(8,128)(2,1)}), bf16[32,130,128]{2,1,0:T(8,128)(2,1)S(1)}, u32[]{:S(2)}, u32[]{:S(2)}) async-start(bf16[32,130,128]{2,1,0:T(8,128)(2,1)} %reshape.99), calls=%async_computation | async-start | bytes 2228224 | tf_op jit(solution)/shard_map/all_to_all | solution.py:61
  16.3 0.0 copy-done.6
  16.4 27.6 %all-to-all-done = bf16[32,130,128]{2,1,0:T(8,128)(2,1)S(1)} async-done(((bf16[32,130,128]{2,1,0:T(8,128)(2,1)}), bf16[32,130,128]{2,1,0:T(8,128)(2,1)S(1)}, u32[]{:S(2)}, u32[]{:S(2)}) %all-to-all-start) | async-done | bytes 1064992 | tf_op jit(solution)/shard_map/all_to_all | solution.py:61
  44.0 0.0 copy-done
  44.0 7.5 %fusion.4 = bf16[4096,128]{0,1:T(8,128)(2,1)S(1)} fusion(bf16[2048,128]{1,0:T(8,128)(2,1)S(1)} %copy-done, s32[4096]{0:T(1024)S(1)} %bitcast.33), kind=kOutput, calls=%fused_computation.7 | convolution fusion | flops 2156396544 | bytes 1589248 | tf_op jit(solution)/shard_map/dot_general | solution.py:69
  51.5 0.0 copy-start.1
  51.5 0.1 slice.68
  51.7 0.8 copy-done.1
  52.5 0.4 fusion.50
  52.9 0.3 copy.23
  53.2 0.0 slice-start
  53.2 0.0 copy-start.5
  53.2 0.3 copy.22
  53.6 0.7 slice-done
  54.3 0.0 copy-done.5
  54.3 0.4 fusion.14
  54.6 0.2 copy-done.2
  54.9 0.6 convolution_convert_fusion
  55.4 0.3 copy_bitcast_fusion
  55.7 1.1 %pad_maximum_fusion = bf16[32,128,128]{1,2,0:T(8,128)(2,1)} fusion(bf16[32,128,64]{1,2,0:T(8,128)(2,1)S(1)} %get-tuple-element.24, bf16[32,128,64]{1,2,0:T(8,128)(2,1)S(1)} %get-tuple-element.25), kind=kLoop, calls=%fused_computation.26 | loop fusion | flops 2097152 | bytes 2097152 | tf_op jit(solution)/shard_map/concatenate | solution.py:18
  56.8 3.8 %all-to-all-start.1 = ((bf16[32,128,128]{1,2,0:T(8,128)(2,1)}), bf16[32,128,128]{1,2,0:T(8,128)(2,1)S(1)}, u32[]{:S(2)}, u32[]{:S(2)}) async-start(bf16[32,128,128]{1,2,0:T(8,128)(2,1)} %pad_maximum_fusion), calls=%async_computation.1 | async-start | bytes 2097152 | tf_op jit(solution)/shard_map/all_to_all | solution.py:75
  60.6 6.5 %fusion.9 = bf16[2048,64]{0,1:T(8,128)(2,1)S(1)} fusion(s32[4096]{0:T(1024)S(1)} %bitcast.34, bf16[4096,128]{0,1:T(8,128)(2,1)S(1)} %convolution_convert_fusion), kind=kOutput, calls=%fused_computation.15 | convolution fusion | flops 1082261504 | bytes 802816 | tf_op jit(solution)/shard_map/dot_general | solution.py:78
  67.1 0.3 copy.17
  67.4 1.0 reshape.101
  68.4 18.2 %all-to-all-done.1 = bf16[32,128,128]{1,2,0:T(8,128)(2,1)S(1)} async-done(((bf16[32,128,128]{1,2,0:T(8,128)(2,1)}), bf16[32,128,128]{1,2,0:T(8,128)(2,1)S(1)}, u32[]{:S(2)}, u32[]{:S(2)}) %all-to-all-start.1) | async-done | bytes 1048608 | tf_op jit(solution)/shard_map/all_to_all | solution.py:75
  86.6 0.7 copy.20
  87.3 3.4 %all-to-all-start.2 = ((bf16[4,256,128]{2,1,0:T(8,128)(2,1)}), bf16[4,256,128]{2,1,0:T(8,128)(2,1)S(1)}, u32[]{:S(2)}, u32[]{:S(2)}) async-start(bf16[4,256,128]{2,1,0:T(8,128)(2,1)} %reshape.101), calls=%async_computation.2 | async-start | bytes 524288 | tf_op jit(solution)/shard_map/all_to_all | solution.py:84
  90.7 3.2 %gather_fusion = bf16[1024,128]{1,0:T(8,128)(2,1)S(1)} fusion(bf16[4096,128]{1,0:T(8,128)(2,1)S(1)} %bitcast.27, s32[1024]{0:T(1024)S(1)} %broadcast_clamp_fusion), kind=kCustom, calls=%fused_computation | custom fusion | bytes 528384 | tf_op jit(solution)/shard_map/jit(_take)/gather | solution.py:82
  93.9 0.0 copy-start.3
  93.9 0.0 copy-start.7
  93.9 0.9 broadcast_select_fusion
  94.8 1.8 %all-to-all-done.2 = bf16[4,256,128]{2,1,0:T(8,128)(2,1)S(1)} async-done(((bf16[4,256,128]{2,1,0:T(8,128)(2,1)}), bf16[4,256,128]{2,1,0:T(8,128)(2,1)S(1)}, u32[]{:S(2)}, u32[]{:S(2)}) %all-to-all-start.2) | async-done | bytes 262176 | tf_op jit(solution)/shard_map/all_to_all | solution.py:84
  96.7 0.2 convert_element_type.87
  96.9 1.1 %fusion.8 = bf16[2048,128]{1,0:T(8,128)(2,1)} fusion(bf16[2048,128]{1,0:T(8,128)(2,1)S(1)} %copy-done.3, bf16[128,128]{1,0:T(8,128)(2,1)S(1)} %copy-done.7, bf16[2048,64]{1,0:T(8,128)(2,1)S(1)} %convert_element_type.87), kind=kOutput, calls=%fused_computation.14 | convolution fusion | flops 68681728 | bytes 1343488 | tf_op jit(solution)/shard_map/dot_general | solution.py:91
  (14 shorter events, 0.1 us)
Async XLA Ops:
  0.6 43.4 %copy-start = (bf16[2048,128]{1,0:T(8,128)(2,1)S(1)}, bf16[2048,128]{1,0:T(8,128)(2,1)}, u32[]{:S(2)}) copy-start(bf16[2048,128]{1,0:T(8,128)(2,1)} %param.13) | copy-start | bytes 1572868
  0.6 1.4 %copy-start.8 = (s32[1024,1]{0,1:T(1,128)S(1)}, s32[1024,1]{0,1:T(1,128)}, u32[]{:S(2)}) copy-start(s32[1024,1]{0,1:T(1,128)} %param.11) | copy-start | bytes 12292
  0.7 1.3 %copy-start.9 = (s32[1024]{0:T(1024)S(1)}, s32[1024]{0:T(1024)}, u32[]{:S(2)}) copy-start(s32[1024]{0:T(1024)} %param.12) | copy-start | bytes 12292
  3.1 1.0 copy-start.4
  9.0 7.3 %copy-start.6 = (bf16[64,64]{1,0:T(8,128)(2,1)S(1)}, bf16[64,64]{1,0:T(8,128)(2,1)}, u32[]{:S(2)}) copy-start(bf16[64,64]{1,0:T(8,128)(2,1)} %param.15) | copy-start | bytes 24580
  9.0 34.9 %all-to-all-start = ((bf16[32,130,128]{2,1,0:T(8,128)(2,1)}), bf16[32,130,128]{2,1,0:T(8,128)(2,1)S(1)}, u32[]{:S(2)}, u32[]{:S(2)}) async-start(bf16[32,130,128]{2,1,0:T(8,128)(2,1)} %reshape.99), calls=%async_computation | async-start | bytes 2228224 | tf_op jit(solution)/shard_map/all_to_all | solution.py:61
  51.5 1.0 %copy-start.1 = (bf16[4096,128]{0,1:T(8,128)(2,1)}, bf16[4096,128]{0,1:T(8,128)(2,1)S(1)}, u32[]{:S(2)}) copy-start(bf16[4096,128]{0,1:T(8,128)(2,1)S(1)} %fusion.4) | copy-start | bytes 3145732
  53.2 1.0 %slice-start = ((bf16[4096,128]{0,1:T(8,128)(2,1)}), bf16[4096,64]{0,1:T(8,128)(2,1)S(1)}, s32[]{:S(2)}) async-start(bf16[4096,128]{0,1:T(8,128)(2,1)} %copy-done.1), calls=%async_computation.3 | async-start | bytes 1048576 | tf_op jit(solution)/shard_map/slice | solution.py:10
  53.2 1.0 %copy-start.5 = (bf16[64,64]{1,0:T(8,128)(2,1)S(1)}, bf16[64,64]{1,0:T(8,128)(2,1)}, u32[]{:S(2)}) copy-start(bf16[64,64]{1,0:T(8,128)(2,1)} %param.14) | copy-start | bytes 24580
  53.6 1.3 %copy-start.2 = (bf16[4096,128]{0,1:T(8,128)(2,1)S(1)}, bf16[4096,128]{0,1:T(8,128)(2,1)}, u32[]{:S(2)}) copy-start(bf16[4096,128]{0,1:T(8,128)(2,1)} %copy-done.1) | copy-start | bytes 3145732
  56.8 29.8 %all-to-all-start.1 = ((bf16[32,128,128]{1,2,0:T(8,128)(2,1)}), bf16[32,128,128]{1,2,0:T(8,128)(2,1)S(1)}, u32[]{:S(2)}, u32[]{:S(2)}) async-start(bf16[32,128,128]{1,2,0:T(8,128)(2,1)} %pad_maximum_fusion), calls=%async_computation.1 | async-start | bytes 2097152 | tf_op jit(solution)/shard_map/all_to_all | solution.py:75
  87.3 9.4 %all-to-all-start.2 = ((bf16[4,256,128]{2,1,0:T(8,128)(2,1)}), bf16[4,256,128]{2,1,0:T(8,128)(2,1)S(1)}, u32[]{:S(2)}, u32[]{:S(2)}) async-start(bf16[4,256,128]{2,1,0:T(8,128)(2,1)} %reshape.101), calls=%async_computation.2 | async-start | bytes 524288 | tf_op jit(solution)/shard_map/all_to_all | solution.py:84
  93.9 3.0 %copy-start.3 = (bf16[2048,128]{1,0:T(8,128)(2,1)S(1)}, bf16[2048,128]{1,0:T(8,128)(2,1)}, u32[]{:S(2)}) copy-start(bf16[2048,128]{1,0:T(8,128)(2,1)} %param.17) | copy-start | bytes 1572868
  93.9 3.0 %copy-start.7 = (bf16[128,128]{1,0:T(8,128)(2,1)S(1)}, bf16[128,128]{1,0:T(8,128)(2,1)}, u32[]{:S(2)}) copy-start(bf16[128,128]{1,0:T(8,128)(2,1)} %param.16) | copy-start | bytes 98308

commit v6 on v5

--- a/solution.py
+++ b/solution.py
@@ -54,13 +54,14 @@
     id_flat = jnp.pad(id_flat, ((0, 0), (0, id_height * row_width - id_count)))
     id_rows = id_flat.reshape(devices, id_height, row_width)
 
-    block = capacity + id_height
-    send = jnp.zeros((devices, block, row_width), bf16).at[:, capacity:, :].set(id_rows.astype(bf16))
+    block = -(-(capacity + id_height) // 16) * 16
+    send = jnp.zeros((devices, block, row_width), bf16)
+    send = send.at[:, capacity:capacity + id_height, :].set(id_rows.astype(bf16))
     send = send.reshape(devices * block, row_width).at[target * block + position].set(casting)
     send = send.reshape(devices, block, row_width)
     got = lax.all_to_all(send, axes, 0, 0, tiled=True)
     got_rows = got[:, :capacity, :].reshape(slots, row_width)
-    got_code = got[:, capacity:, :].astype(f32).reshape(devices, id_height * row_width)
+    got_code = got[:, capacity:capacity + id_height, :].astype(f32).reshape(devices, id_height * row_width)
     got_code = got_code[:, :id_count].reshape(devices, 2, capacity)
     got_ids = (got_code[:, 0, :] * 64.0 + got_code[:, 1, :]).astype(jnp.int32).reshape(slots) - 1
 

time: 98.6 us -> 101 us (1.024)
  waiting for transfers between devices: 47.6 us -> 49 us
    scatter x1, local copies, waits for them, and re-layouts: 3.73 us -> 5.64 us  [local(): send.reshape(devices * block, row_width).at[target * block + position]]
    reshape x2 -> x0, local copies, waits for them, and re-layouts: 1.48 us -> none  [the longest x1 1.16 us: local(): send = send.reshape(devices, block, row_width)]
    all_to_all x1, waiting for transfers between devices: 27.6 us -> 29 us  [local(): got = lax.all_to_all(send, axes, 0, 0, tiled=True)]
    scatter x1, local copies, waits for them, and re-layouts: 0.15 us -> 1.19 us  [local(): send.at[:, capacity:capacity + id_height, :].set(id_rows.astype(bf16))]
where the time goes in v6:
time: 101 us; the launch traced here: 100 us
  waiting for transfers between devices  49 us (49%)
  matrix products  18.3 us (18%)
  local copies, waits for them, and re-layouts  15.2 us (15%)
  starting transfers between devices  14.5 us (14%)
  other arithmetic  2.4 us (2%)
    all_to_all x1, waiting for transfers between devices, local(): got = lax.all_to_all(send, axes, 0, 0, tiled=True)  29 us
    all_to_all x1, waiting for transfers between devices, local(): lax.all_to_all(answers.reshape(devices, capacity, row_width), axes, 0, 0,...  18.2 us
    dot_general x1, matrix products, local(): jnp.dot(selector, mold_faces, preferred_element_type=f32).astype(bf16)  7.5 us
    all_to_all x1, starting transfers between devices, local(): got = lax.all_to_all(send, axes, 0, 0, tiled=True)  7.32 us
    dot_general x1, matrix products, local(): lax.dot_general(selector, gained, contract0, preferred_element_type=f32)  6.51 us
    scatter x1, local copies, waits for them, and re-layouts, local(): send.reshape(devices * block, row_width).at[target * block + position]  5.64 us
    all_to_all x1, starting transfers between devices, local(): lax.all_to_all(answers.reshape(devices, capacity, row_width), axes, 0, 0,...  3.8 us
    all_to_all x1, starting transfers between devices, local(): lax.all_to_all(face_totals, 'vol', split_axis=0, concat_axis=0, tiled=True)  3.42 us
  transfers between devices with their start and end apart: 3, of which 3 were waited for; matrix products, arithmetic and copies ran while one was open for 12% of the time, Pallas kernels for 0%

profile of v6, /device:TPU:0, one launch (start us, length us, event | category | flops | bytes accessed | tf_op | source)
XLA Modules:
  0.0 100.4 jit_solution(17758768775652368158)
XLA Ops:
  0.6 0.0 copy-start
  0.6 0.0 copy-start.8
  0.7 0.0 copy-start.9
  0.7 1.3 %fusion.11 = f32[1024]{0:T(1024)S(1)} fusion(s32[1024]{0:T(1024)} %bitcast.37), kind=kOutput, calls=%fused_computation.17 | convolution fusion | flops 68353024 | bytes 8192 | tf_op jit(solution)/shard_map/dot_general | solution.py:41
  2.0 0.0 copy-start.4
  2.0 0.0 copy-done.9
  2.0 0.0 copy-done.8
  2.0 0.5 fusion.12
  2.5 0.5 fusion.13
  3.0 1.2 %scatter.12.clone = bf16[32,144,128]{2,1,0:T(8,128)(2,1)} pad(bf16[32,2,128]{2,1,0:T(2,128)(2,1)S(1)} %copy.24, bf16[]{:T(256)} %constant.85.clone.1), padding=0_0x128_14x0_0 | pad | bytes 1196034 | tf_op jit(solution)/shard_map/scatter | solution.py:59
  4.2 0.0 copy-done.4
  4.2 5.6 %scatter_fusion = bf16[4608,128]{1,0:T(8,128)(2,1)} fusion(bf16[4608,128]{1,0:T(8,128)(2,1)} %bitcast.4, s32[1024]{0:T(1024)S(1)} %bitcast.34, bf16[1024,128]{1,0:T(8,128)(2,1)S(1)} %copy-done.4), kind=kCustom, calls=%fused_computation.1 | custom fusion | bytes 790528 | tf_op jit(solution)/shard_map/scatter | solution.py:60
  9.9 7.3 %all-to-all-start = ((bf16[32,144,128]{2,1,0:T(8,128)(2,1)}), bf16[32,144,128]{2,1,0:T(8,128)(2,1)S(1)}, u32[]{:S(2)}, u32[]{:S(2)}) async-start(bf16[32,144,128]{2,1,0:T(8,128)(2,1)} %bitcast.6), calls=%async_computation | async-start | bytes 2359296 | tf_op jit(solution)/shard_map/all_to_all | solution.py:62
  17.2 0.0 copy-done.6
  17.2 29.0 %all-to-all-done = bf16[32,144,128]{2,1,0:T(8,128)(2,1)S(1)} async-done(((bf16[32,144,128]{2,1,0:T(8,128)(2,1)}), bf16[32,144,128]{2,1,0:T(8,128)(2,1)S(1)}, u32[]{:S(2)}, u32[]{:S(2)}) %all-to-all-start) | async-done | bytes 1179680 | tf_op jit(solution)/shard_map/all_to_all | solution.py:62
  46.3 0.0 copy-done
  46.3 7.5 %fusion.4 = bf16[4096,128]{0,1:T(8,128)(2,1)S(1)} fusion(bf16[2048,128]{1,0:T(8,128)(2,1)S(1)} %copy-done, s32[4096]{0:T(1024)S(1)} %bitcast.35), kind=kOutput, calls=%fused_computation.7 | convolution fusion | flops 2156396544 | bytes 1589248 | tf_op jit(solution)/shard_map/dot_general | solution.py:70
  53.8 0.0 copy-start.1
  53.8 0.1 slice.68
  53.9 0.8 copy-done.1
  54.8 0.4 fusion.50
  55.2 0.3 copy.23
  55.5 0.0 slice-start
  55.5 0.0 copy-start.5
  55.5 0.3 copy.22
  55.9 0.0 copy-start.2
  55.9 0.7 slice-done
  56.5 0.0 copy-done.5
  56.5 0.4 fusion.14
  56.9 0.2 copy-done.2
  57.1 0.6 convolution_convert_fusion
  57.7 0.3 copy_bitcast_fusion
  58.0 1.1 %pad_maximum_fusion = bf16[32,128,128]{1,2,0:T(8,128)(2,1)} fusion(bf16[32,128,64]{1,2,0:T(8,128)(2,1)S(1)} %get-tuple-element.24, bf16[32,128,64]{1,2,0:T(8,128)(2,1)S(1)} %get-tuple-element.25), kind=kLoop, calls=%fused_computation.26 | loop fusion | flops 2097152 | bytes 2097152 | tf_op jit(solution)/shard_map/concatenate | solution.py:18
  59.0 3.8 %all-to-all-start.1 = ((bf16[32,128,128]{1,2,0:T(8,128)(2,1)}), bf16[32,128,128]{1,2,0:T(8,128)(2,1)S(1)}, u32[]{:S(2)}, u32[]{:S(2)}) async-start(bf16[32,128,128]{1,2,0:T(8,128)(2,1)} %pad_maximum_fusion), calls=%async_computation.1 | async-start | bytes 2097152 | tf_op jit(solution)/shard_map/all_to_all | solution.py:76
  62.9 6.5 %fusion.9 = bf16[2048,64]{0,1:T(8,128)(2,1)S(1)} fusion(s32[4096]{0:T(1024)S(1)} %bitcast.36, bf16[4096,128]{0,1:T(8,128)(2,1)S(1)} %convolution_convert_fusion), kind=kOutput, calls=%fused_computation.15 | convolution fusion | flops 1082261504 | bytes 802816 | tf_op jit(solution)/shard_map/dot_general | solution.py:79
  69.4 0.3 copy.17
  69.7 1.0 reshape.101
  70.7 18.2 %all-to-all-done.1 = bf16[32,128,128]{1,2,0:T(8,128)(2,1)S(1)} async-done(((bf16[32,128,128]{1,2,0:T(8,128)(2,1)}), bf16[32,128,128]{1,2,0:T(8,128)(2,1)S(1)}, u32[]{:S(2)}, u32[]{:S(2)}) %all-to-all-start.1) | async-done | bytes 1048608 | tf_op jit(solution)/shard_map/all_to_all | solution.py:76
  88.9 0.7 copy.20
  89.5 3.4 %all-to-all-start.2 = ((bf16[4,256,128]{2,1,0:T(8,128)(2,1)}), bf16[4,256,128]{2,1,0:T(8,128)(2,1)S(1)}, u32[]{:S(2)}, u32[]{:S(2)}) async-start(bf16[4,256,128]{2,1,0:T(8,128)(2,1)} %reshape.101), calls=%async_computation.2 | async-start | bytes 524288 | tf_op jit(solution)/shard_map/all_to_all | solution.py:85
  93.0 3.2 %gather_fusion = bf16[1024,128]{1,0:T(8,128)(2,1)S(1)} fusion(bf16[4096,128]{1,0:T(8,128)(2,1)S(1)} %bitcast.29, s32[1024]{0:T(1024)S(1)} %broadcast_clamp_fusion), kind=kCustom, calls=%fused_computation | custom fusion | bytes 528384 | tf_op jit(solution)/shard_map/jit(_take)/gather | solution.py:83
  96.2 0.0 copy-start.3
  96.2 0.0 copy-start.7
  96.2 0.9 broadcast_select_fusion
  97.1 1.8 %all-to-all-done.2 = bf16[4,256,128]{2,1,0:T(8,128)(2,1)S(1)} async-done(((bf16[4,256,128]{2,1,0:T(8,128)(2,1)}), bf16[4,256,128]{2,1,0:T(8,128)(2,1)S(1)}, u32[]{:S(2)}, u32[]{:S(2)}) %all-to-all-start.2) | async-done | bytes 262176 | tf_op jit(solution)/shard_map/all_to_all | solution.py:85
  98.9 0.2 convert_element_type.87
  99.2 0.0 copy-done.3
  99.2 1.1 %fusion.8 = bf16[2048,128]{1,0:T(8,128)(2,1)} fusion(bf16[2048,128]{1,0:T(8,128)(2,1)S(1)} %copy-done.3, bf16[128,128]{1,0:T(8,128)(2,1)S(1)} %copy-done.7, bf16[2048,64]{1,0:T(8,128)(2,1)S(1)} %convert_element_type.87), kind=kOutput, calls=%fused_computation.14 | convolution fusion | flops 68681728 | bytes 1343488 | tf_op jit(solution)/shard_map/dot_general | solution.py:92
  (12 shorter events, 0.1 us)
Async XLA Ops:
  0.6 45.6 %copy-start = (bf16[2048,128]{1,0:T(8,128)(2,1)S(1)}, bf16[2048,128]{1,0:T(8,128)(2,1)}, u32[]{:S(2)}) copy-start(bf16[2048,128]{1,0:T(8,128)(2,1)} %param.13) | copy-start | bytes 1572868
  0.6 1.4 %copy-start.8 = (s32[1024,1]{0,1:T(1,128)S(1)}, s32[1024,1]{0,1:T(1,128)}, u32[]{:S(2)}) copy-start(s32[1024,1]{0,1:T(1,128)} %param.11) | copy-start | bytes 12292
  0.7 1.4 %copy-start.9 = (s32[1024]{0:T(1024)S(1)}, s32[1024]{0:T(1024)}, u32[]{:S(2)}) copy-start(s32[1024]{0:T(1024)} %param.12) | copy-start | bytes 12292
  2.0 2.2 %copy-start.4 = (bf16[1024,128]{1,0:T(8,128)(2,1)S(1)}, bf16[1024,128]{1,0:T(8,128)(2,1)}, u32[]{:S(2)}) copy-start(bf16[1024,128]{1,0:T(8,128)(2,1)} %param.10) | copy-start | bytes 786436
  9.9 7.3 %copy-start.6 = (bf16[64,64]{1,0:T(8,128)(2,1)S(1)}, bf16[64,64]{1,0:T(8,128)(2,1)}, u32[]{:S(2)}) copy-start(bf16[64,64]{1,0:T(8,128)(2,1)} %param.15) | copy-start | bytes 24580
  9.9 36.3 %all-to-all-start = ((bf16[32,144,128]{2,1,0:T(8,128)(2,1)}), bf16[32,144,128]{2,1,0:T(8,128)(2,1)S(1)}, u32[]{:S(2)}, u32[]{:S(2)}) async-start(bf16[32,144,128]{2,1,0:T(8,128)(2,1)} %bitcast.6), calls=%async_computation | async-start | bytes 2359296 | tf_op jit(solution)/shard_map/all_to_all | solution.py:62
  53.8 1.0 copy-start.1
  55.5 1.0 %slice-start = ((bf16[4096,128]{0,1:T(8,128)(2,1)}), bf16[4096,64]{0,1:T(8,128)(2,1)S(1)}, s32[]{:S(2)}) async-start(bf16[4096,128]{0,1:T(8,128)(2,1)} %copy-done.1), calls=%async_computation.3 | async-start | bytes 1048576 | tf_op jit(solution)/shard_map/slice | solution.py:10
  55.5 1.0 %copy-start.5 = (bf16[64,64]{1,0:T(8,128)(2,1)S(1)}, bf16[64,64]{1,0:T(8,128)(2,1)}, u32[]{:S(2)}) copy-start(bf16[64,64]{1,0:T(8,128)(2,1)} %param.14) | copy-start | bytes 24580
  55.9 1.3 %copy-start.2 = (bf16[4096,128]{0,1:T(8,128)(2,1)S(1)}, bf16[4096,128]{0,1:T(8,128)(2,1)}, u32[]{:S(2)}) copy-start(bf16[4096,128]{0,1:T(8,128)(2,1)} %copy-done.1) | copy-start | bytes 3145732
  59.0 29.8 %all-to-all-start.1 = ((bf16[32,128,128]{1,2,0:T(8,128)(2,1)}), bf16[32,128,128]{1,2,0:T(8,128)(2,1)S(1)}, u32[]{:S(2)}, u32[]{:S(2)}) async-start(bf16[32,128,128]{1,2,0:T(8,128)(2,1)} %pad_maximum_fusion), calls=%async_computation.1 | async-start | bytes 2097152 | tf_op jit(solution)/shard_map/all_to_all | solution.py:76
  89.5 9.4 %all-to-all-start.2 = ((bf16[4,256,128]{2,1,0:T(8,128)(2,1)}), bf16[4,256,128]{2,1,0:T(8,128)(2,1)S(1)}, u32[]{:S(2)}, u32[]{:S(2)}) async-start(bf16[4,256,128]{2,1,0:T(8,128)(2,1)} %reshape.101), calls=%async_computation.2 | async-start | bytes 524288 | tf_op jit(solution)/shard_map/all_to_all | solution.py:85
  96.2 3.0 %copy-start.3 = (bf16[2048,128]{1,0:T(8,128)(2,1)S(1)}, bf16[2048,128]{1,0:T(8,128)(2,1)}, u32[]{:S(2)}) copy-start(bf16[2048,128]{1,0:T(8,128)(2,1)} %param.17) | copy-start | bytes 1572868
  96.2 3.0 %copy-start.7 = (bf16[128,128]{1,0:T(8,128)(2,1)S(1)}, bf16[128,128]{1,0:T(8,128)(2,1)}, u32[]{:S(2)}) copy-start(bf16[128,128]{1,0:T(8,128)(2,1)} %param.16) | copy-start | bytes 98308

commit v7 on v5

--- a/solution.py
+++ b/solution.py
@@ -1,6 +1,8 @@
 import jax
 import jax.numpy as jnp
 from jax import lax
+from jax.experimental import pallas as pl
+from jax.experimental.pallas import tpu as pltpu
 from jax.sharding import PartitionSpec as P
 
 relax = 0.5
@@ -18,6 +20,66 @@
     answer = jnp.concatenate([projected[:, :node_count], gap_jump], axis=1).astype(jnp.bfloat16)
     gained = projected[:, node_count:].astype(jnp.bfloat16)
     return (answer, gained)
+
+
+def owner_kernel(ids_ref, rows_ref, faces_ref, wc_ref, wm_ref, wj_ref, ans_ref, gain_ref):
+    blk = ids_ref.shape[0]
+    width = faces_ref.shape[1]
+    half = gain_ref.shape[1]
+    f32, bf16 = jnp.float32, jnp.bfloat16
+    ids = ids_ref[...]
+    face_iota = lax.broadcasted_iota(jnp.int32, (blk, faces_ref.shape[0]), 1)
+    sel = (ids == face_iota).astype(bf16)
+    mold = jnp.dot(sel, faces_ref[...], preferred_element_type=f32).astype(bf16)
+    rows = rows_ref[...].reshape(blk, width)
+    gap = jnp.dot(rows, wc_ref[...], preferred_element_type=f32) + jnp.dot(
+        mold, wm_ref[...], preferred_element_type=f32
+    )
+    flux = (rows.astype(f32) * mold.astype(f32) * gap).astype(bf16)
+    projected = jnp.dot(flux, wj_ref[...], preferred_element_type=f32)
+    lane = lax.broadcasted_iota(jnp.int32, (blk, width), 1)
+    ans_ref[...] = jnp.where(lane < half, projected, gap).astype(bf16)
+    gain_ref[...] = projected[:, half:].astype(bf16)
+
+
+def owner_contact(got, got_ids, mold_faces, mortar_d, mortar_m, capacity):
+    devices, _, width = got.shape
+    half = mortar_d.shape[0]
+    slots = devices * capacity
+    face_rows = mold_faces.shape[0]
+    blk = 256
+    per = blk // capacity
+    zero = jnp.zeros((half, half), mortar_d.dtype)
+    wc = jnp.block([[zero, mortar_d.T], [zero, zero]])
+    wm = jnp.block([[zero, -mortar_m.T], [zero, zero]])
+    wj = jnp.block([[zero, zero], [mortar_d, mortar_m]])
+    full = lambda i: (0, 0)
+    cost = pl.CostEstimate(
+        flops=2 * slots * width * (face_rows + 3 * width),
+        bytes_accessed=slots * width * 2 * 3 + face_rows * width * 2,
+        transcendentals=0,
+    )
+    return pl.pallas_call(
+        owner_kernel,
+        grid=(slots // blk,),
+        in_specs=[
+            pl.BlockSpec((blk, 1), lambda i: (i, 0)),
+            pl.BlockSpec((per, capacity, width), lambda i: (i, 0, 0)),
+            pl.BlockSpec((face_rows, width), full),
+            pl.BlockSpec((width, width), full),
+            pl.BlockSpec((width, width), full),
+            pl.BlockSpec((width, width), full),
+        ],
+        out_specs=[
+            pl.BlockSpec((blk, width), lambda i: (i, 0)),
+            pl.BlockSpec((blk, half), lambda i: (i, 0)),
+        ],
+        out_shape=[
+            jax.ShapeDtypeStruct((slots, width), jnp.bfloat16),
+            jax.ShapeDtypeStruct((slots, half), jnp.bfloat16),
+        ],
+        cost_estimate=cost,
+    )(got_ids.reshape(slots, 1), got, mold_faces, wc, wm, wj)
 
 
 def local(casting, owner, face_id, mold_faces, mortar_d, mortar_m, conduct, volume):
@@ -59,18 +121,13 @@
     send = send.reshape(devices * block, row_width).at[target * block + position].set(casting)
     send = send.reshape(devices, block, row_width)
     got = lax.all_to_all(send, axes, 0, 0, tiled=True)
-    got_rows = got[:, :capacity, :].reshape(slots, row_width)
     got_code = got[:, capacity:, :].astype(f32).reshape(devices, id_height * row_width)
     got_code = got_code[:, :id_count].reshape(devices, 2, capacity)
     got_ids = (got_code[:, 0, :] * 64.0 + got_code[:, 1, :]).astype(jnp.int32).reshape(slots) - 1
 
+    answers, gained = owner_contact(got, got_ids, mold_faces, mortar_d, mortar_m, capacity)
     face_range = jnp.arange(face_rows, dtype=jnp.int32)
     selector = (got_ids[:, None] == face_range[None, :]).astype(bf16)
-    mold_rows = jnp.dot(selector, mold_faces, preferred_element_type=f32).astype(bf16)
-
-    stacked = jnp.concatenate([mortar_d.T, -mortar_m.T], axis=0)
-    joined = jnp.concatenate([mortar_d, mortar_m], axis=1)
-    answers, gained = contact(got_rows, mold_rows, stacked, joined, node_count)
 
     returned = lax.all_to_all(
         answers.reshape(devices, capacity, row_width), axes, 0, 0, tiled=True

time: 98.6 us -> 104 us (1.055)
  Pallas kernels: 0 us -> 16.2 us
  matrix products: 18.3 us -> 10.2 us
  local copies, waits for them, and re-layouts: 14.3 us -> 12.9 us
  waiting for transfers between devices: 47.6 us -> 46.3 us
    pallas_call x0 -> x1, Pallas kernels: none -> 16.2 us  [owner_contact(): pl.pallas_call(owner_kernel, grid=(slots // blk,), in_specs=[pl.BlockSpec...]
    dot_general x3 -> x0, matrix products: 8.4 us -> none  [the longest x1 7.5 us: local(): jnp.dot(selector, mold_faces, preferred_element_type=f32).astype(bf16)]
    sub x0 -> x1, local copies, waits for them, and re-layouts: none -> 1.98 us  [local(): (got_code[:, 0, :] * 64.0 + got_code[:, 1, :]).astype(jnp.int32)]
    unnamed x23 -> x21, local copies, waits for them, and re-layouts: 2.39 us -> 0.85 us
    slice x4 -> x0, local copies, waits for them, and re-layouts: 1.18 us -> none  [the longest x2 0.68 us: contact(): mold_rows[:, :node_count]]
  transfers between devices with their start and end apart: 3 -> 3, of which waited for: 3 -> 3; matrix products, arithmetic and copies ran while one was open for 12% -> 13% of each run, Pallas kernels for 0% -> 0%
where the time goes in v7:
time: 104 us; the launch traced here: 103 us
  waiting for transfers between devices  46.3 us (45%)
  Pallas kernels  16.2 us (16%)
  starting transfers between devices  14.5 us (14%)
  local copies, waits for them, and re-layouts  12.9 us (12%)
  matrix products  10.2 us (10%)
  other arithmetic  1.78 us (2%)
    all_to_all x1, waiting for transfers between devices, local(): got = lax.all_to_all(send, axes, 0, 0, tiled=True)  26.6 us
    all_to_all x1, waiting for transfers between devices, local(): lax.all_to_all(answers.reshape(devices, capacity, row_width), axes, 0, 0,...  17.8 us
    pallas_call x1, Pallas kernels, owner_contact(): pl.pallas_call(owner_kernel, grid=(slots // blk,), in_specs=[pl.BlockSpec...  16.2 us
    all_to_all x1, starting transfers between devices, local(): got = lax.all_to_all(send, axes, 0, 0, tiled=True)  7.32 us
    dot_general x1, matrix products, local(): lax.dot_general(selector, gained, contract0, preferred_element_type=f32)  6.83 us
    all_to_all x1, starting transfers between devices, local(): lax.all_to_all(answers.reshape(devices, capacity, row_width), axes, 0, 0,...  3.8 us
    scatter x1, local copies, waits for them, and re-layouts, local(): send.reshape(devices * block, row_width).at[target * block + position]  3.73 us
    all_to_all x1, starting transfers between devices, local(): lax.all_to_all(face_totals, 'vol', split_axis=0, concat_axis=0, tiled=True)  3.41 us
  transfers between devices with their start and end apart: 3, of which 3 were waited for; matrix products, arithmetic and copies ran while one was open for 13% of the time, Pallas kernels for 0%

profile of v7, /device:TPU:0, one launch (start us, length us, event | category | flops | bytes accessed | tf_op | source)
XLA Modules:
  0.0 102.8 jit_solution(15557693229520907679)
XLA Ops:
  0.6 0.0 copy-start
  0.6 0.0 copy-start.6
  0.7 0.0 copy-start.7
  0.7 1.3 %fusion.8 = f32[1024]{0:T(1024)S(1)} fusion(s32[1024]{0:T(1024)} %bitcast.27), kind=kOutput, calls=%fused_computation.13 | convolution fusion | flops 68353024 | bytes 8192 | tf_op jit(solution)/shard_map/dot_general | solution.py:103
  2.0 0.0 copy-done.6
  2.0 0.0 copy-done.7
  2.1 0.5 fusion.9
  2.5 0.5 fusion.10
  3.0 0.1 scatter.12.clone
  3.2 0.0 copy-start.3
  3.2 0.3 reshape.116
  3.5 0.6 copy-done.3
  4.1 3.7 %scatter_fusion = bf16[4160,128]{1,0:T(8,128)(2,1)S(1)} fusion(bf16[4160,128]{1,0:T(8,128)(2,1)S(1)} %reshape.116, s32[1024]{0:T(1024)S(1)} %bitcast.25, bf16[1024,128]{1,0:T(8,128)(2,1)S(1)} %copy-done.3), kind=kCustom, calls=%fused_computation.1 | custom fusion | bytes 790528 | tf_op jit(solution)/shard_map/scatter | solution.py:121
  7.9 1.2 %reshape.117 = bf16[32,130,128]{2,1,0:T(8,128)(2,1)} reshape(bf16[4160,128]{1,0:T(8,128)(2,1)S(1)} %scatter_fusion) | data formatting | bytes 2129920 | tf_op jit(solution)/shard_map/reshape | solution.py:122
  9.0 0.0 copy-start.5
  9.0 0.0 copy-start.4
  9.0 7.3 %all-to-all-start = ((bf16[32,130,128]{2,1,0:T(8,128)(2,1)}), bf16[32,130,128]{2,1,0:T(8,128)(2,1)S(1)}, u32[]{:S(2)}, u32[]{:S(2)}) async-start(bf16[32,130,128]{2,1,0:T(8,128)(2,1)} %reshape.117), calls=%async_computation | async-start | bytes 2228224 | tf_op jit(solution)/shard_map/all_to_all | solution.py:123
  16.4 0.0 copy-done.5
  16.4 0.1 copy.14
  16.5 0.0 copy-done.4
  16.5 0.1 copy.15
  16.6 0.7 maximum_maximum_fusion
  17.3 26.6 %all-to-all-done.rows_ref = bf16[32,130,128]{2,1,0:T(8,128)(2,1)S(1)} async-done(((bf16[32,130,128]{2,1,0:T(8,128)(2,1)}), bf16[32,130,128]{2,1,0:T(8,128)(2,1)S(1)}, u32[]{:S(2)}, u32[]{:S(2)}) %all-to-all-start) | async-done | bytes 1064992 | tf_op jit(solution)/shard_map/all_to_all | solution.py:123
  44.0 0.0 copy-start.1
  44.0 2.0 %copy.16.ids_ref = s32[4096,1]{1,0:T(8,128)} copy(s32[4096,1]{0,1:T(1,128)S(1)} %fusion.38) | data formatting | bytes 32768 | tf_op jit(solution)/shard_map/sub | solution.py:126
  46.0 0.0 copy-done.1
  46.0 16.2 %shard_map.95 = (bf16[4096,128]{1,0:T(8,128)(2,1)}, bf16[4096,64]{1,0:T(8,128)(2,1)}) custom-call(s32[4096,1]{1,0:T(8,128)} %copy.16.ids_ref, bf16[32,130,128]{2,1,0:T(8,128)(2,1)} %copy-done.1, bf16[2048,128]{1,0:T(8,128)(2,1)} %faces_ref.1, bf16[128,128]{1,0:T(8,128)(2,1)} %get-tuple-element.26.wc_ref, bf16[128,128]{1,0:T(8,128)(2,1)} %get-tuple-element.25.wm_ref, ...), custom_call_target="tpu_custom_call" | custom-call | flops 2550136832 | bytes 3670016 | tf_op jit(solution)/shard_map/pallas_call | solution.py:62
  62.2 0.0 copy-start.8
  62.2 3.8 %all-to-all-start.1 = ((bf16[32,128,128]{2,1,0:T(8,128)(2,1)}), bf16[32,128,128]{2,1,0:T(8,128)(2,1)S(1)}, u32[]{:S(2)}, u32[]{:S(2)}) async-start(bf16[32,128,128]{2,1,0:T(8,128)(2,1)} %bitcast.21), calls=%async_computation.1 | async-start | bytes 2097152 | tf_op jit(solution)/shard_map/all_to_all | solution.py:132
  66.1 0.0 copy-done.8
  66.1 6.8 %fusion.6 = bf16[2048,64]{0,1:T(8,128)(2,1)S(1)} fusion(bf16[4096,64]{1,0:T(8,128)(2,1)S(1)} %copy-done.8, s32[4096]{0:T(1024)S(1)} %bitcast.26), kind=kOutput, calls=%fused_computation.11 | convolution fusion | flops 1082261504 | bytes 802816 | tf_op jit(solution)/shard_map/dot_general | solution.py:135
  73.0 0.3 copy.17
  73.2 1.0 reshape.118
  74.2 17.8 %all-to-all-done.1 = bf16[32,128,128]{2,1,0:T(8,128)(2,1)S(1)} async-done(((bf16[32,128,128]{2,1,0:T(8,128)(2,1)}), bf16[32,128,128]{2,1,0:T(8,128)(2,1)S(1)}, u32[]{:S(2)}, u32[]{:S(2)}) %all-to-all-start.1) | async-done | bytes 1048608 | tf_op jit(solution)/shard_map/all_to_all | solution.py:132
  92.1 3.4 %all-to-all-start.2 = ((bf16[4,256,128]{2,1,0:T(8,128)(2,1)}), bf16[4,256,128]{2,1,0:T(8,128)(2,1)S(1)}, u32[]{:S(2)}, u32[]{:S(2)}) async-start(bf16[4,256,128]{2,1,0:T(8,128)(2,1)} %reshape.118), calls=%async_computation.2 | async-start | bytes 524288 | tf_op jit(solution)/shard_map/all_to_all | solution.py:141
  95.5 3.2 %gather_fusion = bf16[1024,128]{1,0:T(8,128)(2,1)S(1)} fusion(bf16[4096,128]{1,0:T(8,128)(2,1)S(1)} %bitcast.20, s32[1024]{0:T(1024)S(1)} %broadcast_clamp_fusion), kind=kCustom, calls=%fused_computation | custom fusion | bytes 528384 | tf_op jit(solution)/shard_map/jit(_take)/gather | solution.py:139
  98.7 0.0 copy-start.2
  98.7 0.9 broadcast_select_fusion
  99.6 1.8 %all-to-all-done.2 = bf16[4,256,128]{2,1,0:T(8,128)(2,1)S(1)} async-done(((bf16[4,256,128]{2,1,0:T(8,128)(2,1)}), bf16[4,256,128]{2,1,0:T(8,128)(2,1)S(1)}, u32[]{:S(2)}, u32[]{:S(2)}) %all-to-all-start.2) | async-done | bytes 262176 | tf_op jit(solution)/shard_map/all_to_all | solution.py:141
  101.4 0.2 convert_element_type.73
  101.7 0.0 copy-done
  101.7 0.0 copy-done.2
  101.7 1.1 %fusion.5 = bf16[2048,128]{1,0:T(8,128)(2,1)} fusion(bf16[2048,128]{1,0:T(8,128)(2,1)S(1)} %copy-done.2, bf16[128,128]{1,0:T(8,128)(2,1)S(1)} %copy-done, bf16[2048,64]{1,0:T(8,128)(2,1)S(1)} %convert_element_type.73), kind=kOutput, calls=%fused_computation.10 | convolution fusion | flops 68681728 | bytes 1343488 | tf_op jit(solution)/shard_map/dot_general | solution.py:148
  (14 shorter events, 0.2 us)
Async XLA Ops:
  0.6 101.1 %copy-start = (bf16[128,128]{1,0:T(8,128)(2,1)S(1)}, bf16[128,128]{1,0:T(8,128)(2,1)}, u32[]{:S(2)}) copy-start(bf16[128,128]{1,0:T(8,128)(2,1)} %param.16) | copy-start | bytes 98308
  0.6 1.4 %copy-start.6 = (s32[1024,1]{0,1:T(1,128)S(1)}, s32[1024,1]{0,1:T(1,128)}, u32[]{:S(2)}) copy-start(s32[1024,1]{0,1:T(1,128)} %param.11) | copy-start | bytes 12292
  0.7 1.4 %copy-start.7 = (s32[1024]{0:T(1024)S(1)}, s32[1024]{0:T(1024)}, u32[]{:S(2)}) copy-start(s32[1024]{0:T(1024)} %param.12) | copy-start | bytes 12292
  3.2 1.0 copy-start.3
  9.0 7.4 %copy-start.5 = (bf16[64,64]{1,0:T(8,128)(2,1)S(1)}, bf16[64,64]{1,0:T(8,128)(2,1)}, u32[]{:S(2)}) copy-start(bf16[64,64]{1,0:T(8,128)(2,1)} %param.14) | copy-start | bytes 24580
  9.0 7.5 %copy-start.4 = (bf16[64,64]{1,0:T(8,128)(2,1)S(1)}, bf16[64,64]{1,0:T(8,128)(2,1)}, u32[]{:S(2)}) copy-start(bf16[64,64]{1,0:T(8,128)(2,1)} %param.15) | copy-start | bytes 24580
  9.0 34.9 %all-to-all-start = ((bf16[32,130,128]{2,1,0:T(8,128)(2,1)}), bf16[32,130,128]{2,1,0:T(8,128)(2,1)S(1)}, u32[]{:S(2)}, u32[]{:S(2)}) async-start(bf16[32,130,128]{2,1,0:T(8,128)(2,1)} %reshape.117), calls=%async_computation | async-start | bytes 2228224 | tf_op jit(solution)/shard_map/all_to_all | solution.py:123
  44.0 2.0 %copy-start.1 = (bf16[32,130,128]{2,1,0:T(8,128)(2,1)}, bf16[32,130,128]{2,1,0:T(8,128)(2,1)S(1)}, u32[]{:S(2)}) copy-start(bf16[32,130,128]{2,1,0:T(8,128)(2,1)S(1)} %all-to-all-done.rows_ref) | copy-start | bytes 3194884
  62.2 3.9 %copy-start.8 = (bf16[4096,64]{1,0:T(8,128)(2,1)S(1)}, bf16[4096,64]{1,0:T(8,128)(2,1)}, u32[]{:S(2)}) copy-start(bf16[4096,64]{1,0:T(8,128)(2,1)} %get-tuple-element.18) | copy-start | bytes 1572868
  62.2 29.8 %all-to-all-start.1 = ((bf16[32,128,128]{2,1,0:T(8,128)(2,1)}), bf16[32,128,128]{2,1,0:T(8,128)(2,1)S(1)}, u32[]{:S(2)}, u32[]{:S(2)}) async-start(bf16[32,128,128]{2,1,0:T(8,128)(2,1)} %bitcast.21), calls=%async_computation.1 | async-start | bytes 2097152 | tf_op jit(solution)/shard_map/all_to_all | solution.py:132
  92.1 9.4 %all-to-all-start.2 = ((bf16[4,256,128]{2,1,0:T(8,128)(2,1)}), bf16[4,256,128]{2,1,0:T(8,128)(2,1)S(1)}, u32[]{:S(2)}, u32[]{:S(2)}) async-start(bf16[4,256,128]{2,1,0:T(8,128)(2,1)} %reshape.118), calls=%async_computation.2 | async-start | bytes 524288 | tf_op jit(solution)/shard_map/all_to_all | solution.py:141
  98.7 3.0 %copy-start.2 = (bf16[2048,128]{1,0:T(8,128)(2,1)S(1)}, bf16[2048,128]{1,0:T(8,128)(2,1)}, u32[]{:S(2)}) copy-start(bf16[2048,128]{1,0:T(8,128)(2,1)} %param.17) | copy-start | bytes 1572868

commit v8 on v7

--- a/solution.py
+++ b/solution.py
@@ -23,14 +23,16 @@
 
 
 def owner_kernel(ids_ref, rows_ref, faces_ref, wc_ref, wm_ref, wj_ref, ans_ref, gain_ref):
-    blk = ids_ref.shape[0]
+    blk = ids_ref.shape[1]
     width = faces_ref.shape[1]
     half = gain_ref.shape[1]
     f32, bf16 = jnp.float32, jnp.bfloat16
     ids = ids_ref[...]
-    face_iota = lax.broadcasted_iota(jnp.int32, (blk, faces_ref.shape[0]), 1)
-    sel = (ids == face_iota).astype(bf16)
-    mold = jnp.dot(sel, faces_ref[...], preferred_element_type=f32).astype(bf16)
+    face_iota = lax.broadcasted_iota(jnp.int32, (faces_ref.shape[0], blk), 0)
+    sel_t = (face_iota == ids).astype(bf16)
+    mold = lax.dot_general(
+        sel_t, faces_ref[...], (((0,), (0,)), ((), ())), preferred_element_type=f32
+    ).astype(bf16)
     rows = rows_ref[...].reshape(blk, width)
     gap = jnp.dot(rows, wc_ref[...], preferred_element_type=f32) + jnp.dot(
         mold, wm_ref[...], preferred_element_type=f32
@@ -63,7 +65,7 @@
         owner_kernel,
         grid=(slots // blk,),
         in_specs=[
-            pl.BlockSpec((blk, 1), lambda i: (i, 0)),
+            pl.BlockSpec((1, blk), lambda i: (0, i)),
             pl.BlockSpec((per, capacity, width), lambda i: (i, 0, 0)),
             pl.BlockSpec((face_rows, width), full),
             pl.BlockSpec((width, width), full),
@@ -79,7 +81,7 @@
             jax.ShapeDtypeStruct((slots, half), jnp.bfloat16),
         ],
         cost_estimate=cost,
-    )(got_ids.reshape(slots, 1), got, mold_faces, wc, wm, wj)
+    )(got_ids.reshape(1, slots), got, mold_faces, wc, wm, wj)
 
 
 def local(casting, owner, face_id, mold_faces, mortar_d, mortar_m, conduct, volume):

time: 104 us -> 102 us (0.981)
  local copies, waits for them, and re-layouts: 12.9 us -> 11.2 us
    sub x1 -> x0, local copies, waits for them, and re-layouts: 1.98 us -> none  [local(): (got_code[:, 0, :] * 64.0 + got_code[:, 1, :]).astype(jnp.int32)]
where the time goes in v8:
time: 102 us; the launch traced here: 101 us
  waiting for transfers between devices  46.5 us (46%)
  Pallas kernels  15.6 us (15%)
  starting transfers between devices  14.4 us (14%)
  local copies, waits for them, and re-layouts  11.2 us (11%)
  matrix products  10.2 us (10%)
  other arithmetic  2.47 us (2%)
    all_to_all x1, waiting for transfers between devices, local(): got = lax.all_to_all(send, axes, 0, 0, tiled=True)  26.6 us
    all_to_all x1, waiting for transfers between devices, local(): lax.all_to_all(answers.reshape(devices, capacity, row_width), axes, 0, 0,...  18 us
    pallas_call x1, Pallas kernels, owner_contact(): pl.pallas_call(owner_kernel, grid=(slots // blk,), in_specs=[pl.BlockSpec...  15.6 us
    all_to_all x1, starting transfers between devices, local(): got = lax.all_to_all(send, axes, 0, 0, tiled=True)  7.33 us
    dot_general x1, matrix products, local(): lax.dot_general(selector, gained, contract0, preferred_element_type=f32)  6.83 us
    scatter x1, local copies, waits for them, and re-layouts, local(): send.reshape(devices * block, row_width).at[target * block + position]  3.73 us
    all_to_all x1, starting transfers between devices, local(): lax.all_to_all(answers.reshape(devices, capacity, row_width), axes, 0, 0,...  3.63 us
    all_to_all x1, starting transfers between devices, local(): lax.all_to_all(face_totals, 'vol', split_axis=0, concat_axis=0, tiled=True)  3.41 us
  transfers between devices with their start and end apart: 3, of which 3 were waited for; matrix products, arithmetic and copies ran while one was open for 13% of the time, Pallas kernels for 0%

profile of v8, /device:TPU:0, one launch (start us, length us, event | category | flops | bytes accessed | tf_op | source)
XLA Modules:
  0.0 101.2 jit_solution(964269375168588917)
XLA Ops:
  0.6 0.0 copy-start
  0.6 0.0 copy-start.6
  0.7 0.0 copy-start.7
  0.7 1.3 %fusion.8 = f32[1024]{0:T(1024)S(1)} fusion(s32[1024]{0:T(1024)} %bitcast.27), kind=kOutput, calls=%fused_computation.13 | convolution fusion | flops 68353024 | bytes 8192 | tf_op jit(solution)/shard_map/dot_general | solution.py:105
  2.0 0.0 copy-done.6
  2.0 0.0 copy-done.7
  2.0 0.5 fusion.9
  2.5 0.5 fusion.10
  3.0 0.1 scatter.12.clone
  3.2 0.0 copy-start.3
  3.2 0.3 reshape.126
  3.5 0.6 copy-done.3
  4.1 3.7 %scatter_fusion = bf16[4160,128]{1,0:T(8,128)(2,1)S(1)} fusion(bf16[4160,128]{1,0:T(8,128)(2,1)S(1)} %reshape.126, s32[1024]{0:T(1024)S(1)} %bitcast.25, bf16[1024,128]{1,0:T(8,128)(2,1)S(1)} %copy-done.3), kind=kCustom, calls=%fused_computation.1 | custom fusion | bytes 790528 | tf_op jit(solution)/shard_map/scatter | solution.py:123
  7.9 1.2 %reshape.127 = bf16[32,130,128]{2,1,0:T(8,128)(2,1)} reshape(bf16[4160,128]{1,0:T(8,128)(2,1)S(1)} %scatter_fusion) | data formatting | bytes 2129920 | tf_op jit(solution)/shard_map/reshape | solution.py:124
  9.0 0.0 copy-start.5
  9.0 0.0 copy-start.4
  9.0 7.3 %all-to-all-start = ((bf16[32,130,128]{2,1,0:T(8,128)(2,1)}), bf16[32,130,128]{2,1,0:T(8,128)(2,1)S(1)}, u32[]{:S(2)}, u32[]{:S(2)}) async-start(bf16[32,130,128]{2,1,0:T(8,128)(2,1)} %reshape.127), calls=%async_computation | async-start | bytes 2228224 | tf_op jit(solution)/shard_map/all_to_all | solution.py:125
  16.4 0.0 copy-done.5
  16.4 0.1 copy.13
  16.5 0.0 copy-done.4
  16.5 0.1 copy.14
  16.6 0.7 maximum_maximum_fusion
  17.3 26.6 %all-to-all-done.rows_ref = bf16[32,130,128]{2,1,0:T(8,128)(2,1)S(1)} async-done(((bf16[32,130,128]{2,1,0:T(8,128)(2,1)}), bf16[32,130,128]{2,1,0:T(8,128)(2,1)S(1)}, u32[]{:S(2)}, u32[]{:S(2)}) %all-to-all-start) | async-done | bytes 1064992 | tf_op jit(solution)/shard_map/all_to_all | solution.py:125
  44.0 0.0 copy-start.1
  44.0 0.7 fusion.38.ids_ref
  44.7 0.3 copy-done.1
  45.0 15.6 %shard_map.95 = (bf16[4096,128]{1,0:T(8,128)(2,1)}, bf16[4096,64]{1,0:T(8,128)(2,1)}) custom-call(s32[1,4096]{1,0:T(1,128)} %fusion.38.ids_ref, bf16[32,130,128]{2,1,0:T(8,128)(2,1)} %copy-done.1, bf16[2048,128]{1,0:T(8,128)(2,1)} %faces_ref.1, bf16[128,128]{1,0:T(8,128)(2,1)} %get-tuple-element.26.wc_ref, bf16[128,128]{1,0:T(8,128)(2,1)} %get-tuple-element.25.wm_ref, ...), custom_call_target="tpu_custom_call" | custom-call | flops 2550136832 | bytes 3670016 | tf_op jit(solution)/shard_map/pallas_call | solution.py:64
  60.5 0.0 copy-start.8
  60.5 3.6 %all-to-all-start.1 = ((bf16[32,128,128]{2,1,0:T(8,128)(2,1)}), bf16[32,128,128]{2,1,0:T(8,128)(2,1)S(1)}, u32[]{:S(2)}, u32[]{:S(2)}) async-start(bf16[32,128,128]{2,1,0:T(8,128)(2,1)} %bitcast.21), calls=%async_computation.1 | async-start | bytes 2097152 | tf_op jit(solution)/shard_map/all_to_all | solution.py:134
  64.3 0.0 copy-done.8
  64.3 6.8 %fusion.6 = bf16[2048,64]{0,1:T(8,128)(2,1)S(1)} fusion(bf16[4096,64]{1,0:T(8,128)(2,1)S(1)} %copy-done.8, s32[4096]{0:T(1024)S(1)} %bitcast.26), kind=kOutput, calls=%fused_computation.11 | convolution fusion | flops 1082261504 | bytes 802816 | tf_op jit(solution)/shard_map/dot_general | solution.py:137
  71.1 0.3 copy.15
  71.4 1.0 reshape.128
  72.4 18.0 %all-to-all-done.1 = bf16[32,128,128]{2,1,0:T(8,128)(2,1)S(1)} async-done(((bf16[32,128,128]{2,1,0:T(8,128)(2,1)}), bf16[32,128,128]{2,1,0:T(8,128)(2,1)S(1)}, u32[]{:S(2)}, u32[]{:S(2)}) %all-to-all-start.1) | async-done | bytes 1048608 | tf_op jit(solution)/shard_map/all_to_all | solution.py:134
  90.4 3.4 %all-to-all-start.2 = ((bf16[4,256,128]{2,1,0:T(8,128)(2,1)}), bf16[4,256,128]{2,1,0:T(8,128)(2,1)S(1)}, u32[]{:S(2)}, u32[]{:S(2)}) async-start(bf16[4,256,128]{2,1,0:T(8,128)(2,1)} %reshape.128), calls=%async_computation.2 | async-start | bytes 524288 | tf_op jit(solution)/shard_map/all_to_all | solution.py:143
  93.8 3.2 %gather_fusion = bf16[1024,128]{1,0:T(8,128)(2,1)S(1)} fusion(bf16[4096,128]{1,0:T(8,128)(2,1)S(1)} %bitcast.20, s32[1024]{0:T(1024)S(1)} %broadcast_clamp_fusion), kind=kCustom, calls=%fused_computation | custom fusion | bytes 528384 | tf_op jit(solution)/shard_map/jit(_take)/gather | solution.py:141
  97.0 0.0 copy-start.2
  97.0 0.9 broadcast_select_fusion
  97.9 1.8 %all-to-all-done.2 = bf16[4,256,128]{2,1,0:T(8,128)(2,1)S(1)} async-done(((bf16[4,256,128]{2,1,0:T(8,128)(2,1)}), bf16[4,256,128]{2,1,0:T(8,128)(2,1)S(1)}, u32[]{:S(2)}, u32[]{:S(2)}) %all-to-all-start.2) | async-done | bytes 262176 | tf_op jit(solution)/shard_map/all_to_all | solution.py:143
  99.8 0.2 convert_element_type.76
  100.0 0.0 copy-done
  100.0 0.0 copy-done.2
  100.0 1.1 %fusion.5 = bf16[2048,128]{1,0:T(8,128)(2,1)} fusion(bf16[2048,128]{1,0:T(8,128)(2,1)S(1)} %copy-done.2, bf16[128,128]{1,0:T(8,128)(2,1)S(1)} %copy-done, bf16[2048,64]{1,0:T(8,128)(2,1)S(1)} %convert_element_type.76), kind=kOutput, calls=%fused_computation.10 | convolution fusion | flops 68681728 | bytes 1343488 | tf_op jit(solution)/shard_map/dot_general | solution.py:150
  (13 shorter events, 0.2 us)
Async XLA Ops:
  0.6 99.4 %copy-start = (bf16[128,128]{1,0:T(8,128)(2,1)S(1)}, bf16[128,128]{1,0:T(8,128)(2,1)}, u32[]{:S(2)}) copy-start(bf16[128,128]{1,0:T(8,128)(2,1)} %param.16) | copy-start | bytes 98308
  0.6 1.3 %copy-start.6 = (s32[1024,1]{0,1:T(1,128)S(1)}, s32[1024,1]{0,1:T(1,128)}, u32[]{:S(2)}) copy-start(s32[1024,1]{0,1:T(1,128)} %param.11) | copy-start | bytes 12292
  0.7 1.4 %copy-start.7 = (s32[1024]{0:T(1024)S(1)}, s32[1024]{0:T(1024)}, u32[]{:S(2)}) copy-start(s32[1024]{0:T(1024)} %param.12) | copy-start | bytes 12292
  3.2 1.0 copy-start.3
  9.0 7.4 %copy-start.5 = (bf16[64,64]{1,0:T(8,128)(2,1)S(1)}, bf16[64,64]{1,0:T(8,128)(2,1)}, u32[]{:S(2)}) copy-start(bf16[64,64]{1,0:T(8,128)(2,1)} %param.14) | copy-start | bytes 24580
  9.0 7.5 %copy-start.4 = (bf16[64,64]{1,0:T(8,128)(2,1)S(1)}, bf16[64,64]{1,0:T(8,128)(2,1)}, u32[]{:S(2)}) copy-start(bf16[64,64]{1,0:T(8,128)(2,1)} %param.15) | copy-start | bytes 24580
  9.0 34.9 %all-to-all-start = ((bf16[32,130,128]{2,1,0:T(8,128)(2,1)}), bf16[32,130,128]{2,1,0:T(8,128)(2,1)S(1)}, u32[]{:S(2)}, u32[]{:S(2)}) async-start(bf16[32,130,128]{2,1,0:T(8,128)(2,1)} %reshape.127), calls=%async_computation | async-start | bytes 2228224 | tf_op jit(solution)/shard_map/all_to_all | solution.py:125
  44.0 1.0 copy-start.1
  60.5 3.7 %copy-start.8 = (bf16[4096,64]{1,0:T(8,128)(2,1)S(1)}, bf16[4096,64]{1,0:T(8,128)(2,1)}, u32[]{:S(2)}) copy-start(bf16[4096,64]{1,0:T(8,128)(2,1)} %get-tuple-element.18) | copy-start | bytes 1572868
  60.5 29.8 %all-to-all-start.1 = ((bf16[32,128,128]{2,1,0:T(8,128)(2,1)}), bf16[32,128,128]{2,1,0:T(8,128)(2,1)S(1)}, u32[]{:S(2)}, u32[]{:S(2)}) async-start(bf16[32,128,128]{2,1,0:T(8,128)(2,1)} %bitcast.21), calls=%async_computation.1 | async-start | bytes 2097152 | tf_op jit(solution)/shard_map/all_to_all | solution.py:134
  90.4 9.4 %all-to-all-start.2 = ((bf16[4,256,128]{2,1,0:T(8,128)(2,1)}), bf16[4,256,128]{2,1,0:T(8,128)(2,1)S(1)}, u32[]{:S(2)}, u32[]{:S(2)}) async-start(bf16[4,256,128]{2,1,0:T(8,128)(2,1)} %reshape.128), calls=%async_computation.2 | async-start | bytes 524288 | tf_op jit(solution)/shard_map/all_to_all | solution.py:143
  97.0 3.0 %copy-start.2 = (bf16[2048,128]{1,0:T(8,128)(2,1)S(1)}, bf16[2048,128]{1,0:T(8,128)(2,1)}, u32[]{:S(2)}) copy-start(bf16[2048,128]{1,0:T(8,128)(2,1)} %param.17) | copy-start | bytes 1572868

commit v9 on v5

--- a/solution.py
+++ b/solution.py
@@ -78,16 +78,10 @@
     totals = lax.dot_general(selector, gained, contract0, preferred_element_type=f32)
     quarter = face_rows // vol_count
     face_totals = totals.astype(bf16).reshape(vol_count, quarter * node_count // row_width, row_width)
-    face_totals, returned = lax.optimization_barrier((face_totals, returned))
     casting_out = jnp.take(returned, slot_index, axis=0)
 
-    relaid = lax.all_to_all(
-        face_totals,
-        "vol",
-        split_axis=0,
-        concat_axis=0,
-        tiled=True,
-    )
+    gathered = lax.all_gather(face_totals, "vol", axis=0)
+    relaid = lax.dynamic_index_in_dim(gathered, lax.axis_index("vol"), axis=1, keepdims=False)
     heat = jnp.dot(volume, conduct, preferred_element_type=f32)
     placed = relaid.reshape(face_rows, node_count).astype(f32)
     inject = jnp.concatenate([placed, jnp.zeros((face_rows, node_count), f32)], axis=1)

time: 98.6 us -> 110 us (1.12)
  between operations: 0.98 us -> 14.4 us
  starting transfers between devices: 14.5 us -> 11.2 us
  local copies, waits for them, and re-layouts: 14.3 us -> 16.2 us
    all_gather x0 -> x1, waiting for transfers between devices: none -> 19.4 us  [local(): gathered = lax.all_gather(face_totals, 'vol', axis=0)]
    all_to_all x1, waiting for transfers between devices: 18.2 us -> 0.01 us  [local(): lax.all_to_all(answers.reshape(devices, capacity, row_width), axes, 0, 0,...]
    all_to_all x1 -> x0, starting transfers between devices: 3.42 us -> none  [local(): lax.all_to_all(face_totals, 'vol', split_axis=0, concat_axis=0, tiled=True)]
    all_to_all x1 -> x0, waiting for transfers between devices: 1.82 us -> none  [local(): lax.all_to_all(face_totals, 'vol', split_axis=0, concat_axis=0, tiled=True)]
  transfers between devices with their start and end apart: 3 -> 3, of which waited for: 3 -> 2; matrix products, arithmetic and copies ran while one was open for 12% -> 9% of each run, Pallas kernels for 0% -> 0%
where the time goes in v9:
time: 110 us; the launch traced here: 109 us
  waiting for transfers between devices  47 us (43%)
  matrix products  18.3 us (17%)
  local copies, waits for them, and re-layouts  16.2 us (15%)
  between operations  14.4 us (13%)
  starting transfers between devices  11.2 us (10%)
  other arithmetic  2.23 us (2%)
    all_to_all x1, waiting for transfers between devices, local(): got = lax.all_to_all(send, axes, 0, 0, tiled=True)  27.6 us
    all_gather x1, waiting for transfers between devices, local(): gathered = lax.all_gather(face_totals, 'vol', axis=0)  19.4 us
    dot_general x1, matrix products, local(): jnp.dot(selector, mold_faces, preferred_element_type=f32).astype(bf16)  7.5 us
    all_to_all x1, starting transfers between devices, local(): got = lax.all_to_all(send, axes, 0, 0, tiled=True)  7.32 us
    dot_general x1, matrix products, local(): lax.dot_general(selector, gained, contract0, preferred_element_type=f32)  6.51 us
    scatter x1, local copies, waits for them, and re-layouts, local(): send.reshape(devices * block, row_width).at[target * block + position]  3.73 us
    all_to_all x1, starting transfers between devices, local(): lax.all_to_all(answers.reshape(devices, capacity, row_width), axes, 0, 0,...  3.62 us
    unnamed x23, local copies, waits for them, and re-layouts  3.25 us
  transfers between devices with their start and end apart: 3, of which 2 were waited for; matrix products, arithmetic and copies ran while one was open for 9% of the time, Pallas kernels for 0%

profile of v9, /device:TPU:0, one launch (start us, length us, event | category | flops | bytes accessed | tf_op | source)
XLA Modules:
  0.0 109.3 jit_solution(12203404548721000272)
XLA Ops:
  7.2 0.0 copy-start
  7.2 0.0 copy-start.8
  7.2 0.0 copy-start.9
  7.2 1.3 %fusion.11 = f32[1024]{0:T(1024)S(1)} fusion(s32[1024]{0:T(1024)} %bitcast.37), kind=kOutput, calls=%fused_computation.17 | convolution fusion | flops 68353024 | bytes 8192 | tf_op jit(solution)/shard_map/dot_general | solution.py:41
  8.5 0.0 copy-done.9
  8.6 0.0 copy-done.8
  8.6 0.5 fusion.12
  9.0 0.5 fusion.13
  9.5 0.1 scatter.12.clone
  9.7 0.0 copy-start.4
  9.7 0.3 reshape.96
  10.0 0.6 copy-done.4
  10.6 3.7 %scatter_fusion = bf16[4160,128]{1,0:T(8,128)(2,1)S(1)} fusion(bf16[4160,128]{1,0:T(8,128)(2,1)S(1)} %reshape.96, s32[1024]{0:T(1024)S(1)} %bitcast.34, bf16[1024,128]{1,0:T(8,128)(2,1)S(1)} %copy-done.4), kind=kCustom, calls=%fused_computation.1 | custom fusion | bytes 790528 | tf_op jit(solution)/shard_map/scatter | solution.py:59
  14.4 1.2 %reshape.97 = bf16[32,130,128]{2,1,0:T(8,128)(2,1)} reshape(bf16[4160,128]{1,0:T(8,128)(2,1)S(1)} %scatter_fusion) | data formatting | bytes 2129920 | tf_op jit(solution)/shard_map/reshape | solution.py:60
  15.5 7.3 %all-to-all-start = ((bf16[32,130,128]{2,1,0:T(8,128)(2,1)}), bf16[32,130,128]{2,1,0:T(8,128)(2,1)S(1)}, u32[]{:S(2)}, u32[]{:S(2)}) async-start(bf16[32,130,128]{2,1,0:T(8,128)(2,1)} %reshape.97), calls=%async_computation | async-start | bytes 2228224 | tf_op jit(solution)/shard_map/all_to_all | solution.py:61
  22.9 0.0 copy-done.6
  22.9 27.6 %all-to-all-done = bf16[32,130,128]{2,1,0:T(8,128)(2,1)S(1)} async-done(((bf16[32,130,128]{2,1,0:T(8,128)(2,1)}), bf16[32,130,128]{2,1,0:T(8,128)(2,1)S(1)}, u32[]{:S(2)}, u32[]{:S(2)}) %all-to-all-start) | async-done | bytes 1064992 | tf_op jit(solution)/shard_map/all_to_all | solution.py:61
  50.5 7.5 %fusion.4 = bf16[4096,128]{0,1:T(8,128)(2,1)S(1)} fusion(bf16[2048,128]{1,0:T(8,128)(2,1)S(1)} %copy-done, s32[4096]{0:T(1024)S(1)} %bitcast.35), kind=kOutput, calls=%fused_computation.7 | convolution fusion | flops 2156396544 | bytes 1589248 | tf_op jit(solution)/shard_map/dot_general | solution.py:69
  58.1 0.1 slice.65
  58.2 0.8 copy-done.1
  59.0 0.4 fusion.50
  59.4 0.3 copy.23
  59.8 0.0 slice-start
  59.8 0.0 copy-start.5
  59.8 0.3 copy.22
  60.1 0.7 slice-done
  60.8 0.4 fusion.14
  61.2 0.1 copy_bitcast_fusion
  61.3 1.1 copy-done.2
  62.4 0.6 convolution_convert_fusion
  63.0 0.1 copy_bitcast_fusion.1
  63.1 1.1 pad_maximum_fusion
  64.2 3.6 %all-to-all-start.1 = ((bf16[32,128,128]{1,2,0:T(8,128)(2,1)}), bf16[32,128,128]{1,2,0:T(8,128)(2,1)S(1)}, u32[]{:S(2)}, u32[]{:S(2)}) async-start(bf16[32,128,128]{1,2,0:T(8,128)(2,1)} %pad_maximum_fusion), calls=%async_computation.1 | async-start | bytes 2097152 | tf_op jit(solution)/shard_map/all_to_all | solution.py:75
  67.8 0.2 all-gather.2.cloned.1.call-start
  68.0 6.5 %fusion.9 = bf16[2048,64]{0,1:T(8,128)(2,1)S(1)} fusion(s32[4096]{0:T(1024)S(1)} %bitcast.36, bf16[4096,128]{0,1:T(8,128)(2,1)S(1)} %convolution_convert_fusion), kind=kOutput, calls=%fused_computation.15 | convolution fusion | flops 1082261504 | bytes 802816 | tf_op jit(solution)/shard_map/dot_general | solution.py:78
  74.5 0.3 copy.20
  74.8 0.0 copy-start.3
  74.8 0.0 copy-start.7
  74.8 1.0 all_gather_reshape.3
  75.8 0.0 all-gather.2.cloned.1.call-update
  75.9 19.4 %all-gather.2.cloned.1.call-done = bf16[4,4,256,128]{3,2,1,0:T(8,128)(2,1)} async-done(((bf16[1,4,256,128]{3,2,1,0:T(8,128)(2,1)}), bf16[4,4,256,128]{3,2,1,0:T(8,128)(2,1)}) %all-gather.2.cloned.1.call-update) | async-done | bytes 1048592 | tf_op jit(solution)/shard_map/all_gather | solution.py:83
  95.3 1.0 constant_dynamic-slice_fusion
  96.3 0.2 convert_element_type.87
  96.6 1.2 %fusion.8 = bf16[2048,128]{1,0:T(8,128)(2,1)} fusion(bf16[2048,128]{1,0:T(8,128)(2,1)S(1)} %copy-done.3, bf16[128,128]{1,0:T(8,128)(2,1)S(1)} %copy-done.7, bf16[2048,64]{1,0:T(8,128)(2,1)S(1)} %convert_element_type.87), kind=kOutput, calls=%fused_computation.14 | convolution fusion | flops 68681728 | bytes 1343488 | tf_op jit(solution)/shard_map/dot_general | solution.py:85
  97.7 0.0 all-to-all-done.1
  97.7 0.7 copy.19
  98.4 3.2 %gather_fusion = bf16[1024,128]{1,0:T(8,128)(2,1)S(1)} fusion(bf16[4096,128]{1,0:T(8,128)(2,1)S(1)} %bitcast.29, s32[1024]{0:T(1024)S(1)} %broadcast_clamp_fusion), kind=kCustom, calls=%fused_computation | custom fusion | bytes 528384 | tf_op jit(solution)/shard_map/jit(_take)/gather | solution.py:81
  101.6 0.9 broadcast_select_fusion
  (17 shorter events, 0.2 us)
Async XLA Ops:
  7.2 43.4 %copy-start = (bf16[2048,128]{1,0:T(8,128)(2,1)S(1)}, bf16[2048,128]{1,0:T(8,128)(2,1)}, u32[]{:S(2)}) copy-start(bf16[2048,128]{1,0:T(8,128)(2,1)} %param.13) | copy-start | bytes 1572868
  7.2 1.4 %copy-start.8 = (s32[1024,1]{0,1:T(1,128)S(1)}, s32[1024,1]{0,1:T(1,128)}, u32[]{:S(2)}) copy-start(s32[1024,1]{0,1:T(1,128)} %param.11) | copy-start | bytes 12292
  7.2 1.3 %copy-start.9 = (s32[1024]{0:T(1024)S(1)}, s32[1024]{0:T(1024)}, u32[]{:S(2)}) copy-start(s32[1024]{0:T(1024)} %param.12) | copy-start | bytes 12292
  9.7 1.0 copy-start.4
  15.5 7.3 %copy-start.6 = (bf16[64,64]{1,0:T(8,128)(2,1)S(1)}, bf16[64,64]{1,0:T(8,128)(2,1)}, u32[]{:S(2)}) copy-start(bf16[64,64]{1,0:T(8,128)(2,1)} %param.15) | copy-start | bytes 24580
  15.5 34.9 %all-to-all-start = ((bf16[32,130,128]{2,1,0:T(8,128)(2,1)}), bf16[32,130,128]{2,1,0:T(8,128)(2,1)S(1)}, u32[]{:S(2)}, u32[]{:S(2)}) async-start(bf16[32,130,128]{2,1,0:T(8,128)(2,1)} %reshape.97), calls=%async_computation | async-start | bytes 2228224 | tf_op jit(solution)/shard_map/all_to_all | solution.py:61
  58.1 1.0 copy-start.1
  59.8 1.0 slice-start
  59.8 1.0 copy-start.5
  61.2 1.2 %copy-start.2 = (bf16[4096,128]{0,1:T(8,128)(2,1)S(1)}, bf16[4096,128]{0,1:T(8,128)(2,1)}, u32[]{:S(2)}) copy-start(bf16[4096,128]{0,1:T(8,128)(2,1)} %copy-done.1) | copy-start | bytes 3145732
  64.2 33.5 %all-to-all-start.1 = ((bf16[32,128,128]{1,2,0:T(8,128)(2,1)}), bf16[32,128,128]{1,2,0:T(8,128)(2,1)S(1)}, u32[]{:S(2)}, u32[]{:S(2)}) async-start(bf16[32,128,128]{1,2,0:T(8,128)(2,1)} %pad_maximum_fusion), calls=%async_computation.1 | async-start | bytes 2097152 | tf_op jit(solution)/shard_map/all_to_all | solution.py:75
  67.8 27.5 %all-gather.2.cloned.1.call-start = ((), (), s32[]{:S(2)}) async-start(), calls=%async_computation.2 | async-start | bytes 1310720 | tf_op jit(solution)/shard_map/all_gather | solution.py:83
  74.8 21.7 %copy-start.3 = (bf16[2048,128]{1,0:T(8,128)(2,1)S(1)}, bf16[2048,128]{1,0:T(8,128)(2,1)}, u32[]{:S(2)}) copy-start(bf16[2048,128]{1,0:T(8,128)(2,1)} %param.17) | copy-start | bytes 1572868
  74.8 21.7 %copy-start.7 = (bf16[128,128]{1,0:T(8,128)(2,1)S(1)}, bf16[128,128]{1,0:T(8,128)(2,1)}, u32[]{:S(2)}) copy-start(bf16[128,128]{1,0:T(8,128)(2,1)} %param.16) | copy-start | bytes 98308
Sparse Core Ops, SparseCore 0:
  75.9 19.3 all-gather.1

commit v10 on v5

--- a/solution.py
+++ b/solution.py
@@ -66,7 +66,7 @@
 
     face_range = jnp.arange(face_rows, dtype=jnp.int32)
     selector = (got_ids[:, None] == face_range[None, :]).astype(bf16)
-    mold_rows = jnp.dot(selector, mold_faces, preferred_element_type=f32).astype(bf16)
+    mold_rows = jnp.take(mold_faces, jnp.maximum(got_ids, 0), axis=0)
 
     stacked = jnp.concatenate([mortar_d.T, -mortar_m.T], axis=0)
     joined = jnp.concatenate([mortar_d, mortar_m], axis=1)

time: 98.6 us -> 107 us (1.085)
  local copies, waits for them, and re-layouts: 14.3 us -> 28.5 us
  matrix products: 18.3 us -> 10.8 us
  other arithmetic: 2.4 us -> 3.74 us
    gather x0 -> x2, local copies, waits for them, and re-layouts: none -> 13.4 us  [local(): mold_rows = jnp.take(mold_faces, jnp.maximum(got_ids, 0), axis=0)]
    dot_general x1 -> x0, matrix products: 7.5 us -> none  [local(): jnp.dot(selector, mold_faces, preferred_element_type=f32).astype(bf16)]
    select_n x0 -> x1, other arithmetic: none -> 1.33 us  [local(): mold_rows = jnp.take(mold_faces, jnp.maximum(got_ids, 0), axis=0)]
    unnamed x23 -> x25, local copies, waits for them, and re-layouts: 2.39 us -> 3.19 us
  transfers between devices with their start and end apart: 3 -> 3, of which waited for: 3 -> 3; matrix products, arithmetic and copies ran while one was open for 12% -> 11% of each run, Pallas kernels for 0% -> 0%
where the time goes in v10:
time: 107 us; the launch traced here: 106 us
  waiting for transfers between devices  47.6 us (44%)
  local copies, waits for them, and re-layouts  28.5 us (27%)
  starting transfers between devices  14.5 us (14%)
  matrix products  10.8 us (10%)
  other arithmetic  3.74 us (3%)
    all_to_all x1, waiting for transfers between devices, local(): got = lax.all_to_all(send, axes, 0, 0, tiled=True)  27.6 us
    all_to_all x1, waiting for transfers between devices, local(): lax.all_to_all(answers.reshape(devices, capacity, row_width), axes, 0, 0,...  18.2 us
    gather x2, local copies, waits for them, and re-layouts, local(): mold_rows = jnp.take(mold_faces, jnp.maximum(got_ids, 0), axis=0)  13.4 us
    all_to_all x1, starting transfers between devices, local(): got = lax.all_to_all(send, axes, 0, 0, tiled=True)  7.32 us
    dot_general x1, matrix products, local(): lax.dot_general(selector, gained, contract0, preferred_element_type=f32)  6.5 us
    all_to_all x1, starting transfers between devices, local(): lax.all_to_all(answers.reshape(devices, capacity, row_width), axes, 0, 0,...  3.8 us
    scatter x1, local copies, waits for them, and re-layouts, local(): send.reshape(devices * block, row_width).at[target * block + position]  3.73 us
    all_to_all x1, starting transfers between devices, local(): lax.all_to_all(face_totals, 'vol', split_axis=0, concat_axis=0, tiled=True)  3.42 us
  transfers between devices with their start and end apart: 3, of which 3 were waited for; matrix products, arithmetic and copies ran while one was open for 11% of the time, Pallas kernels for 0%

profile of v10, /device:TPU:0, one launch (start us, length us, event | category | flops | bytes accessed | tf_op | source)
XLA Modules:
  0.0 106.2 jit_solution(1424289758313055262)
XLA Ops:
  0.6 0.0 copy-start
  0.6 0.0 copy-start.9
  0.7 0.0 copy-start.10
  0.7 1.3 %fusion.8 = f32[1024]{0:T(1024)S(1)} fusion(s32[1024]{0:T(1024)} %bitcast.36), kind=kOutput, calls=%fused_computation.15 | convolution fusion | flops 68353024 | bytes 8192 | tf_op jit(solution)/shard_map/dot_general | solution.py:41
  2.0 0.0 copy-done.10
  2.0 0.5 fusion.10
  2.5 0.5 fusion.9
  3.0 0.1 scatter.12.clone
  3.1 0.0 copy-start.5
  3.2 0.3 reshape.135
  3.5 0.6 copy-done.5
  4.1 3.7 %scatter_fusion = bf16[4160,128]{1,0:T(8,128)(2,1)S(1)} fusion(bf16[4160,128]{1,0:T(8,128)(2,1)S(1)} %reshape.135, s32[1024]{0:T(1024)S(1)} %bitcast.35, bf16[1024,128]{1,0:T(8,128)(2,1)S(1)} %copy-done.5), kind=kCustom, calls=%fused_computation.2 | custom fusion | bytes 790528 | tf_op jit(solution)/shard_map/scatter | solution.py:59
  7.8 1.2 %reshape.136 = bf16[32,130,128]{2,1,0:T(8,128)(2,1)} reshape(bf16[4160,128]{1,0:T(8,128)(2,1)S(1)} %scatter_fusion) | data formatting | bytes 2129920 | tf_op jit(solution)/shard_map/reshape | solution.py:60
  9.0 7.3 %all-to-all-start = ((bf16[32,130,128]{2,1,0:T(8,128)(2,1)}), bf16[32,130,128]{2,1,0:T(8,128)(2,1)S(1)}, u32[]{:S(2)}, u32[]{:S(2)}) async-start(bf16[32,130,128]{2,1,0:T(8,128)(2,1)} %reshape.136), calls=%async_computation | async-start | bytes 2228224 | tf_op jit(solution)/shard_map/all_to_all | solution.py:61
  16.4 27.6 %all-to-all-done = bf16[32,130,128]{2,1,0:T(8,128)(2,1)S(1)} async-done(((bf16[32,130,128]{2,1,0:T(8,128)(2,1)}), bf16[32,130,128]{2,1,0:T(8,128)(2,1)S(1)}, u32[]{:S(2)}, u32[]{:S(2)}) %all-to-all-start) | async-done | bytes 1064992 | tf_op jit(solution)/shard_map/all_to_all | solution.py:61
  44.0 0.0 copy-done
  44.1 12.1 %gather_fusion = bf16[4096,128]{1,0:T(8,128)(2,1)S(1)} fusion(bf16[2048,128]{1,0:T(8,128)(2,1)S(1)} %copy-done, s32[4096]{0:T(1024)S(1)} %broadcast_clamp_fusion), kind=kCustom, calls=%fused_computation | custom fusion | bytes 2113536 | tf_op jit(solution)/shard_map/jit(_take)/gather | solution.py:69
  56.2 1.3 %copy.19 = bf16[4096,128]{0,1:T(8,128)(2,1)} copy(bf16[4096,128]{1,0:T(8,128)(2,1)S(1)} %gather_fusion) | data formatting | bytes 2097152 | tf_op jit(solution)/shard_map/jit(_take)/gather | solution.py:69
  57.5 1.3 %broadcast_select_fusion = bf16[4096,128]{0,1:T(8,128)(2,1)S(1)} fusion(bf16[4096,128]{0,1:T(8,128)(2,1)} %copy.19, pred[4096]{0:T(1024)(128)(4,1)S(1)} %maximum_compare_fusion), kind=kLoop, calls=%fused_computation.26 | loop fusion | flops 524288 | bytes 2101248 | tf_op jit(solution)/shard_map/jit(_take)/select_n | solution.py:69
  58.9 0.0 copy-start.1
  58.9 0.1 slice.70
  59.0 0.8 copy-done.1
  59.8 0.4 fusion.48
  60.2 1.1 %copy.26 = bf16[4096,64]{0,1:T(8,128)(2,1)} copy(bf16[4096,64]{1,0:T(8,128)(2,1)S(1)} %get-tuple-element.23) | data formatting | bytes 1048576
  61.3 0.3 copy.25
  61.7 0.0 copy-start.2
  61.7 0.7 slice-done
  62.4 0.2 copy-done.3
  62.5 0.0 copy-done.6
  62.5 0.4 fusion.11
  62.9 0.1 copy-done.2
  63.0 0.6 convolution_convert_fusion
  63.5 0.3 copy_bitcast_fusion
  63.8 1.1 %pad_maximum_fusion = bf16[32,128,128]{1,2,0:T(8,128)(2,1)} fusion(bf16[32,128,64]{1,2,0:T(8,128)(2,1)S(1)} %get-tuple-element.26, bf16[32,128,64]{1,2,0:T(8,128)(2,1)S(1)} %get-tuple-element.27), kind=kLoop, calls=%fused_computation.24 | loop fusion | flops 2097152 | bytes 2097152 | tf_op jit(solution)/shard_map/concatenate | solution.py:18
  64.9 3.8 %all-to-all-start.1 = ((bf16[32,128,128]{1,2,0:T(8,128)(2,1)}), bf16[32,128,128]{1,2,0:T(8,128)(2,1)S(1)}, u32[]{:S(2)}, u32[]{:S(2)}) async-start(bf16[32,128,128]{1,2,0:T(8,128)(2,1)} %pad_maximum_fusion), calls=%async_computation.1 | async-start | bytes 2097152 | tf_op jit(solution)/shard_map/all_to_all | solution.py:75
  68.8 6.5 %fusion.6 = bf16[2048,64]{0,1:T(8,128)(2,1)S(1)} fusion(s32[4096]{0:T(1024)S(1)} %bitcast.31, bf16[4096,128]{0,1:T(8,128)(2,1)S(1)} %convolution_convert_fusion), kind=kOutput, calls=%fused_computation.13 | convolution fusion | flops 1082261504 | bytes 802816 | tf_op jit(solution)/shard_map/dot_general | solution.py:78
  75.3 0.3 copy.20
  75.5 1.0 reshape.138
  76.5 18.2 %all-to-all-done.1 = bf16[32,128,128]{1,2,0:T(8,128)(2,1)S(1)} async-done(((bf16[32,128,128]{1,2,0:T(8,128)(2,1)}), bf16[32,128,128]{1,2,0:T(8,128)(2,1)S(1)}, u32[]{:S(2)}, u32[]{:S(2)}) %all-to-all-start.1) | async-done | bytes 1048608 | tf_op jit(solution)/shard_map/all_to_all | solution.py:75
  94.7 0.7 copy.23
  95.4 3.4 %all-to-all-start.2 = ((bf16[4,256,128]{2,1,0:T(8,128)(2,1)}), bf16[4,256,128]{2,1,0:T(8,128)(2,1)S(1)}, u32[]{:S(2)}, u32[]{:S(2)}) async-start(bf16[4,256,128]{2,1,0:T(8,128)(2,1)} %reshape.138), calls=%async_computation.2 | async-start | bytes 524288 | tf_op jit(solution)/shard_map/all_to_all | solution.py:84
  98.8 3.2 %gather_fusion.1 = bf16[1024,128]{1,0:T(8,128)(2,1)S(1)} fusion(bf16[4096,128]{1,0:T(8,128)(2,1)S(1)} %bitcast.27, s32[1024]{0:T(1024)S(1)} %broadcast_clamp_fusion.1), kind=kCustom, calls=%fused_computation.1 | custom fusion | bytes 528384 | tf_op jit(solution)/shard_map/jit(_take)/gather | solution.py:82
  102.0 0.0 copy-start.4
  102.1 0.0 copy-start.8
  102.1 0.9 broadcast_select_fusion.1
  103.0 1.8 %all-to-all-done.2 = bf16[4,256,128]{2,1,0:T(8,128)(2,1)S(1)} async-done(((bf16[4,256,128]{2,1,0:T(8,128)(2,1)}), bf16[4,256,128]{2,1,0:T(8,128)(2,1)S(1)}, u32[]{:S(2)}, u32[]{:S(2)}) %all-to-all-start.2) | async-done | bytes 262176 | tf_op jit(solution)/shard_map/all_to_all | solution.py:84
  104.8 0.2 convert_element_type.92
  105.1 1.1 %fusion.5 = bf16[2048,128]{1,0:T(8,128)(2,1)} fusion(bf16[2048,128]{1,0:T(8,128)(2,1)S(1)} %copy-done.4, bf16[128,128]{1,0:T(8,128)(2,1)S(1)} %copy-done.8, bf16[2048,64]{1,0:T(8,128)(2,1)S(1)} %convert_element_type.92), kind=kOutput, calls=%fused_computation.12 | convolution fusion | flops 68681728 | bytes 1343488 | tf_op jit(solution)/shard_map/dot_general | solution.py:91
  (20 shorter events, 0.2 us)
Async XLA Ops:
  0.6 43.4 %copy-start = (bf16[2048,128]{1,0:T(8,128)(2,1)S(1)}, bf16[2048,128]{1,0:T(8,128)(2,1)}, u32[]{:S(2)}) copy-start(bf16[2048,128]{1,0:T(8,128)(2,1)} %param.13) | copy-start | bytes 1572868
  0.6 1.4 %copy-start.9 = (s32[1024,1]{0,1:T(1,128)S(1)}, s32[1024,1]{0,1:T(1,128)}, u32[]{:S(2)}) copy-start(s32[1024,1]{0,1:T(1,128)} %param.11) | copy-start | bytes 12292
  0.7 1.3 %copy-start.10 = (s32[1024]{0:T(1024)S(1)}, s32[1024]{0:T(1024)}, u32[]{:S(2)}) copy-start(s32[1024]{0:T(1024)} %param.12) | copy-start | bytes 12292
  3.1 1.0 copy-start.5
  9.0 7.3 %copy-start.7 = (bf16[64,64]{1,0:T(8,128)(2,1)S(1)}, bf16[64,64]{1,0:T(8,128)(2,1)}, u32[]{:S(2)}) copy-start(bf16[64,64]{1,0:T(8,128)(2,1)} %param.15) | copy-start | bytes 24580
  9.0 34.9 %all-to-all-start = ((bf16[32,130,128]{2,1,0:T(8,128)(2,1)}), bf16[32,130,128]{2,1,0:T(8,128)(2,1)S(1)}, u32[]{:S(2)}, u32[]{:S(2)}) async-start(bf16[32,130,128]{2,1,0:T(8,128)(2,1)} %reshape.136), calls=%async_computation | async-start | bytes 2228224 | tf_op jit(solution)/shard_map/all_to_all | solution.py:61
  58.9 1.0 copy-start.1
  61.3 1.0 slice-start
  61.3 1.2 %copy-start.3 = (bf16[4096,64]{0,1:T(8,128)(2,1)S(1)}, bf16[4096,64]{0,1:T(8,128)(2,1)}, u32[]{:S(2)}) copy-start(bf16[4096,64]{0,1:T(8,128)(2,1)} %copy.26) | copy-start | bytes 1572868
  61.3 1.2 %copy-start.6 = (bf16[64,64]{1,0:T(8,128)(2,1)S(1)}, bf16[64,64]{1,0:T(8,128)(2,1)}, u32[]{:S(2)}) copy-start(bf16[64,64]{1,0:T(8,128)(2,1)} %param.14) | copy-start | bytes 24580
  61.7 1.3 %copy-start.2 = (bf16[4096,128]{0,1:T(8,128)(2,1)S(1)}, bf16[4096,128]{0,1:T(8,128)(2,1)}, u32[]{:S(2)}) copy-start(bf16[4096,128]{0,1:T(8,128)(2,1)} %copy-done.1) | copy-start | bytes 3145732
  64.9 29.8 %all-to-all-start.1 = ((bf16[32,128,128]{1,2,0:T(8,128)(2,1)}), bf16[32,128,128]{1,2,0:T(8,128)(2,1)S(1)}, u32[]{:S(2)}, u32[]{:S(2)}) async-start(bf16[32,128,128]{1,2,0:T(8,128)(2,1)} %pad_maximum_fusion), calls=%async_computation.1 | async-start | bytes 2097152 | tf_op jit(solution)/shard_map/all_to_all | solution.py:75
  95.4 9.4 %all-to-all-start.2 = ((bf16[4,256,128]{2,1,0:T(8,128)(2,1)}), bf16[4,256,128]{2,1,0:T(8,128)(2,1)S(1)}, u32[]{:S(2)}, u32[]{:S(2)}) async-start(bf16[4,256,128]{2,1,0:T(8,128)(2,1)} %reshape.138), calls=%async_computation.2 | async-start | bytes 524288 | tf_op jit(solution)/shard_map/all_to_all | solution.py:84
  102.0 3.0 %copy-start.4 = (bf16[2048,128]{1,0:T(8,128)(2,1)S(1)}, bf16[2048,128]{1,0:T(8,128)(2,1)}, u32[]{:S(2)}) copy-start(bf16[2048,128]{1,0:T(8,128)(2,1)} %param.17) | copy-start | bytes 1572868
  102.1 3.0 %copy-start.8 = (bf16[128,128]{1,0:T(8,128)(2,1)S(1)}, bf16[128,128]{1,0:T(8,128)(2,1)}, u32[]{:S(2)}) copy-start(bf16[128,128]{1,0:T(8,128)(2,1)} %param.16) | copy-start | bytes 98308

commit v11 on v5

--- a/solution.py
+++ b/solution.py
@@ -68,9 +68,18 @@
     selector = (got_ids[:, None] == face_range[None, :]).astype(bf16)
     mold_rows = jnp.dot(selector, mold_faces, preferred_element_type=f32).astype(bf16)
 
-    stacked = jnp.concatenate([mortar_d.T, -mortar_m.T], axis=0)
-    joined = jnp.concatenate([mortar_d, mortar_m], axis=1)
-    answers, gained = contact(got_rows, mold_rows, stacked, joined, node_count)
+    zero = jnp.zeros((node_count, node_count), bf16)
+    wc = jnp.block([[zero, mortar_d.T], [zero, zero]])
+    wm = jnp.block([[zero, -mortar_m.T], [zero, zero]])
+    wj = jnp.block([[zero, zero], [mortar_d, mortar_m]])
+    gap = jnp.dot(got_rows, wc, preferred_element_type=f32) + jnp.dot(
+        mold_rows, wm, preferred_element_type=f32
+    )
+    flux = (got_rows.astype(f32) * mold_rows.astype(f32) * gap).astype(bf16)
+    projected = jnp.dot(flux, wj, preferred_element_type=f32)
+    lane = lax.broadcasted_iota(jnp.int32, (slots, row_width), 1)
+    answers = jnp.where(lane < node_count, projected, gap).astype(bf16)
+    gained = projected[:, node_count:].astype(bf16)
 
     returned = lax.all_to_all(
         answers.reshape(devices, capacity, row_width), axes, 0, 0, tiled=True

time: 98.6 us -> 96 us (0.974)
  local copies, waits for them, and re-layouts: 14.3 us -> 10.4 us
  matrix products: 18.3 us -> 20.8 us
    unnamed x23 -> x17, local copies, waits for them, and re-layouts: 2.39 us -> 0.24 us
    dot_general x2 -> x3, matrix products: 0.9 us -> 2.63 us  [the longest x1 1.64 us: local(): projected = jnp.dot(flux, wj, preferred_element_type=f32)]
    concatenate x2 -> x0, other arithmetic: 1.36 us -> none  [contact(): jnp.concatenate([projected[:, :node_count], gap_jump], axis=1)]
    dot_general x1, matrix products: 7.5 us -> 6.43 us  [local(): jnp.dot(selector, mold_faces, preferred_element_type=f32).astype(bf16)]
    slice x3 -> x0, local copies, waits for them, and re-layouts: 1.06 us -> none  [the longest x2 0.68 us: contact(): mold_rows[:, :node_count]]
  transfers between devices with their start and end apart: 3 -> 3, of which waited for: 3 -> 3; matrix products, arithmetic and copies ran while one was open for 12% -> 13% of each run, Pallas kernels for 0% -> 0%
where the time goes in v11:
time: 96 us; the launch traced here: 95.5 us
  waiting for transfers between devices  47 us (49%)
  matrix products  20.8 us (22%)
  starting transfers between devices  14.7 us (15%)
  local copies, waits for them, and re-layouts  10.4 us (11%)
  other arithmetic  1.73 us (2%)
    all_to_all x1, waiting for transfers between devices, local(): got = lax.all_to_all(send, axes, 0, 0, tiled=True)  27.4 us
    all_to_all x1, waiting for transfers between devices, local(): lax.all_to_all(answers.reshape(devices, capacity, row_width), axes, 0, 0,...  17.8 us
    all_to_all x1, starting transfers between devices, local(): got = lax.all_to_all(send, axes, 0, 0, tiled=True)  7.32 us
    dot_general x1, matrix products, local(): lax.dot_general(selector, gained, contract0, preferred_element_type=f32)  6.94 us
    dot_general x1, matrix products, local(): jnp.dot(selector, mold_faces, preferred_element_type=f32).astype(bf16)  6.43 us
    all_to_all x1, starting transfers between devices, local(): lax.all_to_all(answers.reshape(devices, capacity, row_width), axes, 0, 0,...  3.81 us
    scatter x1, local copies, waits for them, and re-layouts, local(): send.reshape(devices * block, row_width).at[target * block + position]  3.74 us
    all_to_all x1, starting transfers between devices, local(): lax.all_to_all(face_totals, 'vol', split_axis=0, concat_axis=0, tiled=True)  3.54 us
  transfers between devices with their start and end apart: 3, of which 3 were waited for; matrix products, arithmetic and copies ran while one was open for 13% of the time, Pallas kernels for 0%

profile of v11, /device:TPU:0, one launch (start us, length us, event | category | flops | bytes accessed | tf_op | source)
XLA Modules:
  0.0 95.5 jit_solution(11148072988733705854)
XLA Ops:
  0.6 0.0 copy-start
  0.6 1.3 %fusion.11 = f32[1024]{0:T(1024)S(1)} fusion(s32[1024]{0:T(1024)} %bitcast.29), kind=kOutput, calls=%fused_computation.20 | convolution fusion | flops 68353024 | bytes 8192 | tf_op jit(solution)/shard_map/dot_general | solution.py:41
  2.0 0.7 fusion.47
  2.7 0.0 copy-start.6
  2.7 0.0 copy-start.2
  2.7 1.2 %fusion.12 = bf16[32,1,128]{2,0,1:T(8,128)(2,1)S(1)} fusion(s32[1024]{0:T(1024)S(1)} %convert_element_type.76, bf16[1024]{0:T(1024)(128)(2,1)S(1)} %get-tuple-element.20, s32[1024]{0:T(1024)} %bitcast.30), kind=kOutput, calls=%fused_computation.23 | convolution fusion | flops 8687616 | bytes 18432 | tf_op jit(solution)/shard_map/dot_general | solution.py:49
  3.9 1.1 %fusion.13 = bf16[32,1,128]{2,0,1:T(8,128)(2,1)S(1)} fusion(s32[1024]{0:T(1024)S(1)} %convert_element_type.76, bf16[1024]{0:T(1024)(128)(2,1)S(1)} %get-tuple-element.21, s32[1024]{0:T(1024)} %bitcast.31), kind=kOutput, calls=%fused_computation.24 | convolution fusion | flops 8687616 | bytes 18432 | tf_op jit(solution)/shard_map/dot_general | solution.py:50
  5.1 0.1 scatter.12.clone
  5.2 0.3 reshape.96
  5.6 0.0 copy-done.6
  5.6 0.0 copy-done.2
  5.6 3.7 %scatter_fusion = bf16[4160,128]{1,0:T(8,128)(2,1)S(1)} fusion(bf16[4160,128]{1,0:T(8,128)(2,1)S(1)} %reshape.96, s32[1024]{0:T(1024)S(1)} %bitcast.26, bf16[1024,128]{1,0:T(8,128)(2,1)S(1)} %copy-done.2), kind=kCustom, calls=%fused_computation.1 | custom fusion | bytes 790528 | tf_op jit(solution)/shard_map/scatter | solution.py:59
  9.3 0.0 copy-start.3
  9.4 0.0 copy-start.4
  9.4 1.2 %reshape.97 = bf16[32,130,128]{2,1,0:T(8,128)(2,1)} reshape(bf16[4160,128]{1,0:T(8,128)(2,1)S(1)} %scatter_fusion) | data formatting | bytes 2129920 | tf_op jit(solution)/shard_map/reshape | solution.py:60
  10.5 7.3 %all-to-all-start = ((bf16[32,130,128]{2,1,0:T(8,128)(2,1)}), bf16[32,130,128]{2,1,0:T(8,128)(2,1)S(1)}, u32[]{:S(2)}, u32[]{:S(2)}) async-start(bf16[32,130,128]{2,1,0:T(8,128)(2,1)} %reshape.97), calls=%async_computation | async-start | bytes 2228224 | tf_op jit(solution)/shard_map/all_to_all | solution.py:61
  17.9 0.0 copy-done.3
  17.9 0.1 copy.13
  18.0 0.0 copy-done.4
  18.0 0.1 copy.14
  18.1 27.4 %all-to-all-done = bf16[32,130,128]{2,1,0:T(8,128)(2,1)S(1)} async-done(((bf16[32,130,128]{2,1,0:T(8,128)(2,1)}), bf16[32,130,128]{2,1,0:T(8,128)(2,1)S(1)}, u32[]{:S(2)}, u32[]{:S(2)}) %all-to-all-start) | async-done | bytes 1064992 | tf_op jit(solution)/shard_map/all_to_all | solution.py:61
  45.5 0.0 copy-done
  45.5 6.4 %fusion.4 = bf16[4096,128]{1,0:T(8,128)(2,1)S(1)} fusion(bf16[2048,128]{1,0:T(8,128)(2,1)S(1)} %copy-done, s32[4096]{0:T(1024)S(1)} %bitcast.27), kind=kOutput, calls=%fused_computation.8 | convolution fusion | flops 2156396544 | bytes 1589248 | tf_op jit(solution)/shard_map/dot_general | solution.py:69
  52.0 0.1 slice.47
  52.1 0.5 fusion.31
  52.6 0.5 convolution_add_fusion
  53.1 1.6 %select_convert_fusion = (bf16[4096,128]{1,0:T(8,128)(2,1)}, bf16[4096,128]{1,0:T(8,128)(2,1)S(1)}) fusion(f32[4096,128]{1,0:T(8,128)S(1)} %convolution_add_fusion, pred[128]{0:T(512)(128)(4,1)S(1)} %iota_compare_fusion.19, bf16[64,64]{1,0:T(8,128)(2,1)S(1)} %copy-done.4, bf16[64,64]{1,0:T(8,128)(2,1)S(1)} %copy-done.3, ...), kind=kOutput, calls=%fused_computation.17 | convolution fusion | flops 137461760 | bytes 6324352 | tf_op jit(solution)/shard_map/dot_general | solution.py:79
  54.8 3.8 %all-to-all-start.1 = ((bf16[32,128,128]{2,1,0:T(8,128)(2,1)}), bf16[32,128,128]{2,1,0:T(8,128)(2,1)S(1)}, u32[]{:S(2)}, u32[]{:S(2)}) async-start(bf16[32,128,128]{2,1,0:T(8,128)(2,1)} %bitcast.9), calls=%async_computation.1 | async-start | bytes 2097152 | tf_op jit(solution)/shard_map/all_to_all | solution.py:84
  58.6 6.9 %fusion.9 = bf16[2048,64]{0,1:T(8,128)(2,1)S(1)} fusion(s32[4096]{0:T(1024)S(1)} %bitcast.28, bf16[4096,128]{1,0:T(8,128)(2,1)S(1)} %get-tuple-element.23), kind=kOutput, calls=%fused_computation.15 | convolution fusion | flops 1082261504 | bytes 1327104 | tf_op jit(solution)/shard_map/dot_general | solution.py:87
  65.6 0.3 copy.15
  65.9 1.0 %reshape.99 = bf16[4,256,128]{2,1,0:T(8,128)(2,1)} reshape(bf16[2048,64]{1,0:T(8,128)(2,1)S(1)} %copy.15) | data formatting | bytes 524288 | tf_op jit(solution)/shard_map/reshape | solution.py:89
  66.8 17.8 %all-to-all-done.1 = bf16[32,128,128]{2,1,0:T(8,128)(2,1)S(1)} async-done(((bf16[32,128,128]{2,1,0:T(8,128)(2,1)}), bf16[32,128,128]{2,1,0:T(8,128)(2,1)S(1)}, u32[]{:S(2)}, u32[]{:S(2)}) %all-to-all-start.1) | async-done | bytes 1048608 | tf_op jit(solution)/shard_map/all_to_all | solution.py:84
  84.6 0.0 copy-start.1
  84.6 0.0 copy-start.5
  84.6 3.5 %all-to-all-start.2 = ((bf16[4,256,128]{2,1,0:T(8,128)(2,1)}), bf16[4,256,128]{2,1,0:T(8,128)(2,1)S(1)}, u32[]{:S(2)}, u32[]{:S(2)}) async-start(bf16[4,256,128]{2,1,0:T(8,128)(2,1)} %reshape.99), calls=%async_computation.2 | async-start | bytes 524288 | tf_op jit(solution)/shard_map/all_to_all | solution.py:93
  88.2 3.2 %gather_fusion = bf16[1024,128]{1,0:T(8,128)(2,1)S(1)} fusion(bf16[4096,128]{1,0:T(8,128)(2,1)S(1)} %bitcast.22, s32[1024]{0:T(1024)S(1)} %broadcast_clamp_fusion), kind=kCustom, calls=%fused_computation | custom fusion | bytes 528384 | tf_op jit(solution)/shard_map/jit(_take)/gather | solution.py:91
  91.4 0.9 broadcast_select_fusion
  92.3 1.8 %all-to-all-done.2 = bf16[4,256,128]{2,1,0:T(8,128)(2,1)S(1)} async-done(((bf16[4,256,128]{2,1,0:T(8,128)(2,1)}), bf16[4,256,128]{2,1,0:T(8,128)(2,1)S(1)}, u32[]{:S(2)}, u32[]{:S(2)}) %all-to-all-start.2) | async-done | bytes 262176 | tf_op jit(solution)/shard_map/all_to_all | solution.py:93
  94.1 0.2 convert_element_type.89
  94.4 0.0 copy-done.1
  94.4 0.0 copy-done.5
  94.4 1.1 %fusion.8 = bf16[2048,128]{1,0:T(8,128)(2,1)} fusion(bf16[2048,128]{1,0:T(8,128)(2,1)S(1)} %copy-done.1, bf16[128,128]{1,0:T(8,128)(2,1)S(1)} %copy-done.5, bf16[2048,64]{1,0:T(8,128)(2,1)S(1)} %convert_element_type.89), kind=kOutput, calls=%fused_computation.14 | convolution fusion | flops 68681728 | bytes 1343488 | tf_op jit(solution)/shard_map/dot_general | solution.py:100
  (13 shorter events, 0.1 us)
Async XLA Ops:
  0.6 44.9 %copy-start = (bf16[2048,128]{1,0:T(8,128)(2,1)S(1)}, bf16[2048,128]{1,0:T(8,128)(2,1)}, u32[]{:S(2)}) copy-start(bf16[2048,128]{1,0:T(8,128)(2,1)} %param.13) | copy-start | bytes 1572868
  2.7 2.9 %copy-start.6 = (s32[1024,1]{0,1:T(1,128)S(1)}, s32[1024,1]{0,1:T(1,128)}, u32[]{:S(2)}) copy-start(s32[1024,1]{0,1:T(1,128)} %param.11) | copy-start | bytes 12292
  2.7 2.9 %copy-start.2 = (bf16[1024,128]{1,0:T(8,128)(2,1)S(1)}, bf16[1024,128]{1,0:T(8,128)(2,1)}, u32[]{:S(2)}) copy-start(bf16[1024,128]{1,0:T(8,128)(2,1)} %param.10) | copy-start | bytes 786436
  9.3 8.5 %copy-start.3 = (bf16[64,64]{1,0:T(8,128)(2,1)S(1)}, bf16[64,64]{1,0:T(8,128)(2,1)}, u32[]{:S(2)}) copy-start(bf16[64,64]{1,0:T(8,128)(2,1)} %param.14) | copy-start | bytes 24580
  9.4 8.6 %copy-start.4 = (bf16[64,64]{1,0:T(8,128)(2,1)S(1)}, bf16[64,64]{1,0:T(8,128)(2,1)}, u32[]{:S(2)}) copy-start(bf16[64,64]{1,0:T(8,128)(2,1)} %param.15) | copy-start | bytes 24580
  10.5 34.9 %all-to-all-start = ((bf16[32,130,128]{2,1,0:T(8,128)(2,1)}), bf16[32,130,128]{2,1,0:T(8,128)(2,1)S(1)}, u32[]{:S(2)}, u32[]{:S(2)}) async-start(bf16[32,130,128]{2,1,0:T(8,128)(2,1)} %reshape.97), calls=%async_computation | async-start | bytes 2228224 | tf_op jit(solution)/shard_map/all_to_all | solution.py:61
  54.8 29.8 %all-to-all-start.1 = ((bf16[32,128,128]{2,1,0:T(8,128)(2,1)}), bf16[32,128,128]{2,1,0:T(8,128)(2,1)S(1)}, u32[]{:S(2)}, u32[]{:S(2)}) async-start(bf16[32,128,128]{2,1,0:T(8,128)(2,1)} %bitcast.9), calls=%async_computation.1 | async-start | bytes 2097152 | tf_op jit(solution)/shard_map/all_to_all | solution.py:84
  84.6 9.8 %copy-start.1 = (bf16[2048,128]{1,0:T(8,128)(2,1)S(1)}, bf16[2048,128]{1,0:T(8,128)(2,1)}, u32[]{:S(2)}) copy-start(bf16[2048,128]{1,0:T(8,128)(2,1)} %param.17) | copy-start | bytes 1572868
  84.6 9.8 %copy-start.5 = (bf16[128,128]{1,0:T(8,128)(2,1)S(1)}, bf16[128,128]{1,0:T(8,128)(2,1)}, u32[]{:S(2)}) copy-start(bf16[128,128]{1,0:T(8,128)(2,1)} %param.16) | copy-start | bytes 98308
  84.6 9.5 %all-to-all-start.2 = ((bf16[4,256,128]{2,1,0:T(8,128)(2,1)}), bf16[4,256,128]{2,1,0:T(8,128)(2,1)S(1)}, u32[]{:S(2)}, u32[]{:S(2)}) async-start(bf16[4,256,128]{2,1,0:T(8,128)(2,1)} %reshape.99), calls=%async_computation.2 | async-start | bytes 524288 | tf_op jit(solution)/shard_map/all_to_all | solution.py:93

commit v12 on v11

--- a/solution.py
+++ b/solution.py
@@ -46,18 +46,17 @@
     pos_hot = (position[:, None] == jnp.arange(capacity, dtype=jnp.int32)[None, :]).astype(bf16)
     hi = (code // 64).astype(bf16)[:, None]
     lo = (code % 64).astype(bf16)[:, None]
-    id_hi = lax.dot_general(hits, pos_hot * hi, contract0, preferred_element_type=f32)
-    id_lo = lax.dot_general(hits, pos_hot * lo, contract0, preferred_element_type=f32)
     id_count = 2 * capacity
     id_height = -(-id_count // row_width)
-    id_flat = jnp.stack([id_hi, id_lo], axis=1).reshape(devices, id_count)
+    codes = jnp.concatenate([pos_hot * hi, pos_hot * lo], axis=1)
+    id_flat = lax.dot_general(hits, codes, contract0, preferred_element_type=f32)
     id_flat = jnp.pad(id_flat, ((0, 0), (0, id_height * row_width - id_count)))
     id_rows = id_flat.reshape(devices, id_height, row_width)
 
-    block = capacity + id_height
-    send = jnp.zeros((devices, block, row_width), bf16).at[:, capacity:, :].set(id_rows.astype(bf16))
-    send = send.reshape(devices * block, row_width).at[target * block + position].set(casting)
-    send = send.reshape(devices, block, row_width)
+    send_rows = jnp.zeros((slots, row_width), bf16).at[slot_index].set(casting)
+    send = jnp.concatenate(
+        [send_rows.reshape(devices, capacity, row_width), id_rows.astype(bf16)], axis=1
+    )
     got = lax.all_to_all(send, axes, 0, 0, tiled=True)
     got_rows = got[:, :capacity, :].reshape(slots, row_width)
     got_code = got[:, capacity:, :].astype(f32).reshape(devices, id_height * row_width)

time: 96 us -> 95.3 us (level)
  other arithmetic: 1.73 us -> 3.95 us
  matrix products: 20.8 us -> 19.3 us
  local copies, waits for them, and re-layouts: 10.4 us -> 8.93 us
    reshape x2 -> x0, local copies, waits for them, and re-layouts: 1.48 us -> none  [the longest x1 1.16 us: local(): send = send.reshape(devices, block, row_width)]
    dot_general x2 -> x1, matrix products: 2.34 us -> 0.89 us  [local(): lax.dot_general(hits, codes, contract0, preferred_element_type=f32)]
    concatenate x0 -> x1, other arithmetic: none -> 1.08 us  [local(): jnp.concatenate([send_rows.reshape(devices, capacity, row_width), id_rows...]
    scatter x2 -> x1, local copies, waits for them, and re-layouts: 3.89 us -> 3.89 us  [local(): send_rows = jnp.zeros((slots, row_width), bf16).at[slot_index].set(casting)]
where the time goes in v12:
time: 95.3 us; the launch traced here: 94.8 us
  waiting for transfers between devices  47 us (49%)
  matrix products  19.3 us (20%)
  starting transfers between devices  14.7 us (15%)
  local copies, waits for them, and re-layouts  8.93 us (9%)
  other arithmetic  3.95 us (4%)
    all_to_all x1, waiting for transfers between devices, local(): got = lax.all_to_all(send, axes, 0, 0, tiled=True)  27.4 us
    all_to_all x1, waiting for transfers between devices, local(): lax.all_to_all(answers.reshape(devices, capacity, row_width), axes, 0, 0,...  17.8 us
    all_to_all x1, starting transfers between devices, local(): got = lax.all_to_all(send, axes, 0, 0, tiled=True)  7.32 us
    dot_general x1, matrix products, local(): lax.dot_general(selector, gained, contract0, preferred_element_type=f32)  6.94 us
    dot_general x1, matrix products, local(): jnp.dot(selector, mold_faces, preferred_element_type=f32).astype(bf16)  6.44 us
    scatter x1, local copies, waits for them, and re-layouts, local(): send_rows = jnp.zeros((slots, row_width), bf16).at[slot_index].set(casting)  3.89 us
    all_to_all x1, starting transfers between devices, local(): lax.all_to_all(answers.reshape(devices, capacity, row_width), axes, 0, 0,...  3.81 us
    all_to_all x1, starting transfers between devices, local(): lax.all_to_all(face_totals, 'vol', split_axis=0, concat_axis=0, tiled=True)  3.54 us
  transfers between devices with their start and end apart: 3, of which 3 were waited for; matrix products, arithmetic and copies ran while one was open for 13% of the time, Pallas kernels for 0%

profile of v12, /device:TPU:0, one launch (start us, length us, event | category | flops | bytes accessed | tf_op | source)
XLA Modules:
  0.0 94.8 jit_solution(4749484525670771308)
XLA Ops:
  0.6 0.0 copy-start
  0.6 1.3 %fusion.11 = f32[1024]{0:T(1024)S(1)} fusion(s32[1024]{0:T(1024)} %bitcast.27), kind=kOutput, calls=%fused_computation.20 | convolution fusion | flops 68353024 | bytes 8192 | tf_op jit(solution)/shard_map/dot_general | solution.py:41
  2.0 0.7 fusion.41
  2.7 0.7 and_reduce_fusion
  3.4 0.5 fusion.17
  3.9 0.9 convolution_convert_fusion
  4.8 3.9 %scatter_custom_fusion = bf16[4096,128]{1,0:T(8,128)(2,1)S(1)} fusion(s32[1024]{0:T(1024)S(1)} %bitcast.25, bf16[1024,128]{1,0:T(8,128)(2,1)} %param.8, bf16[]{:T(256)} %constant.56.clone.1), kind=kCustom, calls=%fused_computation.30 | custom fusion | bytes 1049088 | tf_op jit(solution)/shard_map/scatter | solution.py:56
  8.7 0.0 copy-start.2
  8.7 0.0 copy-start.3
  8.7 1.1 %pad_maximum_fusion = bf16[32,130,128]{2,1,0:T(8,128)(2,1)} fusion(bf16[32,2,128]{2,1,0:T(2,128)(2,1)S(1)} %convert_element_type.85, bf16[32,128,128]{2,1,0:T(8,128)(2,1)S(1)} %bitcast.20), kind=kLoop, calls=%fused_computation.21 | loop fusion | flops 2129920 | bytes 2129920 | tf_op jit(solution)/shard_map/concatenate | solution.py:57
  9.8 7.3 %all-to-all-start = ((bf16[32,130,128]{2,1,0:T(8,128)(2,1)}), bf16[32,130,128]{2,1,0:T(8,128)(2,1)S(1)}, u32[]{:S(2)}, u32[]{:S(2)}) async-start(bf16[32,130,128]{2,1,0:T(8,128)(2,1)} %pad_maximum_fusion), calls=%async_computation | async-start | bytes 2228224 | tf_op jit(solution)/shard_map/all_to_all | solution.py:60
  17.1 0.0 copy-done.2
  17.1 0.1 copy.12
  17.2 0.0 copy-done.3
  17.2 0.1 copy.13
  17.4 27.4 %all-to-all-done = bf16[32,130,128]{2,1,0:T(8,128)(2,1)S(1)} async-done(((bf16[32,130,128]{2,1,0:T(8,128)(2,1)}), bf16[32,130,128]{2,1,0:T(8,128)(2,1)S(1)}, u32[]{:S(2)}, u32[]{:S(2)}) %all-to-all-start) | async-done | bytes 1064992 | tf_op jit(solution)/shard_map/all_to_all | solution.py:60
  44.8 0.0 copy-done
  44.8 6.4 %fusion.4 = bf16[4096,128]{1,0:T(8,128)(2,1)S(1)} fusion(bf16[2048,128]{1,0:T(8,128)(2,1)S(1)} %copy-done, s32[4096]{0:T(1024)S(1)} %bitcast.23), kind=kOutput, calls=%fused_computation.8 | convolution fusion | flops 2156396544 | bytes 1589248 | tf_op jit(solution)/shard_map/dot_general | solution.py:68
  51.2 0.1 slice.26
  51.4 0.5 fusion.25
  51.9 0.5 convolution_add_fusion
  52.4 1.6 %select_convert_fusion = (bf16[4096,128]{1,0:T(8,128)(2,1)}, bf16[4096,128]{1,0:T(8,128)(2,1)S(1)}) fusion(f32[4096,128]{1,0:T(8,128)S(1)} %convolution_add_fusion, pred[128]{0:T(512)(128)(4,1)S(1)} %iota_compare_fusion.18, bf16[64,64]{1,0:T(8,128)(2,1)S(1)} %copy-done.3, bf16[64,64]{1,0:T(8,128)(2,1)S(1)} %copy-done.2, ...), kind=kOutput, calls=%fused_computation.17 | convolution fusion | flops 137461760 | bytes 6324352 | tf_op jit(solution)/shard_map/dot_general | solution.py:78
  54.0 3.8 %all-to-all-start.1 = ((bf16[32,128,128]{2,1,0:T(8,128)(2,1)}), bf16[32,128,128]{2,1,0:T(8,128)(2,1)S(1)}, u32[]{:S(2)}, u32[]{:S(2)}) async-start(bf16[32,128,128]{2,1,0:T(8,128)(2,1)} %bitcast.8), calls=%async_computation.1 | async-start | bytes 2097152 | tf_op jit(solution)/shard_map/all_to_all | solution.py:83
  57.8 6.9 %fusion.9 = bf16[2048,64]{0,1:T(8,128)(2,1)S(1)} fusion(s32[4096]{0:T(1024)S(1)} %bitcast.24, bf16[4096,128]{1,0:T(8,128)(2,1)S(1)} %get-tuple-element.13), kind=kOutput, calls=%fused_computation.15 | convolution fusion | flops 1082261504 | bytes 1327104 | tf_op jit(solution)/shard_map/dot_general | solution.py:86
  64.8 0.3 copy.14
  65.1 1.0 %reshape.63 = bf16[4,256,128]{2,1,0:T(8,128)(2,1)} reshape(bf16[2048,64]{1,0:T(8,128)(2,1)S(1)} %copy.14) | data formatting | bytes 524288 | tf_op jit(solution)/shard_map/reshape | solution.py:88
  66.0 17.8 %all-to-all-done.1 = bf16[32,128,128]{2,1,0:T(8,128)(2,1)S(1)} async-done(((bf16[32,128,128]{2,1,0:T(8,128)(2,1)}), bf16[32,128,128]{2,1,0:T(8,128)(2,1)S(1)}, u32[]{:S(2)}, u32[]{:S(2)}) %all-to-all-start.1) | async-done | bytes 1048608 | tf_op jit(solution)/shard_map/all_to_all | solution.py:83
  83.8 0.0 copy-start.1
  83.8 0.0 copy-start.4
  83.8 3.5 %all-to-all-start.2 = ((bf16[4,256,128]{2,1,0:T(8,128)(2,1)}), bf16[4,256,128]{2,1,0:T(8,128)(2,1)S(1)}, u32[]{:S(2)}, u32[]{:S(2)}) async-start(bf16[4,256,128]{2,1,0:T(8,128)(2,1)} %reshape.63), calls=%async_computation.2 | async-start | bytes 524288 | tf_op jit(solution)/shard_map/all_to_all | solution.py:92
  87.4 3.2 %gather_fusion = bf16[1024,128]{1,0:T(8,128)(2,1)S(1)} fusion(bf16[4096,128]{1,0:T(8,128)(2,1)S(1)} %bitcast.19, s32[1024]{0:T(1024)S(1)} %broadcast_clamp_fusion), kind=kCustom, calls=%fused_computation | custom fusion | bytes 528384 | tf_op jit(solution)/shard_map/jit(_take)/gather | solution.py:90
  90.6 0.9 broadcast_select_fusion
  91.5 1.8 %all-to-all-done.2 = bf16[4,256,128]{2,1,0:T(8,128)(2,1)S(1)} async-done(((bf16[4,256,128]{2,1,0:T(8,128)(2,1)}), bf16[4,256,128]{2,1,0:T(8,128)(2,1)S(1)}, u32[]{:S(2)}, u32[]{:S(2)}) %all-to-all-start.2) | async-done | bytes 262176 | tf_op jit(solution)/shard_map/all_to_all | solution.py:92
  93.4 0.2 convert_element_type.95
  93.6 0.0 copy-done.1
  93.6 0.0 copy-done.4
  93.6 1.2 %fusion.8 = bf16[2048,128]{1,0:T(8,128)(2,1)} fusion(bf16[2048,128]{1,0:T(8,128)(2,1)S(1)} %copy-done.1, bf16[128,128]{1,0:T(8,128)(2,1)S(1)} %copy-done.4, bf16[2048,64]{1,0:T(8,128)(2,1)S(1)} %convert_element_type.95), kind=kOutput, calls=%fused_computation.14 | convolution fusion | flops 68681728 | bytes 1343488 | tf_op jit(solution)/shard_map/dot_general | solution.py:99
  (10 shorter events, 0.1 us)
Async XLA Ops:
  0.6 44.1 %copy-start = (bf16[2048,128]{1,0:T(8,128)(2,1)S(1)}, bf16[2048,128]{1,0:T(8,128)(2,1)}, u32[]{:S(2)}) copy-start(bf16[2048,128]{1,0:T(8,128)(2,1)} %param.11) | copy-start | bytes 1572868
  8.7 8.5 %copy-start.2 = (bf16[64,64]{1,0:T(8,128)(2,1)S(1)}, bf16[64,64]{1,0:T(8,128)(2,1)}, u32[]{:S(2)}) copy-start(bf16[64,64]{1,0:T(8,128)(2,1)} %param.12) | copy-start | bytes 24580
  8.7 8.6 %copy-start.3 = (bf16[64,64]{1,0:T(8,128)(2,1)S(1)}, bf16[64,64]{1,0:T(8,128)(2,1)}, u32[]{:S(2)}) copy-start(bf16[64,64]{1,0:T(8,128)(2,1)} %param.13) | copy-start | bytes 24580
  9.8 34.9 %all-to-all-start = ((bf16[32,130,128]{2,1,0:T(8,128)(2,1)}), bf16[32,130,128]{2,1,0:T(8,128)(2,1)S(1)}, u32[]{:S(2)}, u32[]{:S(2)}) async-start(bf16[32,130,128]{2,1,0:T(8,128)(2,1)} %pad_maximum_fusion), calls=%async_computation | async-start | bytes 2228224 | tf_op jit(solution)/shard_map/all_to_all | solution.py:60
  54.0 29.8 %all-to-all-start.1 = ((bf16[32,128,128]{2,1,0:T(8,128)(2,1)}), bf16[32,128,128]{2,1,0:T(8,128)(2,1)S(1)}, u32[]{:S(2)}, u32[]{:S(2)}) async-start(bf16[32,128,128]{2,1,0:T(8,128)(2,1)} %bitcast.8), calls=%async_computation.1 | async-start | bytes 2097152 | tf_op jit(solution)/shard_map/all_to_all | solution.py:83
  83.8 9.8 %copy-start.1 = (bf16[2048,128]{1,0:T(8,128)(2,1)S(1)}, bf16[2048,128]{1,0:T(8,128)(2,1)}, u32[]{:S(2)}) copy-start(bf16[2048,128]{1,0:T(8,128)(2,1)} %param.15) | copy-start | bytes 1572868
  83.8 9.8 %copy-start.4 = (bf16[128,128]{1,0:T(8,128)(2,1)S(1)}, bf16[128,128]{1,0:T(8,128)(2,1)}, u32[]{:S(2)}) copy-start(bf16[128,128]{1,0:T(8,128)(2,1)} %param.14) | copy-start | bytes 98308
  83.8 9.5 %all-to-all-start.2 = ((bf16[4,256,128]{2,1,0:T(8,128)(2,1)}), bf16[4,256,128]{2,1,0:T(8,128)(2,1)S(1)}, u32[]{:S(2)}, u32[]{:S(2)}) async-start(bf16[4,256,128]{2,1,0:T(8,128)(2,1)} %reshape.63), calls=%async_computation.2 | async-start | bytes 524288 | tf_op jit(solution)/shard_map/all_to_all | solution.py:92

commit v13 on v12

--- a/solution.py
+++ b/solution.py
@@ -87,7 +87,7 @@
     quarter = face_rows // vol_count
     face_totals = totals.astype(bf16).reshape(vol_count, quarter * node_count // row_width, row_width)
     face_totals, returned = lax.optimization_barrier((face_totals, returned))
-    casting_out = jnp.take(returned, slot_index, axis=0)
+    casting_out = jnp.take(returned, slot_index, axis=0, mode="clip")
 
     relaid = lax.all_to_all(
         face_totals,
@@ -97,9 +97,11 @@
         tiled=True,
     )
     heat = jnp.dot(volume, conduct, preferred_element_type=f32)
+    settled = volume.astype(f32) - relax * heat
+    settled, relaid = lax.optimization_barrier((settled, relaid))
     placed = relaid.reshape(face_rows, node_count).astype(f32)
     inject = jnp.concatenate([placed, jnp.zeros((face_rows, node_count), f32)], axis=1)
-    mold_out = (volume.astype(f32) + relax * (inject - heat)).astype(bf16)
+    mold_out = (settled + relax * inject).astype(bf16)
     return (casting_out, mold_out)
 
 

time: 95.3 us -> 94.6 us (level)
  waiting for transfers between devices: 47 us -> 45.3 us
  local copies, waits for them, and re-layouts: 8.93 us -> 10 us
    all_to_all x1, waiting for transfers between devices: 17.8 us -> 16.3 us  [local(): lax.all_to_all(answers.reshape(devices, capacity, row_width), axes, 0, 0,...]
    dot_general x1, matrix products: 6.94 us -> 8.16 us  [local(): lax.dot_general(selector, gained, contract0, preferred_element_type=f32)]
    gather x1, local copies, waits for them, and re-layouts: 3.21 us -> 4.31 us  [local(): casting_out = jnp.take(returned, slot_index, axis=0, mode='clip')]
    convert_element_type x0 -> x1, other arithmetic: none -> 0.97 us  [local(): mold_out = (settled + relax * inject).astype(bf16)]
  transfers between devices with their start and end apart: 3 -> 3, of which waited for: 3 -> 3; matrix products, arithmetic and copies ran while one was open for 13% -> 15% of each run, Pallas kernels for 0% -> 0%
where the time goes in v13:
time: 94.6 us; the launch traced here: 94.1 us
  waiting for transfers between devices  45.3 us (48%)
  matrix products  20 us (21%)
  starting transfers between devices  14.5 us (15%)
  local copies, waits for them, and re-layouts  10 us (11%)
  other arithmetic  3.31 us (3%)
    all_to_all x1, waiting for transfers between devices, local(): got = lax.all_to_all(send, axes, 0, 0, tiled=True)  27.4 us
    all_to_all x1, waiting for transfers between devices, local(): lax.all_to_all(answers.reshape(devices, capacity, row_width), axes, 0, 0,...  16.3 us
    dot_general x1, matrix products, local(): lax.dot_general(selector, gained, contract0, preferred_element_type=f32)  8.16 us
    all_to_all x1, starting transfers between devices, local(): got = lax.all_to_all(send, axes, 0, 0, tiled=True)  7.32 us
    dot_general x1, matrix products, local(): jnp.dot(selector, mold_faces, preferred_element_type=f32).astype(bf16)  6.43 us
    gather x1, local copies, waits for them, and re-layouts, local(): casting_out = jnp.take(returned, slot_index, axis=0, mode='clip')  4.31 us
    scatter x1, local copies, waits for them, and re-layouts, local(): send_rows = jnp.zeros((slots, row_width), bf16).at[slot_index].set(casting)  3.89 us
    all_to_all x1, starting transfers between devices, local(): lax.all_to_all(answers.reshape(devices, capacity, row_width), axes, 0, 0,...  3.81 us
  transfers between devices with their start and end apart: 3, of which 3 were waited for; matrix products, arithmetic and copies ran while one was open for 15% of the time, Pallas kernels for 0%

profile of v13, /device:TPU:0, one launch (start us, length us, event | category | flops | bytes accessed | tf_op | source)
XLA Modules:
  0.0 94.1 jit_solution(9594704421034201458)
XLA Ops:
  0.6 0.0 copy-start
  0.6 0.0 copy-start.5
  0.7 1.3 %fusion.9 = f32[1024]{0:T(1024)S(1)} fusion(s32[1024]{0:T(1024)} %bitcast.26), kind=kOutput, calls=%fused_computation.18 | convolution fusion | flops 68353024 | bytes 8192 | tf_op jit(solution)/shard_map/dot_general | solution.py:41
  2.0 0.7 fusion.39
  2.7 0.5 fusion.15
  3.2 0.9 convolution_convert_fusion
  4.1 0.0 copy-done.5
  4.1 3.9 %scatter_custom_fusion = bf16[4096,128]{1,0:T(8,128)(2,1)S(1)} fusion(s32[1024]{0:T(1024)S(1)} %bitcast.28, bf16[1024,128]{1,0:T(8,128)(2,1)} %param.8, bf16[]{:T(256)} %constant.39.clone.1), kind=kCustom, calls=%fused_computation.29 | custom fusion | bytes 1049088 | tf_op jit(solution)/shard_map/scatter | solution.py:56
  8.0 0.0 copy-start.2
  8.0 0.0 copy-start.3
  8.0 1.1 %pad_maximum_fusion = bf16[32,130,128]{2,1,0:T(8,128)(2,1)} fusion(bf16[32,2,128]{2,1,0:T(2,128)(2,1)S(1)} %convert_element_type.85, bf16[32,128,128]{2,1,0:T(8,128)(2,1)S(1)} %bitcast.20), kind=kLoop, calls=%fused_computation.19 | loop fusion | flops 2129920 | bytes 2129920 | tf_op jit(solution)/shard_map/concatenate | solution.py:57
  9.1 7.3 %all-to-all-start = ((bf16[32,130,128]{2,1,0:T(8,128)(2,1)}), bf16[32,130,128]{2,1,0:T(8,128)(2,1)S(1)}, u32[]{:S(2)}, u32[]{:S(2)}) async-start(bf16[32,130,128]{2,1,0:T(8,128)(2,1)} %pad_maximum_fusion), calls=%async_computation | async-start | bytes 2228224 | tf_op jit(solution)/shard_map/all_to_all | solution.py:60
  16.5 0.0 copy-done.2
  16.5 0.1 copy.12
  16.6 0.0 copy-done.3
  16.6 0.1 copy.13
  16.7 27.4 %all-to-all-done = bf16[32,130,128]{2,1,0:T(8,128)(2,1)S(1)} async-done(((bf16[32,130,128]{2,1,0:T(8,128)(2,1)}), bf16[32,130,128]{2,1,0:T(8,128)(2,1)S(1)}, u32[]{:S(2)}, u32[]{:S(2)}) %all-to-all-start) | async-done | bytes 1064992 | tf_op jit(solution)/shard_map/all_to_all | solution.py:60
  44.1 0.0 copy-done
  44.1 6.4 %fusion.4 = bf16[4096,128]{1,0:T(8,128)(2,1)S(1)} fusion(bf16[2048,128]{1,0:T(8,128)(2,1)S(1)} %copy-done, s32[4096]{0:T(1024)S(1)} %bitcast.23), kind=kOutput, calls=%fused_computation.8 | convolution fusion | flops 2156396544 | bytes 1589248 | tf_op jit(solution)/shard_map/dot_general | solution.py:68
  50.6 0.1 slice.26
  50.7 0.5 fusion.23
  51.2 0.5 convolution_add_fusion
  51.7 2.0 %select_convert_fusion = (bf16[4096,128]{1,0:T(8,128)(2,1)}, bf16[4096,128]{1,0:T(8,128)(2,1)}) fusion(f32[4096,128]{1,0:T(8,128)S(1)} %convolution_add_fusion, pred[128]{0:T(512)(128)(4,1)S(1)} %iota_compare_fusion.18, bf16[64,64]{1,0:T(8,128)(2,1)S(1)} %copy-done.3, bf16[64,64]{1,0:T(8,128)(2,1)S(1)} %copy-done.2, bf16[64,128]{1,0:T(8,128)(2,1)S(1)} %concatenate.43, ...), kind=kOutput, calls=%fused_computation.15 | convolution fusion | flops 137461760 | bytes 6324352 | tf_op jit(solution)/shard_map/dot_general | solution.py:78
  53.7 0.0 copy-start.1
  53.7 0.0 copy-start.4
  53.7 3.8 %all-to-all-start.1 = ((bf16[32,128,128]{2,1,0:T(8,128)(2,1)}), bf16[32,128,128]{2,1,0:T(8,128)(2,1)S(1)}, u32[]{:S(2)}, u32[]{:S(2)}) async-start(bf16[32,128,128]{2,1,0:T(8,128)(2,1)} %bitcast.8), calls=%async_computation.1 | async-start | bytes 2097152 | tf_op jit(solution)/shard_map/all_to_all | solution.py:83
  57.5 0.0 copy-done.1
  57.5 0.0 copy-done.4
  57.5 0.3 fusion.6
  57.8 8.2 %fusion.7 = bf16[2048,64]{0,1:T(8,128)(2,1)S(1)} fusion(s32[4096]{0:T(1024)S(1)} %bitcast.24, bf16[4096,128]{1,0:T(8,128)(2,1)} %get-tuple-element.17), kind=kOutput, calls=%fused_computation.13 | convolution fusion | flops 1082261504 | bytes 1327104 | tf_op jit(solution)/shard_map/dot_general | solution.py:86
  66.0 0.3 copy.14
  66.3 1.0 %reshape.59 = bf16[4,256,128]{2,1,0:T(8,128)(2,1)} reshape(bf16[2048,64]{1,0:T(8,128)(2,1)S(1)} %copy.14) | data formatting | bytes 524288 | tf_op jit(solution)/shard_map/reshape | solution.py:88
  67.2 16.3 %all-to-all-done.1 = bf16[32,128,128]{2,1,0:T(8,128)(2,1)S(1)} async-done(((bf16[32,128,128]{2,1,0:T(8,128)(2,1)}), bf16[32,128,128]{2,1,0:T(8,128)(2,1)S(1)}, u32[]{:S(2)}, u32[]{:S(2)}) %all-to-all-start.1) | async-done | bytes 1048608 | tf_op jit(solution)/shard_map/all_to_all | solution.py:83
  83.5 3.4 %all-to-all-start.2 = ((bf16[4,256,128]{2,1,0:T(8,128)(2,1)}), bf16[4,256,128]{2,1,0:T(8,128)(2,1)S(1)}, u32[]{:S(2)}, u32[]{:S(2)}) async-start(bf16[4,256,128]{2,1,0:T(8,128)(2,1)} %reshape.59), calls=%async_computation.2 | async-start | bytes 524288 | tf_op jit(solution)/shard_map/all_to_all | solution.py:92
  87.0 4.3 %gather_fusion = bf16[1024,128]{1,0:T(8,128)(2,1)} fusion(bf16[4096,128]{1,0:T(8,128)(2,1)S(1)} %bitcast.19, s32[1024]{0:T(1024)S(1)} %broadcast_clamp_fusion), kind=kCustom, calls=%fused_computation | custom fusion | bytes 528384 | tf_op jit(solution)/shard_map/jit(_take)/gather | solution.py:90
  91.3 1.6 %all-to-all-done.2 = bf16[4,256,128]{2,1,0:T(8,128)(2,1)S(1)} async-done(((bf16[4,256,128]{2,1,0:T(8,128)(2,1)}), bf16[4,256,128]{2,1,0:T(8,128)(2,1)S(1)}, u32[]{:S(2)}, u32[]{:S(2)}) %all-to-all-start.2) | async-done | bytes 262176 | tf_op jit(solution)/shard_map/all_to_all | solution.py:92
  92.9 0.2 convert_element_type.95
  93.2 1.0 %add_convert_fusion = bf16[2048,128]{1,0:T(8,128)(2,1)} fusion(f32[2048,128]{1,0:T(8,128)S(1)} %fusion.6, bf16[2048,64]{1,0:T(8,128)(2,1)S(1)} %convert_element_type.95), kind=kLoop, calls=%fused_computation.22 | loop fusion | flops 1048576 | bytes 1835008 | tf_op jit(solution)/shard_map/convert_element_type | solution.py:104
  (11 shorter events, 0.1 us)
Async XLA Ops:
  0.6 43.5 %copy-start = (bf16[2048,128]{1,0:T(8,128)(2,1)S(1)}, bf16[2048,128]{1,0:T(8,128)(2,1)}, u32[]{:S(2)}) copy-start(bf16[2048,128]{1,0:T(8,128)(2,1)} %param.11) | copy-start | bytes 1572868
  0.6 3.4 %copy-start.5 = (s32[1024,1]{0,1:T(1,128)S(1)}, s32[1024,1]{0,1:T(1,128)}, u32[]{:S(2)}) copy-start(s32[1024,1]{0,1:T(1,128)} %param.9) | copy-start | bytes 12292
  8.0 8.5 %copy-start.2 = (bf16[64,64]{1,0:T(8,128)(2,1)S(1)}, bf16[64,64]{1,0:T(8,128)(2,1)}, u32[]{:S(2)}) copy-start(bf16[64,64]{1,0:T(8,128)(2,1)} %param.12) | copy-start | bytes 24580
  8.0 8.6 %copy-start.3 = (bf16[64,64]{1,0:T(8,128)(2,1)S(1)}, bf16[64,64]{1,0:T(8,128)(2,1)}, u32[]{:S(2)}) copy-start(bf16[64,64]{1,0:T(8,128)(2,1)} %param.13) | copy-start | bytes 24580
  9.1 34.9 %all-to-all-start = ((bf16[32,130,128]{2,1,0:T(8,128)(2,1)}), bf16[32,130,128]{2,1,0:T(8,128)(2,1)S(1)}, u32[]{:S(2)}, u32[]{:S(2)}) async-start(bf16[32,130,128]{2,1,0:T(8,128)(2,1)} %pad_maximum_fusion), calls=%async_computation | async-start | bytes 2228224 | tf_op jit(solution)/shard_map/all_to_all | solution.py:60
  53.7 3.8 %copy-start.1 = (bf16[2048,128]{1,0:T(8,128)(2,1)S(1)}, bf16[2048,128]{1,0:T(8,128)(2,1)}, u32[]{:S(2)}) copy-start(bf16[2048,128]{1,0:T(8,128)(2,1)} %param.15) | copy-start | bytes 1572868
  53.7 3.8 %copy-start.4 = (bf16[128,128]{1,0:T(8,128)(2,1)S(1)}, bf16[128,128]{1,0:T(8,128)(2,1)}, u32[]{:S(2)}) copy-start(bf16[128,128]{1,0:T(8,128)(2,1)} %param.14) | copy-start | bytes 98308
  53.7 29.8 %all-to-all-start.1 = ((bf16[32,128,128]{2,1,0:T(8,128)(2,1)}), bf16[32,128,128]{2,1,0:T(8,128)(2,1)S(1)}, u32[]{:S(2)}, u32[]{:S(2)}) async-start(bf16[32,128,128]{2,1,0:T(8,128)(2,1)} %bitcast.8), calls=%async_computation.1 | async-start | bytes 2097152 | tf_op jit(solution)/shard_map/all_to_all | solution.py:83
  83.5 9.4 %all-to-all-start.2 = ((bf16[4,256,128]{2,1,0:T(8,128)(2,1)}), bf16[4,256,128]{2,1,0:T(8,128)(2,1)S(1)}, u32[]{:S(2)}, u32[]{:S(2)}) async-start(bf16[4,256,128]{2,1,0:T(8,128)(2,1)} %reshape.59), calls=%async_computation.2 | async-start | bytes 524288 | tf_op jit(solution)/shard_map/all_to_all | solution.py:92

commit v14 on v13

--- a/solution.py
+++ b/solution.py
@@ -1,3 +1,5 @@
+import math
+
 import jax
 import jax.numpy as jnp
 from jax import lax
@@ -35,11 +37,19 @@
 
     target = owner[:, 0]
     hits = (target[:, None] == jnp.arange(devices, dtype=jnp.int32)[None, :]).astype(bf16)
-    row_i = lax.broadcasted_iota(jnp.int32, (seg_rows, seg_rows), 0)
-    row_j = lax.broadcasted_iota(jnp.int32, (seg_rows, seg_rows), 1)
+    span = math.gcd(seg_rows, 128)
+    spans = seg_rows // span
+    row_i = lax.broadcasted_iota(jnp.int32, (span, span), 0)
+    row_j = lax.broadcasted_iota(jnp.int32, (span, span), 1)
     earlier = (row_j < row_i).astype(bf16)
-    before = jnp.dot(earlier, hits, preferred_element_type=f32)
-    position = jnp.sum(before * hits.astype(f32), axis=1).astype(jnp.int32)
+    hit_blocks = hits.reshape(spans, span, devices)
+    within = jnp.einsum("ij,bjd->bid", earlier, hit_blocks, preferred_element_type=f32)
+    block_totals = jnp.sum(hit_blocks.astype(f32), axis=1).astype(bf16)
+    blk_i = lax.broadcasted_iota(jnp.int32, (spans, spans), 0)
+    blk_j = lax.broadcasted_iota(jnp.int32, (spans, spans), 1)
+    prior = jnp.dot((blk_j < blk_i).astype(bf16), block_totals, preferred_element_type=f32)
+    before = within + prior[:, None, :]
+    position = jnp.sum(before * hit_blocks.astype(f32), axis=2).reshape(seg_rows).astype(jnp.int32)
     slot_index = target * capacity + position
 
     code = face_id + 1

time: 94.6 us -> 96.2 us (1.017)
  other arithmetic: 3.31 us -> 4.85 us
where the time goes in v14:
time: 96.2 us; the launch traced here: 95.7 us
  waiting for transfers between devices  45.3 us (47%)
  matrix products  20 us (21%)
  starting transfers between devices  14.5 us (15%)
  local copies, waits for them, and re-layouts  10.1 us (10%)
  other arithmetic  4.85 us (5%)
    all_to_all x1, waiting for transfers between devices, local(): got = lax.all_to_all(send, axes, 0, 0, tiled=True)  27.4 us
    all_to_all x1, waiting for transfers between devices, local(): lax.all_to_all(answers.reshape(devices, capacity, row_width), axes, 0, 0,...  16.3 us
    dot_general x1, matrix products, local(): lax.dot_general(selector, gained, contract0, preferred_element_type=f32)  8.17 us
    all_to_all x1, starting transfers between devices, local(): got = lax.all_to_all(send, axes, 0, 0, tiled=True)  7.33 us
    dot_general x1, matrix products, local(): jnp.dot(selector, mold_faces, preferred_element_type=f32).astype(bf16)  6.44 us
    gather x1, local copies, waits for them, and re-layouts, local(): casting_out = jnp.take(returned, slot_index, axis=0, mode='clip')  4.31 us
    scatter x1, local copies, waits for them, and re-layouts, local(): send_rows = jnp.zeros((slots, row_width), bf16).at[slot_index].set(casting)  3.89 us
    all_to_all x1, starting transfers between devices, local(): lax.all_to_all(answers.reshape(devices, capacity, row_width), axes, 0, 0,...  3.81 us
  transfers between devices with their start and end apart: 3, of which 3 were waited for; matrix products, arithmetic and copies ran while one was open for 15% of the time, Pallas kernels for 0%

profile of v14, /device:TPU:0, one launch (start us, length us, event | category | flops | bytes accessed | tf_op | source)
XLA Modules:
  0.0 95.7 jit_solution(11579121108036392978)
XLA Ops:
  0.6 0.0 copy-start
  0.6 0.9 fusion.20
  1.5 0.1 fusion.44
  1.6 1.0 fusion.9
  2.6 0.7 fusion.42
  3.3 0.5 fusion.15
  3.8 1.1 %convolution_convert_fusion = bf16[32,256]{1,0:T(8,128)(2,1)S(1)} fusion(bf16[1024,128]{1,0:T(8,128)(2,1)S(1)} %get-tuple-element.15, bf16[1024,128]{1,0:T(8,128)(2,1)S(1)} %get-tuple-element.14, s32[1024]{0:T(1024)} %bitcast.40), kind=kOutput, calls=%fused_computation.20 | convolution fusion | flops 17866752 | bytes 544768 | tf_op jit(solution)/shard_map/dot_general | solution.py:62
  4.9 0.7 compare_select_fusion
  5.6 3.9 %scatter_custom_fusion = bf16[4096,128]{1,0:T(8,128)(2,1)S(1)} fusion(s32[1024]{0:T(1024)S(1)} %bitcast.42, bf16[1024,128]{1,0:T(8,128)(2,1)} %param.8, bf16[]{:T(256)} %constant.40.clone.1), kind=kCustom, calls=%fused_computation.30 | custom fusion | bytes 1049088 | tf_op jit(solution)/shard_map/scatter | solution.py:66
  9.5 0.0 copy-start.2
  9.5 0.0 copy-start.3
  9.6 1.1 %pad_maximum_fusion = bf16[32,130,128]{2,1,0:T(8,128)(2,1)} fusion(bf16[32,2,128]{2,1,0:T(2,128)(2,1)S(1)} %convert_element_type.93, bf16[32,128,128]{2,1,0:T(8,128)(2,1)S(1)} %bitcast.33), kind=kLoop, calls=%fused_computation.19 | loop fusion | flops 2129920 | bytes 2129920 | tf_op jit(solution)/shard_map/concatenate | solution.py:67
  10.7 7.3 %all-to-all-start = ((bf16[32,130,128]{2,1,0:T(8,128)(2,1)}), bf16[32,130,128]{2,1,0:T(8,128)(2,1)S(1)}, u32[]{:S(2)}, u32[]{:S(2)}) async-start(bf16[32,130,128]{2,1,0:T(8,128)(2,1)} %pad_maximum_fusion), calls=%async_computation | async-start | bytes 2228224 | tf_op jit(solution)/shard_map/all_to_all | solution.py:70
  18.0 0.0 copy-done.2
  18.0 0.1 copy.12
  18.1 0.0 copy-done.3
  18.1 0.1 copy.13
  18.2 27.4 %all-to-all-done = bf16[32,130,128]{2,1,0:T(8,128)(2,1)S(1)} async-done(((bf16[32,130,128]{2,1,0:T(8,128)(2,1)}), bf16[32,130,128]{2,1,0:T(8,128)(2,1)S(1)}, u32[]{:S(2)}, u32[]{:S(2)}) %all-to-all-start) | async-done | bytes 1064992 | tf_op jit(solution)/shard_map/all_to_all | solution.py:70
  45.7 0.0 copy-done
  45.7 6.4 %fusion.4 = bf16[4096,128]{1,0:T(8,128)(2,1)S(1)} fusion(bf16[2048,128]{1,0:T(8,128)(2,1)S(1)} %copy-done, s32[4096]{0:T(1024)S(1)} %bitcast.35), kind=kOutput, calls=%fused_computation.8 | convolution fusion | flops 2156396544 | bytes 1589248 | tf_op jit(solution)/shard_map/dot_general | solution.py:78
  52.1 0.1 slice.26
  52.2 0.5 fusion.26
  52.7 0.5 convolution_add_fusion
  53.2 2.0 %select_convert_fusion = (bf16[4096,128]{1,0:T(8,128)(2,1)}, bf16[4096,128]{1,0:T(8,128)(2,1)}) fusion(f32[4096,128]{1,0:T(8,128)S(1)} %convolution_add_fusion, pred[128]{0:T(512)(128)(4,1)S(1)} %iota_compare_fusion.16, bf16[64,64]{1,0:T(8,128)(2,1)S(1)} %copy-done.3, bf16[64,64]{1,0:T(8,128)(2,1)S(1)} %copy-done.2, bf16[64,128]{1,0:T(8,128)(2,1)S(1)} %concatenate.43, ...), kind=kOutput, calls=%fused_computation.13 | convolution fusion | flops 137461760 | bytes 6324352 | tf_op jit(solution)/shard_map/dot_general | solution.py:88
  55.2 0.0 copy-start.1
  55.2 0.0 copy-start.4
  55.2 3.8 %all-to-all-start.1 = ((bf16[32,128,128]{2,1,0:T(8,128)(2,1)}), bf16[32,128,128]{2,1,0:T(8,128)(2,1)S(1)}, u32[]{:S(2)}, u32[]{:S(2)}) async-start(bf16[32,128,128]{2,1,0:T(8,128)(2,1)} %bitcast.12), calls=%async_computation.1 | async-start | bytes 2097152 | tf_op jit(solution)/shard_map/all_to_all | solution.py:93
  59.1 0.0 copy-done.1
  59.1 0.0 copy-done.4
  59.1 0.3 fusion.5
  59.4 8.2 %fusion.6 = bf16[2048,64]{0,1:T(8,128)(2,1)S(1)} fusion(s32[4096]{0:T(1024)S(1)} %bitcast.36, bf16[4096,128]{1,0:T(8,128)(2,1)} %get-tuple-element.19), kind=kOutput, calls=%fused_computation.11 | convolution fusion | flops 1082261504 | bytes 1327104 | tf_op jit(solution)/shard_map/dot_general | solution.py:96
  67.5 0.3 copy.14
  67.8 1.0 %reshape.83 = bf16[4,256,128]{2,1,0:T(8,128)(2,1)} reshape(bf16[2048,64]{1,0:T(8,128)(2,1)S(1)} %copy.14) | data formatting | bytes 524288 | tf_op jit(solution)/shard_map/reshape | solution.py:98
  68.8 16.3 %all-to-all-done.1 = bf16[32,128,128]{2,1,0:T(8,128)(2,1)S(1)} async-done(((bf16[32,128,128]{2,1,0:T(8,128)(2,1)}), bf16[32,128,128]{2,1,0:T(8,128)(2,1)S(1)}, u32[]{:S(2)}, u32[]{:S(2)}) %all-to-all-start.1) | async-done | bytes 1048608 | tf_op jit(solution)/shard_map/all_to_all | solution.py:93
  85.1 3.4 %all-to-all-start.2 = ((bf16[4,256,128]{2,1,0:T(8,128)(2,1)}), bf16[4,256,128]{2,1,0:T(8,128)(2,1)S(1)}, u32[]{:S(2)}, u32[]{:S(2)}) async-start(bf16[4,256,128]{2,1,0:T(8,128)(2,1)} %reshape.83), calls=%async_computation.2 | async-start | bytes 524288 | tf_op jit(solution)/shard_map/all_to_all | solution.py:102
  88.5 4.3 %gather_fusion = bf16[1024,128]{1,0:T(8,128)(2,1)} fusion(bf16[4096,128]{1,0:T(8,128)(2,1)S(1)} %bitcast.32, s32[1024]{0:T(1024)S(1)} %broadcast_clamp_fusion), kind=kCustom, calls=%fused_computation | custom fusion | bytes 528384 | tf_op jit(solution)/shard_map/jit(_take)/gather | solution.py:100
  92.8 1.6 %all-to-all-done.2 = bf16[4,256,128]{2,1,0:T(8,128)(2,1)S(1)} async-done(((bf16[4,256,128]{2,1,0:T(8,128)(2,1)}), bf16[4,256,128]{2,1,0:T(8,128)(2,1)S(1)}, u32[]{:S(2)}, u32[]{:S(2)}) %all-to-all-start.2) | async-done | bytes 262176 | tf_op jit(solution)/shard_map/all_to_all | solution.py:102
  94.5 0.2 convert_element_type.103
  94.7 1.0 %add_convert_fusion = bf16[2048,128]{1,0:T(8,128)(2,1)} fusion(f32[2048,128]{1,0:T(8,128)S(1)} %fusion.5, bf16[2048,64]{1,0:T(8,128)(2,1)S(1)} %convert_element_type.103), kind=kLoop, calls=%fused_computation.22 | loop fusion | flops 1048576 | bytes 1835008 | tf_op jit(solution)/shard_map/convert_element_type | solution.py:114
  (10 shorter events, 0.1 us)
Async XLA Ops:
  0.6 45.0 %copy-start = (bf16[2048,128]{1,0:T(8,128)(2,1)S(1)}, bf16[2048,128]{1,0:T(8,128)(2,1)}, u32[]{:S(2)}) copy-start(bf16[2048,128]{1,0:T(8,128)(2,1)} %param.11) | copy-start | bytes 1572868
  9.5 8.5 %copy-start.2 = (bf16[64,64]{1,0:T(8,128)(2,1)S(1)}, bf16[64,64]{1,0:T(8,128)(2,1)}, u32[]{:S(2)}) copy-start(bf16[64,64]{1,0:T(8,128)(2,1)} %param.12) | copy-start | bytes 24580
  9.5 8.6 %copy-start.3 = (bf16[64,64]{1,0:T(8,128)(2,1)S(1)}, bf16[64,64]{1,0:T(8,128)(2,1)}, u32[]{:S(2)}) copy-start(bf16[64,64]{1,0:T(8,128)(2,1)} %param.13) | copy-start | bytes 24580
  10.7 34.9 %all-to-all-start = ((bf16[32,130,128]{2,1,0:T(8,128)(2,1)}), bf16[32,130,128]{2,1,0:T(8,128)(2,1)S(1)}, u32[]{:S(2)}, u32[]{:S(2)}) async-start(bf16[32,130,128]{2,1,0:T(8,128)(2,1)} %pad_maximum_fusion), calls=%async_computation | async-start | bytes 2228224 | tf_op jit(solution)/shard_map/all_to_all | solution.py:70
  55.2 3.8 %copy-start.1 = (bf16[2048,128]{1,0:T(8,128)(2,1)S(1)}, bf16[2048,128]{1,0:T(8,128)(2,1)}, u32[]{:S(2)}) copy-start(bf16[2048,128]{1,0:T(8,128)(2,1)} %param.15) | copy-start | bytes 1572868
  55.2 3.8 %copy-start.4 = (bf16[128,128]{1,0:T(8,128)(2,1)S(1)}, bf16[128,128]{1,0:T(8,128)(2,1)}, u32[]{:S(2)}) copy-start(bf16[128,128]{1,0:T(8,128)(2,1)} %param.14) | copy-start | bytes 98308
  55.2 29.8 %all-to-all-start.1 = ((bf16[32,128,128]{2,1,0:T(8,128)(2,1)}), bf16[32,128,128]{2,1,0:T(8,128)(2,1)S(1)}, u32[]{:S(2)}, u32[]{:S(2)}) async-start(bf16[32,128,128]{2,1,0:T(8,128)(2,1)} %bitcast.12), calls=%async_computation.1 | async-start | bytes 2097152 | tf_op jit(solution)/shard_map/all_to_all | solution.py:93
  85.1 9.4 %all-to-all-start.2 = ((bf16[4,256,128]{2,1,0:T(8,128)(2,1)}), bf16[4,256,128]{2,1,0:T(8,128)(2,1)S(1)}, u32[]{:S(2)}, u32[]{:S(2)}) async-start(bf16[4,256,128]{2,1,0:T(8,128)(2,1)} %reshape.83), calls=%async_computation.2 | async-start | bytes 524288 | tf_op jit(solution)/shard_map/all_to_all | solution.py:102

commit v15 on v13

--- a/solution.py
+++ b/solution.py
@@ -70,15 +70,14 @@
     zero = jnp.zeros((node_count, node_count), bf16)
     wc = jnp.block([[zero, mortar_d.T], [zero, zero]])
     wm = jnp.block([[zero, -mortar_m.T], [zero, zero]])
-    wj = jnp.block([[zero, zero], [mortar_d, mortar_m]])
+    wb = jnp.block([[zero, zero], [mortar_d, zero]])
+    wg = jnp.concatenate([zero, mortar_m], axis=0)
     gap = jnp.dot(got_rows, wc, preferred_element_type=f32) + jnp.dot(
         mold_rows, wm, preferred_element_type=f32
     )
     flux = (got_rows.astype(f32) * mold_rows.astype(f32) * gap).astype(bf16)
-    projected = jnp.dot(flux, wj, preferred_element_type=f32)
-    lane = lax.broadcasted_iota(jnp.int32, (slots, row_width), 1)
-    answers = jnp.where(lane < node_count, projected, gap).astype(bf16)
-    gained = projected[:, node_count:].astype(bf16)
+    answers = (jnp.dot(flux, wb, preferred_element_type=f32) + gap).astype(bf16)
+    gained = jnp.dot(flux, wg, preferred_element_type=f32).astype(bf16)
 
     returned = lax.all_to_all(
         answers.reshape(devices, capacity, row_width), axes, 0, 0, tiled=True

time: 94.6 us -> 96.9 us (1.024)
  local copies, waits for them, and re-layouts: 10 us -> 12.5 us
  waiting for transfers between devices: 45.3 us -> 43.6 us
  matrix products: 20 us -> 21.5 us
    all_to_all x1, waiting for transfers between devices: 16.3 us -> 14.5 us  [local(): lax.all_to_all(answers.reshape(devices, capacity, row_width), axes, 0, 0,...]
    slice x1, local copies, waits for them, and re-layouts: 0.12 us -> 1.68 us  [local(): got_rows = got[:, :capacity, :].reshape(slots, row_width)]
    dot_general x1, matrix products: 0.28 us -> 1.26 us  [local(): heat = jnp.dot(volume, conduct, preferred_element_type=f32)]
  transfers between devices with their start and end apart: 3 -> 3, of which waited for: 3 -> 3; matrix products, arithmetic and copies ran while one was open for 15% -> 16% of each run, Pallas kernels for 0% -> 0%
where the time goes in v15:
time: 96.9 us; the launch traced here: 96.4 us
  waiting for transfers between devices  43.6 us (45%)
  matrix products  21.5 us (22%)
  starting transfers between devices  14.5 us (15%)
  local copies, waits for them, and re-layouts  12.5 us (13%)
  other arithmetic  3.31 us (3%)
    all_to_all x1, waiting for transfers between devices, local(): got = lax.all_to_all(send, axes, 0, 0, tiled=True)  27.5 us
    all_to_all x1, waiting for transfers between devices, local(): lax.all_to_all(answers.reshape(devices, capacity, row_width), axes, 0, 0,...  14.5 us
    dot_general x1, matrix products, local(): lax.dot_general(selector, gained, contract0, preferred_element_type=f32)  8.97 us
    all_to_all x1, starting transfers between devices, local(): got = lax.all_to_all(send, axes, 0, 0, tiled=True)  7.32 us
    dot_general x1, matrix products, local(): jnp.dot(selector, mold_faces, preferred_element_type=f32).astype(bf16)  6.42 us
    gather x1, local copies, waits for them, and re-layouts, local(): casting_out = jnp.take(returned, slot_index, axis=0, mode='clip')  4.31 us
    scatter x1, local copies, waits for them, and re-layouts, local(): send_rows = jnp.zeros((slots, row_width), bf16).at[slot_index].set(casting)  3.89 us
    all_to_all x1, starting transfers between devices, local(): lax.all_to_all(answers.reshape(devices, capacity, row_width), axes, 0, 0,...  3.8 us
  transfers between devices with their start and end apart: 3, of which 3 were waited for; matrix products, arithmetic and copies ran while one was open for 16% of the time, Pallas kernels for 0%

profile of v15, /device:TPU:0, one launch (start us, length us, event | category | flops | bytes accessed | tf_op | source)
XLA Modules:
  0.0 96.4 jit_solution(11737966799376835735)
XLA Ops:
  0.6 0.0 copy-start
  0.6 0.0 copy-start.9
  0.7 1.3 %fusion.10 = f32[1024]{0:T(1024)S(1)} fusion(s32[1024]{0:T(1024)} %bitcast.28), kind=kOutput, calls=%fused_computation.19 | convolution fusion | flops 68353024 | bytes 8192 | tf_op jit(solution)/shard_map/dot_general | solution.py:41
  2.0 0.7 fusion.43
  2.7 0.5 fusion.15
  3.2 0.9 convolution_convert_fusion.1
  4.1 0.0 copy-done.9
  4.1 3.9 %scatter_custom_fusion = bf16[4096,128]{1,0:T(8,128)(2,1)S(1)} fusion(s32[1024]{0:T(1024)S(1)} %bitcast.30, bf16[1024,128]{1,0:T(8,128)(2,1)} %param.8, bf16[]{:T(256)} %constant.38.clone.1), kind=kCustom, calls=%fused_computation.29 | custom fusion | bytes 1049088 | tf_op jit(solution)/shard_map/scatter | solution.py:56
  8.0 0.0 copy-start.6
  8.0 0.0 copy-start.8
  8.0 1.1 %pad_maximum_fusion = bf16[32,130,128]{2,1,0:T(8,128)(2,1)} fusion(bf16[32,2,128]{2,1,0:T(2,128)(2,1)S(1)} %convert_element_type.87, bf16[32,128,128]{2,1,0:T(8,128)(2,1)S(1)} %bitcast.22), kind=kLoop, calls=%fused_computation.20 | loop fusion | flops 2129920 | bytes 2129920 | tf_op jit(solution)/shard_map/concatenate | solution.py:57
  9.1 7.3 %all-to-all-start = ((bf16[32,130,128]{2,1,0:T(8,128)(2,1)}), bf16[32,130,128]{2,1,0:T(8,128)(2,1)S(1)}, u32[]{:S(2)}, u32[]{:S(2)}) async-start(bf16[32,130,128]{2,1,0:T(8,128)(2,1)} %pad_maximum_fusion), calls=%async_computation | async-start | bytes 2228224 | tf_op jit(solution)/shard_map/all_to_all | solution.py:60
  16.5 0.0 copy-done.6
  16.5 0.1 copy.12
  16.6 0.0 copy-done.8
  16.6 27.5 %all-to-all-done = bf16[32,130,128]{2,1,0:T(8,128)(2,1)S(1)} async-done(((bf16[32,130,128]{2,1,0:T(8,128)(2,1)}), bf16[32,130,128]{2,1,0:T(8,128)(2,1)S(1)}, u32[]{:S(2)}, u32[]{:S(2)}) %all-to-all-start) | async-done | bytes 1064992 | tf_op jit(solution)/shard_map/all_to_all | solution.py:60
  44.1 0.0 copy-start.2
  44.1 0.9 copy-done.2
  45.1 0.0 copy-done
  45.1 6.4 %fusion.5 = bf16[4096,128]{1,0:T(8,128)(2,1)S(1)} fusion(bf16[2048,128]{1,0:T(8,128)(2,1)S(1)} %copy-done, s32[4096]{0:T(1024)S(1)} %bitcast.25), kind=kOutput, calls=%fused_computation.10 | convolution fusion | flops 2156396544 | bytes 1589248 | tf_op jit(solution)/shard_map/dot_general | solution.py:68
  51.5 0.0 copy-start.3
  51.5 1.7 %slice.21 = bf16[32,128,128]{2,1,0:T(8,128)(2,1)S(1)} slice(bf16[32,130,128]{2,1,0:T(8,128)(2,1)} %copy-done.2), slice={[0:32], [0:128], [0:128]} | slice | bytes 2097152 | tf_op jit(solution)/shard_map/slice | solution.py:61
  53.2 0.1 concatenate.46
  53.3 0.5 fusion.24
  53.8 0.5 convolution_add_fusion.1
  54.3 0.0 copy-done.3
  54.3 0.0 copy-start.1
  54.3 1.7 %fusion.4 = bf16[4096,128]{1,0:T(8,128)(2,1)} fusion(f32[4096,128]{1,0:T(8,128)S(1)} %convolution_add_fusion.1, bf16[4096,128]{1,0:T(8,128)(2,1)S(1)} %fusion.5, bf16[4096,128]{1,0:T(8,128)(2,1)S(1)} %bitcast.18, bf16[64,64]{0,1:T(8,128)(2,1)S(1)} %copy.12, bf16[64,128]{0,1:T(8,128)(2,1)S(1)} %concatenate.46), kind=kOutput, calls=%fused_computation.9 | convolution fusion | flops 137986048 | bytes 5267456 | tf_op jit(solution)/shard_map/dot_general | solution.py:79
  56.0 0.0 copy-done.1
  56.0 0.0 copy-start.5
  56.0 0.0 copy-start.7
  56.0 3.8 %all-to-all-start.1 = ((bf16[32,128,128]{2,1,0:T(8,128)(2,1)}), bf16[32,128,128]{2,1,0:T(8,128)(2,1)S(1)}, u32[]{:S(2)}, u32[]{:S(2)}) async-start(bf16[32,128,128]{2,1,0:T(8,128)(2,1)} %bitcast.21), calls=%async_computation.1 | async-start | bytes 2097152 | tf_op jit(solution)/shard_map/all_to_all | solution.py:82
  59.8 0.0 copy-done.5
  59.8 0.0 copy-done.7
  59.8 1.3 %fusion.7 = f32[2048,128]{1,0:T(8,128)} fusion(bf16[2048,128]{1,0:T(8,128)(2,1)S(1)} %copy-done.5, bf16[128,128]{1,0:T(8,128)(2,1)S(1)} %copy-done.7), kind=kOutput, calls=%fused_computation.15 | convolution fusion | flops 67895296 | bytes 1605632 | tf_op jit(solution)/shard_map/dot_general | solution.py:98
  61.1 9.0 %fusion.8 = bf16[2048,64]{0,1:T(8,128)(2,1)S(1)} fusion(s32[4096]{0:T(1024)S(1)} %bitcast.26, f32[4096,128]{1,0:T(8,128)} %copy-done.1, bf16[4096,128]{1,0:T(8,128)(2,1)} %copy-done.3, bf16[4096,128]{1,0:T(8,128)(2,1)S(1)} %bitcast.19, bf16[64,64]{1,0:T(8,128)(2,1)S(1)} %copy-done.8), kind=kOutput, calls=%fused_computation.16 | convolution fusion | flops 1152253952 | bytes 4481024 | tf_op jit(solution)/shard_map/dot_general | solution.py:85
  70.0 0.3 copy.11
  70.3 0.0 copy-start.4
  70.3 1.0 reshape.59
  71.3 14.5 %all-to-all-done.1 = bf16[32,128,128]{2,1,0:T(8,128)(2,1)S(1)} async-done(((bf16[32,128,128]{2,1,0:T(8,128)(2,1)}), bf16[32,128,128]{2,1,0:T(8,128)(2,1)S(1)}, u32[]{:S(2)}, u32[]{:S(2)}) %all-to-all-start.1) | async-done | bytes 1048608 | tf_op jit(solution)/shard_map/all_to_all | solution.py:82
  85.8 3.4 %all-to-all-start.2 = ((bf16[4,256,128]{2,1,0:T(8,128)(2,1)}), bf16[4,256,128]{2,1,0:T(8,128)(2,1)S(1)}, u32[]{:S(2)}, u32[]{:S(2)}) async-start(bf16[4,256,128]{2,1,0:T(8,128)(2,1)} %reshape.59), calls=%async_computation.2 | async-start | bytes 524288 | tf_op jit(solution)/shard_map/all_to_all | solution.py:91
  89.2 4.3 %gather_fusion = bf16[1024,128]{1,0:T(8,128)(2,1)} fusion(bf16[4096,128]{1,0:T(8,128)(2,1)S(1)} %bitcast.20, s32[1024]{0:T(1024)S(1)} %broadcast_clamp_fusion), kind=kCustom, calls=%fused_computation | custom fusion | bytes 528384 | tf_op jit(solution)/shard_map/jit(_take)/gather | solution.py:89
  93.6 1.6 %all-to-all-done.2 = bf16[4,256,128]{2,1,0:T(8,128)(2,1)S(1)} async-done(((bf16[4,256,128]{2,1,0:T(8,128)(2,1)}), bf16[4,256,128]{2,1,0:T(8,128)(2,1)S(1)}, u32[]{:S(2)}, u32[]{:S(2)}) %all-to-all-start.2) | async-done | bytes 262176 | tf_op jit(solution)/shard_map/all_to_all | solution.py:91
  95.2 0.2 convert_element_type.98
  95.5 0.0 copy-done.4
  95.5 1.0 %add_convert_fusion = bf16[2048,128]{1,0:T(8,128)(2,1)} fusion(f32[2048,128]{1,0:T(8,128)S(1)} %copy-done.4, bf16[2048,64]{1,0:T(8,128)(2,1)S(1)} %convert_element_type.98), kind=kLoop, calls=%fused_computation.22 | loop fusion | flops 1048576 | bytes 1835008 | tf_op jit(solution)/shard_map/convert_element_type | solution.py:103
  (9 shorter events, 0.1 us)
Async XLA Ops:
  0.6 44.4 %copy-start = (bf16[2048,128]{1,0:T(8,128)(2,1)S(1)}, bf16[2048,128]{1,0:T(8,128)(2,1)}, u32[]{:S(2)}) copy-start(bf16[2048,128]{1,0:T(8,128)(2,1)} %param.11) | copy-start | bytes 1572868
  0.6 3.4 %copy-start.9 = (s32[1024,1]{0,1:T(1,128)S(1)}, s32[1024,1]{0,1:T(1,128)}, u32[]{:S(2)}) copy-start(s32[1024,1]{0,1:T(1,128)} %param.9) | copy-start | bytes 12292
  8.0 8.5 %copy-start.6 = (bf16[64,64]{1,0:T(8,128)(2,1)S(1)}, bf16[64,64]{1,0:T(8,128)(2,1)}, u32[]{:S(2)}) copy-start(bf16[64,64]{1,0:T(8,128)(2,1)} %param.12) | copy-start | bytes 24580
  8.0 8.6 %copy-start.8 = (bf16[64,64]{1,0:T(8,128)(2,1)S(1)}, bf16[64,64]{1,0:T(8,128)(2,1)}, u32[]{:S(2)}) copy-start(bf16[64,64]{1,0:T(8,128)(2,1)} %param.13) | copy-start | bytes 24580
  9.1 34.9 %all-to-all-start = ((bf16[32,130,128]{2,1,0:T(8,128)(2,1)}), bf16[32,130,128]{2,1,0:T(8,128)(2,1)S(1)}, u32[]{:S(2)}, u32[]{:S(2)}) async-start(bf16[32,130,128]{2,1,0:T(8,128)(2,1)} %pad_maximum_fusion), calls=%async_computation | async-start | bytes 2228224 | tf_op jit(solution)/shard_map/all_to_all | solution.py:60
  44.1 1.0 %copy-start.2 = (bf16[32,130,128]{2,1,0:T(8,128)(2,1)}, bf16[32,130,128]{2,1,0:T(8,128)(2,1)S(1)}, u32[]{:S(2)}) copy-start(bf16[32,130,128]{2,1,0:T(8,128)(2,1)S(1)} %all-to-all-done) | copy-start | bytes 3194884
  51.5 2.8 %copy-start.3 = (bf16[4096,128]{1,0:T(8,128)(2,1)}, bf16[4096,128]{1,0:T(8,128)(2,1)S(1)}, u32[]{:S(2)}) copy-start(bf16[4096,128]{1,0:T(8,128)(2,1)S(1)} %fusion.5) | copy-start | bytes 3145732
  54.3 1.7 %copy-start.1 = (f32[4096,128]{1,0:T(8,128)}, f32[4096,128]{1,0:T(8,128)S(1)}, u32[]{:S(2)}) copy-start(f32[4096,128]{1,0:T(8,128)S(1)} %convolution_add_fusion.1) | copy-start | bytes 6291460
  56.0 3.8 %copy-start.5 = (bf16[2048,128]{1,0:T(8,128)(2,1)S(1)}, bf16[2048,128]{1,0:T(8,128)(2,1)}, u32[]{:S(2)}) copy-start(bf16[2048,128]{1,0:T(8,128)(2,1)} %param.15) | copy-start | bytes 1572868
  56.0 3.8 %copy-start.7 = (bf16[128,128]{1,0:T(8,128)(2,1)S(1)}, bf16[128,128]{1,0:T(8,128)(2,1)}, u32[]{:S(2)}) copy-start(bf16[128,128]{1,0:T(8,128)(2,1)} %param.14) | copy-start | bytes 98308
  56.0 29.8 %all-to-all-start.1 = ((bf16[32,128,128]{2,1,0:T(8,128)(2,1)}), bf16[32,128,128]{2,1,0:T(8,128)(2,1)S(1)}, u32[]{:S(2)}, u32[]{:S(2)}) async-start(bf16[32,128,128]{2,1,0:T(8,128)(2,1)} %bitcast.21), calls=%async_computation.1 | async-start | bytes 2097152 | tf_op jit(solution)/shard_map/all_to_all | solution.py:82
  70.3 25.1 %copy-start.4 = (f32[2048,128]{1,0:T(8,128)S(1)}, f32[2048,128]{1,0:T(8,128)}, u32[]{:S(2)}) copy-start(f32[2048,128]{1,0:T(8,128)} %fusion.7) | copy-start | bytes 3145732
  85.8 9.4 %all-to-all-start.2 = ((bf16[4,256,128]{2,1,0:T(8,128)(2,1)}), bf16[4,256,128]{2,1,0:T(8,128)(2,1)S(1)}, u32[]{:S(2)}, u32[]{:S(2)}) async-start(bf16[4,256,128]{2,1,0:T(8,128)(2,1)} %reshape.59), calls=%async_computation.2 | async-start | bytes 524288 | tf_op jit(solution)/shard_map/all_to_all | solution.py:91

commit v16 on v13

--- a/solution.py
+++ b/solution.py
@@ -53,7 +53,8 @@
     id_flat = jnp.pad(id_flat, ((0, 0), (0, id_height * row_width - id_count)))
     id_rows = id_flat.reshape(devices, id_height, row_width)
 
-    send_rows = jnp.zeros((slots, row_width), bf16).at[slot_index].set(casting)
+    slot_hot = (lax.broadcasted_iota(jnp.int32, (slots, seg_rows), 0) == slot_index[None, :]).astype(bf16)
+    send_rows = jnp.dot(slot_hot, casting, preferred_element_type=f32).astype(bf16)
     send = jnp.concatenate(
         [send_rows.reshape(devices, capacity, row_width), id_rows.astype(bf16)], axis=1
     )

time: 94.6 us -> 94.4 us (level)
  local copies, waits for them, and re-layouts: 10 us -> 6.16 us
  matrix products: 20 us -> 23 us
    scatter x1 -> x0, local copies, waits for them, and re-layouts: 3.89 us -> none  [local(): send_rows = jnp.zeros((slots, row_width), bf16).at[slot_index].set(casting)]
    dot_general x0 -> x1, matrix products: none -> 2.95 us  [local(): jnp.dot(slot_hot, casting, preferred_element_type=f32).astype(bf16)]
where the time goes in v16:
time: 94.4 us; the launch traced here: 93.9 us
  waiting for transfers between devices  45.3 us (48%)
  matrix products  23 us (24%)
  starting transfers between devices  14.5 us (15%)
  local copies, waits for them, and re-layouts  6.16 us (7%)
  other arithmetic  4.01 us (4%)
    all_to_all x1, waiting for transfers between devices, local(): got = lax.all_to_all(send, axes, 0, 0, tiled=True)  27.4 us
    all_to_all x1, waiting for transfers between devices, local(): lax.all_to_all(answers.reshape(devices, capacity, row_width), axes, 0, 0,...  16.3 us
    dot_general x1, matrix products, local(): lax.dot_general(selector, gained, contract0, preferred_element_type=f32)  8.16 us
    all_to_all x1, starting transfers between devices, local(): got = lax.all_to_all(send, axes, 0, 0, tiled=True)  7.32 us
    dot_general x1, matrix products, local(): jnp.dot(selector, mold_faces, preferred_element_type=f32).astype(bf16)  6.43 us
    gather x1, local copies, waits for them, and re-layouts, local(): casting_out = jnp.take(returned, slot_index, axis=0, mode='clip')  4.31 us
    all_to_all x1, starting transfers between devices, local(): lax.all_to_all(answers.reshape(devices, capacity, row_width), axes, 0, 0,...  3.81 us
    all_to_all x1, starting transfers between devices, local(): lax.all_to_all(face_totals, 'vol', split_axis=0, concat_axis=0, tiled=True)  3.41 us
  transfers between devices with their start and end apart: 3, of which 3 were waited for; matrix products, arithmetic and copies ran while one was open for 15% of the time, Pallas kernels for 0%

profile of v16, /device:TPU:0, one launch (start us, length us, event | category | flops | bytes accessed | tf_op | source)
XLA Modules:
  0.0 93.9 jit_solution(17618541798585303577)
XLA Ops:
  0.6 0.0 copy-start
  0.6 0.0 copy-start.6
  0.7 1.3 %fusion.12 = f32[1024]{0:T(1024)S(1)} fusion(s32[1024]{0:T(1024)} %bitcast.25), kind=kOutput, calls=%fused_computation.21 | convolution fusion | flops 68353024 | bytes 8192 | tf_op jit(solution)/shard_map/dot_general | solution.py:41
  2.0 0.7 multiply_add_fusion.1
  2.7 0.7 fusion.40
  3.4 0.5 fusion.18
  3.8 0.9 convolution_convert_fusion
  4.8 0.0 copy-done.6
  4.8 2.9 %fusion.6 = bf16[4096,128]{1,0:T(8,128)(2,1)S(1)} fusion(bf16[1024,128]{1,0:T(8,128)(2,1)S(1)} %copy-done.6, s32[1024]{0:T(1024)S(1)} %multiply_add_fusion.1), kind=kOutput, calls=%fused_computation.10 | convolution fusion | flops 1078460416 | bytes 1314816 | tf_op jit(solution)/shard_map/dot_general | solution.py:57
  7.7 0.0 copy-start.2
  7.7 0.0 copy-start.3
  7.7 1.1 %pad_maximum_fusion = bf16[32,130,128]{2,1,0:T(8,128)(2,1)} fusion(bf16[32,2,128]{2,1,0:T(2,128)(2,1)S(1)} %convert_element_type.92, bf16[32,128,128]{2,1,0:T(8,128)(2,1)S(1)} %bitcast.20), kind=kLoop, calls=%fused_computation.22 | loop fusion | flops 2129920 | bytes 2129920 | tf_op jit(solution)/shard_map/concatenate | solution.py:58
  8.8 7.3 %all-to-all-start = ((bf16[32,130,128]{2,1,0:T(8,128)(2,1)}), bf16[32,130,128]{2,1,0:T(8,128)(2,1)S(1)}, u32[]{:S(2)}, u32[]{:S(2)}) async-start(bf16[32,130,128]{2,1,0:T(8,128)(2,1)} %pad_maximum_fusion), calls=%async_computation | async-start | bytes 2228224 | tf_op jit(solution)/shard_map/all_to_all | solution.py:61
  16.2 0.0 copy-done.2
  16.2 0.1 copy.12
  16.3 0.0 copy-done.3
  16.3 0.1 copy.13
  16.4 27.4 %all-to-all-done = bf16[32,130,128]{2,1,0:T(8,128)(2,1)S(1)} async-done(((bf16[32,130,128]{2,1,0:T(8,128)(2,1)}), bf16[32,130,128]{2,1,0:T(8,128)(2,1)S(1)}, u32[]{:S(2)}, u32[]{:S(2)}) %all-to-all-start) | async-done | bytes 1064992 | tf_op jit(solution)/shard_map/all_to_all | solution.py:61
  43.8 0.0 copy-done
  43.9 6.4 %fusion.7 = bf16[4096,128]{1,0:T(8,128)(2,1)S(1)} fusion(bf16[2048,128]{1,0:T(8,128)(2,1)S(1)} %copy-done, s32[4096]{0:T(1024)S(1)} %bitcast.23), kind=kOutput, calls=%fused_computation.11 | convolution fusion | flops 2156396544 | bytes 1589248 | tf_op jit(solution)/shard_map/dot_general | solution.py:69
  50.3 0.1 slice.26
  50.4 0.5 fusion.24
  50.9 0.5 convolution_add_fusion
  51.4 2.0 %select_convert_fusion = (bf16[4096,128]{1,0:T(8,128)(2,1)}, bf16[4096,128]{1,0:T(8,128)(2,1)}) fusion(f32[4096,128]{1,0:T(8,128)S(1)} %convolution_add_fusion, pred[128]{0:T(512)(128)(4,1)S(1)} %iota_compare_fusion.22, bf16[64,64]{1,0:T(8,128)(2,1)S(1)} %copy-done.3, bf16[64,64]{1,0:T(8,128)(2,1)S(1)} %copy-done.2, bf16[64,128]{1,0:T(8,128)(2,1)S(1)} %concatenate.43, ...), kind=kOutput, calls=%fused_computation.18 | convolution fusion | flops 137461760 | bytes 6324352 | tf_op jit(solution)/shard_map/dot_general | solution.py:79
  53.4 0.0 copy-start.5
  53.4 0.0 copy-start.1
  53.4 0.0 copy-start.4
  53.4 3.8 %all-to-all-start.1 = ((bf16[32,128,128]{2,1,0:T(8,128)(2,1)}), bf16[32,128,128]{2,1,0:T(8,128)(2,1)S(1)}, u32[]{:S(2)}, u32[]{:S(2)}) async-start(bf16[32,128,128]{2,1,0:T(8,128)(2,1)} %bitcast.6), calls=%async_computation.1 | async-start | bytes 2097152 | tf_op jit(solution)/shard_map/all_to_all | solution.py:84
  57.2 0.0 copy-done.5
  57.3 0.0 copy-done.1
  57.3 0.0 copy-done.4
  57.3 0.3 fusion.9
  57.6 8.2 %fusion.10 = bf16[2048,64]{0,1:T(8,128)(2,1)S(1)} fusion(s32[4096]{0:T(1024)S(1)} %bitcast.24, bf16[4096,128]{1,0:T(8,128)(2,1)} %get-tuple-element.15), kind=kOutput, calls=%fused_computation.16 | convolution fusion | flops 1082261504 | bytes 1327104 | tf_op jit(solution)/shard_map/dot_general | solution.py:87
  65.7 0.3 copy.14
  66.0 1.0 %reshape.67 = bf16[4,256,128]{2,1,0:T(8,128)(2,1)} reshape(bf16[2048,64]{1,0:T(8,128)(2,1)S(1)} %copy.14) | data formatting | bytes 524288 | tf_op jit(solution)/shard_map/reshape | solution.py:89
  67.0 16.3 %all-to-all-done.1 = bf16[32,128,128]{2,1,0:T(8,128)(2,1)S(1)} async-done(((bf16[32,128,128]{2,1,0:T(8,128)(2,1)}), bf16[32,128,128]{2,1,0:T(8,128)(2,1)S(1)}, u32[]{:S(2)}, u32[]{:S(2)}) %all-to-all-start.1) | async-done | bytes 1048608 | tf_op jit(solution)/shard_map/all_to_all | solution.py:84
  83.3 3.4 %all-to-all-start.2 = ((bf16[4,256,128]{2,1,0:T(8,128)(2,1)}), bf16[4,256,128]{2,1,0:T(8,128)(2,1)S(1)}, u32[]{:S(2)}, u32[]{:S(2)}) async-start(bf16[4,256,128]{2,1,0:T(8,128)(2,1)} %reshape.67), calls=%async_computation.2 | async-start | bytes 524288 | tf_op jit(solution)/shard_map/all_to_all | solution.py:93
  86.7 4.3 %gather_fusion = bf16[1024,128]{1,0:T(8,128)(2,1)} fusion(bf16[4096,128]{1,0:T(8,128)(2,1)S(1)} %bitcast.19, s32[1024]{0:T(1024)S(1)} %broadcast_clamp_fusion), kind=kCustom, calls=%fused_computation | custom fusion | bytes 528384 | tf_op jit(solution)/shard_map/jit(_take)/gather | solution.py:91
  91.0 1.6 %all-to-all-done.2 = bf16[4,256,128]{2,1,0:T(8,128)(2,1)S(1)} async-done(((bf16[4,256,128]{2,1,0:T(8,128)(2,1)}), bf16[4,256,128]{2,1,0:T(8,128)(2,1)S(1)}, u32[]{:S(2)}, u32[]{:S(2)}) %all-to-all-start.2) | async-done | bytes 262176 | tf_op jit(solution)/shard_map/all_to_all | solution.py:93
  92.6 0.2 convert_element_type.103
  92.9 1.0 %add_convert_fusion = bf16[2048,128]{1,0:T(8,128)(2,1)} fusion(f32[2048,128]{1,0:T(8,128)S(1)} %fusion.9, bf16[2048,64]{1,0:T(8,128)(2,1)S(1)} %convert_element_type.103), kind=kLoop, calls=%fused_computation.25 | loop fusion | flops 1048576 | bytes 1835008 | tf_op jit(solution)/shard_map/convert_element_type | solution.py:105
  (11 shorter events, 0.1 us)
Async XLA Ops:
  0.6 43.2 %copy-start = (bf16[2048,128]{1,0:T(8,128)(2,1)S(1)}, bf16[2048,128]{1,0:T(8,128)(2,1)}, u32[]{:S(2)}) copy-start(bf16[2048,128]{1,0:T(8,128)(2,1)} %param.11) | copy-start | bytes 1572868
  0.6 4.1 %copy-start.6 = (bf16[1024,128]{1,0:T(8,128)(2,1)S(1)}, bf16[1024,128]{1,0:T(8,128)(2,1)}, u32[]{:S(2)}) copy-start(bf16[1024,128]{1,0:T(8,128)(2,1)} %param.8) | copy-start | bytes 786436
  7.7 8.5 %copy-start.2 = (bf16[64,64]{1,0:T(8,128)(2,1)S(1)}, bf16[64,64]{1,0:T(8,128)(2,1)}, u32[]{:S(2)}) copy-start(bf16[64,64]{1,0:T(8,128)(2,1)} %param.12) | copy-start | bytes 24580
  7.7 8.6 %copy-start.3 = (bf16[64,64]{1,0:T(8,128)(2,1)S(1)}, bf16[64,64]{1,0:T(8,128)(2,1)}, u32[]{:S(2)}) copy-start(bf16[64,64]{1,0:T(8,128)(2,1)} %param.13) | copy-start | bytes 24580
  8.8 34.9 %all-to-all-start = ((bf16[32,130,128]{2,1,0:T(8,128)(2,1)}), bf16[32,130,128]{2,1,0:T(8,128)(2,1)S(1)}, u32[]{:S(2)}, u32[]{:S(2)}) async-start(bf16[32,130,128]{2,1,0:T(8,128)(2,1)} %pad_maximum_fusion), calls=%async_computation | async-start | bytes 2228224 | tf_op jit(solution)/shard_map/all_to_all | solution.py:61
  53.4 3.8 %copy-start.5 = (s32[1024,1]{0,1:T(1,128)S(1)}, s32[1024,1]{0,1:T(1,128)}, u32[]{:S(2)}) copy-start(s32[1024,1]{0,1:T(1,128)} %param.9) | copy-start | bytes 12292
  53.4 3.8 %copy-start.1 = (bf16[2048,128]{1,0:T(8,128)(2,1)S(1)}, bf16[2048,128]{1,0:T(8,128)(2,1)}, u32[]{:S(2)}) copy-start(bf16[2048,128]{1,0:T(8,128)(2,1)} %param.15) | copy-start | bytes 1572868
  53.4 3.9 %copy-start.4 = (bf16[128,128]{1,0:T(8,128)(2,1)S(1)}, bf16[128,128]{1,0:T(8,128)(2,1)}, u32[]{:S(2)}) copy-start(bf16[128,128]{1,0:T(8,128)(2,1)} %param.14) | copy-start | bytes 98308
  53.4 29.8 %all-to-all-start.1 = ((bf16[32,128,128]{2,1,0:T(8,128)(2,1)}), bf16[32,128,128]{2,1,0:T(8,128)(2,1)S(1)}, u32[]{:S(2)}, u32[]{:S(2)}) async-start(bf16[32,128,128]{2,1,0:T(8,128)(2,1)} %bitcast.6), calls=%async_computation.1 | async-start | bytes 2097152 | tf_op jit(solution)/shard_map/all_to_all | solution.py:84
  83.3 9.4 %all-to-all-start.2 = ((bf16[4,256,128]{2,1,0:T(8,128)(2,1)}), bf16[4,256,128]{2,1,0:T(8,128)(2,1)S(1)}, u32[]{:S(2)}, u32[]{:S(2)}) async-start(bf16[4,256,128]{2,1,0:T(8,128)(2,1)} %reshape.67), calls=%async_computation.2 | async-start | bytes 524288 | tf_op jit(solution)/shard_map/all_to_all | solution.py:93

commit v17 on v13

--- a/solution.py
+++ b/solution.py
@@ -64,8 +64,10 @@
     got_ids = (got_code[:, 0, :] * 64.0 + got_code[:, 1, :]).astype(jnp.int32).reshape(slots) - 1
 
     face_range = jnp.arange(face_rows, dtype=jnp.int32)
-    selector = (got_ids[:, None] == face_range[None, :]).astype(bf16)
-    mold_rows = jnp.dot(selector, mold_faces, preferred_element_type=f32).astype(bf16)
+    selector_t = (face_range[:, None] == got_ids[None, :]).astype(bf16)
+    mold_rows = lax.dot_general(
+        selector_t, mold_faces, contract0, preferred_element_type=f32
+    ).astype(bf16)
 
     zero = jnp.zeros((node_count, node_count), bf16)
     wc = jnp.block([[zero, mortar_d.T], [zero, zero]])
@@ -83,7 +85,7 @@
     returned = lax.all_to_all(
         answers.reshape(devices, capacity, row_width), axes, 0, 0, tiled=True
     ).reshape(slots, row_width)
-    totals = lax.dot_general(selector, gained, contract0, preferred_element_type=f32)
+    totals = jnp.dot(selector_t, gained, preferred_element_type=f32)
     quarter = face_rows // vol_count
     face_totals = totals.astype(bf16).reshape(vol_count, quarter * node_count // row_width, row_width)
     face_totals, returned = lax.optimization_barrier((face_totals, returned))

time: 94.6 us -> 97 us (1.025)
  matrix products: 20 us -> 22.4 us
    dot_general x2, matrix products: 14.6 us -> 16.9 us  [the longest x1 8.85 us: local(): lax.dot_general(selector_t, mold_faces, contract0, preferred_element_type...]
where the time goes in v17:
time: 97 us; the launch traced here: 96.5 us
  waiting for transfers between devices  45.2 us (47%)
  matrix products  22.4 us (23%)
  starting transfers between devices  14.7 us (15%)
  local copies, waits for them, and re-layouts  10 us (10%)
  other arithmetic  3.31 us (3%)
    all_to_all x1, waiting for transfers between devices, local(): got = lax.all_to_all(send, axes, 0, 0, tiled=True)  27.2 us
    all_to_all x1, waiting for transfers between devices, local(): lax.all_to_all(answers.reshape(devices, capacity, row_width), axes, 0, 0,...  16.4 us
    dot_general x1, matrix products, local(): lax.dot_general(selector_t, mold_faces, contract0, preferred_element_type...  8.85 us
    dot_general x1, matrix products, local(): totals = jnp.dot(selector_t, gained, preferred_element_type=f32)  8.08 us
    all_to_all x1, starting transfers between devices, local(): got = lax.all_to_all(send, axes, 0, 0, tiled=True)  7.5 us
    gather x1, local copies, waits for them, and re-layouts, local(): casting_out = jnp.take(returned, slot_index, axis=0, mode='clip')  4.31 us
    scatter x1, local copies, waits for them, and re-layouts, local(): send_rows = jnp.zeros((slots, row_width), bf16).at[slot_index].set(casting)  3.89 us
    all_to_all x1, starting transfers between devices, local(): lax.all_to_all(answers.reshape(devices, capacity, row_width), axes, 0, 0,...  3.82 us
  transfers between devices with their start and end apart: 3, of which 3 were waited for; matrix products, arithmetic and copies ran while one was open for 15% of the time, Pallas kernels for 0%

profile of v17, /device:TPU:0, one launch (start us, length us, event | category | flops | bytes accessed | tf_op | source)
XLA Modules:
  0.0 96.5 jit_solution(17760124442562683243)
XLA Ops:
  0.6 0.0 copy-start
  0.6 0.0 copy-start.5
  0.7 1.3 %fusion.9 = f32[1024]{0:T(1024)S(1)} fusion(s32[1024]{0:T(1024)} %bitcast.26), kind=kOutput, calls=%fused_computation.18 | convolution fusion | flops 68353024 | bytes 8192 | tf_op jit(solution)/shard_map/dot_general | solution.py:41
  2.0 0.7 fusion.39
  2.7 0.5 fusion.15
  3.2 0.9 convolution_convert_fusion
  4.1 0.0 copy-done.5
  4.1 3.9 %scatter_custom_fusion = bf16[4096,128]{1,0:T(8,128)(2,1)S(1)} fusion(s32[1024]{0:T(1024)S(1)} %bitcast.28, bf16[1024,128]{1,0:T(8,128)(2,1)} %param.8, bf16[]{:T(256)} %constant.39.clone.1), kind=kCustom, calls=%fused_computation.29 | custom fusion | bytes 1049088 | tf_op jit(solution)/shard_map/scatter | solution.py:56
  8.0 0.0 copy-start.2
  8.0 0.0 copy-start.3
  8.0 1.1 %pad_maximum_fusion = bf16[32,130,128]{2,1,0:T(8,128)(2,1)} fusion(bf16[32,2,128]{2,1,0:T(2,128)(2,1)S(1)} %convert_element_type.85, bf16[32,128,128]{2,1,0:T(8,128)(2,1)S(1)} %bitcast.20), kind=kLoop, calls=%fused_computation.19 | loop fusion | flops 2129920 | bytes 2129920 | tf_op jit(solution)/shard_map/concatenate | solution.py:57
  9.1 7.5 %all-to-all-start = ((bf16[32,130,128]{2,1,0:T(8,128)(2,1)}), bf16[32,130,128]{2,1,0:T(8,128)(2,1)S(1)}, u32[]{:S(2)}, u32[]{:S(2)}) async-start(bf16[32,130,128]{2,1,0:T(8,128)(2,1)} %pad_maximum_fusion), calls=%async_computation | async-start | bytes 2228224 | tf_op jit(solution)/shard_map/all_to_all | solution.py:60
  16.7 0.0 copy-done.2
  16.7 0.1 copy.12
  16.8 0.0 copy-done.3
  16.8 0.1 copy.13
  16.9 27.2 %all-to-all-done = bf16[32,130,128]{2,1,0:T(8,128)(2,1)S(1)} async-done(((bf16[32,130,128]{2,1,0:T(8,128)(2,1)}), bf16[32,130,128]{2,1,0:T(8,128)(2,1)S(1)}, u32[]{:S(2)}, u32[]{:S(2)}) %all-to-all-start) | async-done | bytes 1064992 | tf_op jit(solution)/shard_map/all_to_all | solution.py:60
  44.1 0.0 copy-done
  44.1 8.9 %fusion.4 = bf16[4096,128]{1,0:T(8,128)(2,1)S(1)} fusion(bf16[2048,128]{1,0:T(8,128)(2,1)S(1)} %copy-done, s32[4096]{0:T(1024)S(1)} %bitcast.23), kind=kOutput, calls=%fused_computation.8 | convolution fusion | flops 2156396544 | bytes 1589248 | tf_op jit(solution)/shard_map/dot_general | solution.py:68
  53.0 0.1 slice.26
  53.1 0.5 fusion.23
  53.6 0.5 convolution_add_fusion
  54.1 2.0 %select_convert_fusion = (bf16[4096,128]{1,0:T(8,128)(2,1)}, bf16[4096,128]{1,0:T(8,128)(2,1)}) fusion(f32[4096,128]{1,0:T(8,128)S(1)} %convolution_add_fusion, pred[128]{0:T(512)(128)(4,1)S(1)} %iota_compare_fusion.18, bf16[64,64]{1,0:T(8,128)(2,1)S(1)} %copy-done.3, bf16[64,64]{1,0:T(8,128)(2,1)S(1)} %copy-done.2, bf16[64,128]{1,0:T(8,128)(2,1)S(1)} %concatenate.43, ...), kind=kOutput, calls=%fused_computation.15 | convolution fusion | flops 137461760 | bytes 6324352 | tf_op jit(solution)/shard_map/dot_general | solution.py:80
  56.1 0.0 copy-start.1
  56.1 0.0 copy-start.4
  56.1 3.8 %all-to-all-start.1 = ((bf16[32,128,128]{2,1,0:T(8,128)(2,1)}), bf16[32,128,128]{2,1,0:T(8,128)(2,1)S(1)}, u32[]{:S(2)}, u32[]{:S(2)}) async-start(bf16[32,128,128]{2,1,0:T(8,128)(2,1)} %bitcast.8), calls=%async_computation.1 | async-start | bytes 2097152 | tf_op jit(solution)/shard_map/all_to_all | solution.py:85
  59.9 0.0 copy-done.1
  60.0 0.0 copy-done.4
  60.0 0.3 fusion.6
  60.3 8.1 %fusion.7 = bf16[2048,64]{0,1:T(8,128)(2,1)S(1)} fusion(s32[4096]{0:T(1024)S(1)} %bitcast.24, bf16[4096,128]{1,0:T(8,128)(2,1)} %get-tuple-element.17), kind=kOutput, calls=%fused_computation.13 | convolution fusion | flops 1082261504 | bytes 1327104 | tf_op jit(solution)/shard_map/dot_general | solution.py:88
  68.3 0.3 copy.14
  68.6 1.0 reshape.59
  69.6 16.4 %all-to-all-done.1 = bf16[32,128,128]{2,1,0:T(8,128)(2,1)S(1)} async-done(((bf16[32,128,128]{2,1,0:T(8,128)(2,1)}), bf16[32,128,128]{2,1,0:T(8,128)(2,1)S(1)}, u32[]{:S(2)}, u32[]{:S(2)}) %all-to-all-start.1) | async-done | bytes 1048608 | tf_op jit(solution)/shard_map/all_to_all | solution.py:85
  85.9 3.4 %all-to-all-start.2 = ((bf16[4,256,128]{2,1,0:T(8,128)(2,1)}), bf16[4,256,128]{2,1,0:T(8,128)(2,1)S(1)}, u32[]{:S(2)}, u32[]{:S(2)}) async-start(bf16[4,256,128]{2,1,0:T(8,128)(2,1)} %reshape.59), calls=%async_computation.2 | async-start | bytes 524288 | tf_op jit(solution)/shard_map/all_to_all | solution.py:94
  89.4 4.3 %gather_fusion = bf16[1024,128]{1,0:T(8,128)(2,1)} fusion(bf16[4096,128]{1,0:T(8,128)(2,1)S(1)} %bitcast.19, s32[1024]{0:T(1024)S(1)} %broadcast_clamp_fusion), kind=kCustom, calls=%fused_computation | custom fusion | bytes 528384 | tf_op jit(solution)/shard_map/jit(_take)/gather | solution.py:92
  93.7 1.6 %all-to-all-done.2 = bf16[4,256,128]{2,1,0:T(8,128)(2,1)S(1)} async-done(((bf16[4,256,128]{2,1,0:T(8,128)(2,1)}), bf16[4,256,128]{2,1,0:T(8,128)(2,1)S(1)}, u32[]{:S(2)}, u32[]{:S(2)}) %all-to-all-start.2) | async-done | bytes 262176 | tf_op jit(solution)/shard_map/all_to_all | solution.py:94
  95.3 0.2 convert_element_type.95
  95.6 1.0 %add_convert_fusion = bf16[2048,128]{1,0:T(8,128)(2,1)} fusion(f32[2048,128]{1,0:T(8,128)S(1)} %fusion.6, bf16[2048,64]{1,0:T(8,128)(2,1)S(1)} %convert_element_type.95), kind=kLoop, calls=%fused_computation.22 | loop fusion | flops 1048576 | bytes 1835008 | tf_op jit(solution)/shard_map/convert_element_type | solution.py:106
  (11 shorter events, 0.1 us)
Async XLA Ops:
  0.6 43.5 %copy-start = (bf16[2048,128]{1,0:T(8,128)(2,1)S(1)}, bf16[2048,128]{1,0:T(8,128)(2,1)}, u32[]{:S(2)}) copy-start(bf16[2048,128]{1,0:T(8,128)(2,1)} %param.11) | copy-start | bytes 1572868
  0.6 3.4 %copy-start.5 = (s32[1024,1]{0,1:T(1,128)S(1)}, s32[1024,1]{0,1:T(1,128)}, u32[]{:S(2)}) copy-start(s32[1024,1]{0,1:T(1,128)} %param.9) | copy-start | bytes 12292
  8.0 8.7 %copy-start.2 = (bf16[64,64]{1,0:T(8,128)(2,1)S(1)}, bf16[64,64]{1,0:T(8,128)(2,1)}, u32[]{:S(2)}) copy-start(bf16[64,64]{1,0:T(8,128)(2,1)} %param.12) | copy-start | bytes 24580
  8.0 8.7 %copy-start.3 = (bf16[64,64]{1,0:T(8,128)(2,1)S(1)}, bf16[64,64]{1,0:T(8,128)(2,1)}, u32[]{:S(2)}) copy-start(bf16[64,64]{1,0:T(8,128)(2,1)} %param.13) | copy-start | bytes 24580
  9.1 34.9 %all-to-all-start = ((bf16[32,130,128]{2,1,0:T(8,128)(2,1)}), bf16[32,130,128]{2,1,0:T(8,128)(2,1)S(1)}, u32[]{:S(2)}, u32[]{:S(2)}) async-start(bf16[32,130,128]{2,1,0:T(8,128)(2,1)} %pad_maximum_fusion), calls=%async_computation | async-start | bytes 2228224 | tf_op jit(solution)/shard_map/all_to_all | solution.py:60
  56.1 3.8 %copy-start.1 = (bf16[2048,128]{1,0:T(8,128)(2,1)S(1)}, bf16[2048,128]{1,0:T(8,128)(2,1)}, u32[]{:S(2)}) copy-start(bf16[2048,128]{1,0:T(8,128)(2,1)} %param.15) | copy-start | bytes 1572868
  56.1 3.8 %copy-start.4 = (bf16[128,128]{1,0:T(8,128)(2,1)S(1)}, bf16[128,128]{1,0:T(8,128)(2,1)}, u32[]{:S(2)}) copy-start(bf16[128,128]{1,0:T(8,128)(2,1)} %param.14) | copy-start | bytes 98308
  56.1 29.8 %all-to-all-start.1 = ((bf16[32,128,128]{2,1,0:T(8,128)(2,1)}), bf16[32,128,128]{2,1,0:T(8,128)(2,1)S(1)}, u32[]{:S(2)}, u32[]{:S(2)}) async-start(bf16[32,128,128]{2,1,0:T(8,128)(2,1)} %bitcast.8), calls=%async_computation.1 | async-start | bytes 2097152 | tf_op jit(solution)/shard_map/all_to_all | solution.py:85
  85.9 9.4 %all-to-all-start.2 = ((bf16[4,256,128]{2,1,0:T(8,128)(2,1)}), bf16[4,256,128]{2,1,0:T(8,128)(2,1)S(1)}, u32[]{:S(2)}, u32[]{:S(2)}) async-start(bf16[4,256,128]{2,1,0:T(8,128)(2,1)} %reshape.59), calls=%async_computation.2 | async-start | bytes 524288 | tf_op jit(solution)/shard_map/all_to_all | solution.py:94

commit v18 on v13

--- a/solution.py
+++ b/solution.py
@@ -87,7 +87,7 @@
     quarter = face_rows // vol_count
     face_totals = totals.astype(bf16).reshape(vol_count, quarter * node_count // row_width, row_width)
     face_totals, returned = lax.optimization_barrier((face_totals, returned))
-    casting_out = jnp.take(returned, slot_index, axis=0, mode="clip")
+    casting_out = returned.at[slot_index].get(mode="promise_in_bounds")
 
     relaid = lax.all_to_all(
         face_totals,

time: 94.6 us -> 94.6 us (level)
  no operation moved by 1% of the time
where the time goes in v18:
time: 94.6 us; the launch traced here: 94.1 us
  waiting for transfers between devices  45.3 us (48%)
  matrix products  20 us (21%)
  starting transfers between devices  14.5 us (15%)
  local copies, waits for them, and re-layouts  10 us (11%)
  other arithmetic  3.31 us (3%)
    all_to_all x1, waiting for transfers between devices, local(): got = lax.all_to_all(send, axes, 0, 0, tiled=True)  27.4 us
    all_to_all x1, waiting for transfers between devices, local(): lax.all_to_all(answers.reshape(devices, capacity, row_width), axes, 0, 0,...  16.3 us
    dot_general x1, matrix products, local(): lax.dot_general(selector, gained, contract0, preferred_element_type=f32)  8.16 us
    all_to_all x1, starting transfers between devices, local(): got = lax.all_to_all(send, axes, 0, 0, tiled=True)  7.32 us
    dot_general x1, matrix products, local(): jnp.dot(selector, mold_faces, preferred_element_type=f32).astype(bf16)  6.43 us
    gather x1, local copies, waits for them, and re-layouts, local(): casting_out = returned.at[slot_index].get(mode='promise_in_bounds')  4.31 us
    scatter x1, local copies, waits for them, and re-layouts, local(): send_rows = jnp.zeros((slots, row_width), bf16).at[slot_index].set(casting)  3.89 us
    all_to_all x1, starting transfers between devices, local(): lax.all_to_all(answers.reshape(devices, capacity, row_width), axes, 0, 0,...  3.81 us
  transfers between devices with their start and end apart: 3, of which 3 were waited for; matrix products, arithmetic and copies ran while one was open for 15% of the time, Pallas kernels for 0%

profile of v18, /device:TPU:0, one launch (start us, length us, event | category | flops | bytes accessed | tf_op | source)
XLA Modules:
  0.0 94.1 jit_solution(12961046741610756244)
XLA Ops:
  0.6 0.0 copy-start
  0.6 0.0 copy-start.5
  0.7 1.3 %fusion.9 = f32[1024]{0:T(1024)S(1)} fusion(s32[1024]{0:T(1024)} %bitcast.26), kind=kOutput, calls=%fused_computation.18 | convolution fusion | flops 68353024 | bytes 8192 | tf_op jit(solution)/shard_map/dot_general | solution.py:41
  2.0 0.7 fusion.39
  2.7 0.5 fusion.15
  3.2 0.9 convolution_convert_fusion
  4.1 0.0 copy-done.5
  4.1 3.9 %scatter_custom_fusion = bf16[4096,128]{1,0:T(8,128)(2,1)S(1)} fusion(s32[1024]{0:T(1024)S(1)} %bitcast.24, bf16[1024,128]{1,0:T(8,128)(2,1)} %param.8, bf16[]{:T(256)} %constant.39.clone.1), kind=kCustom, calls=%fused_computation.29 | custom fusion | bytes 1049088 | tf_op jit(solution)/shard_map/scatter | solution.py:56
  8.0 0.0 copy-start.2
  8.0 0.0 copy-start.3
  8.0 1.1 %pad_maximum_fusion = bf16[32,130,128]{2,1,0:T(8,128)(2,1)} fusion(bf16[32,2,128]{2,1,0:T(2,128)(2,1)S(1)} %convert_element_type.84, bf16[32,128,128]{2,1,0:T(8,128)(2,1)S(1)} %bitcast.19), kind=kLoop, calls=%fused_computation.19 | loop fusion | flops 2129920 | bytes 2129920 | tf_op jit(solution)/shard_map/concatenate | solution.py:57
  9.1 7.3 %all-to-all-start = ((bf16[32,130,128]{2,1,0:T(8,128)(2,1)}), bf16[32,130,128]{2,1,0:T(8,128)(2,1)S(1)}, u32[]{:S(2)}, u32[]{:S(2)}) async-start(bf16[32,130,128]{2,1,0:T(8,128)(2,1)} %pad_maximum_fusion), calls=%async_computation | async-start | bytes 2228224 | tf_op jit(solution)/shard_map/all_to_all | solution.py:60
  16.5 0.0 copy-done.2
  16.5 0.1 copy.12
  16.6 0.0 copy-done.3
  16.6 0.1 copy.13
  16.7 27.4 %all-to-all-done = bf16[32,130,128]{2,1,0:T(8,128)(2,1)S(1)} async-done(((bf16[32,130,128]{2,1,0:T(8,128)(2,1)}), bf16[32,130,128]{2,1,0:T(8,128)(2,1)S(1)}, u32[]{:S(2)}, u32[]{:S(2)}) %all-to-all-start) | async-done | bytes 1064992 | tf_op jit(solution)/shard_map/all_to_all | solution.py:60
  44.1 0.0 copy-done
  44.1 6.4 %fusion.4 = bf16[4096,128]{1,0:T(8,128)(2,1)S(1)} fusion(bf16[2048,128]{1,0:T(8,128)(2,1)S(1)} %copy-done, s32[4096]{0:T(1024)S(1)} %bitcast.22), kind=kOutput, calls=%fused_computation.8 | convolution fusion | flops 2156396544 | bytes 1589248 | tf_op jit(solution)/shard_map/dot_general | solution.py:68
  50.6 0.1 slice.26
  50.7 0.5 fusion.23
  51.2 0.5 convolution_add_fusion
  51.7 2.0 %select_convert_fusion = (bf16[4096,128]{1,0:T(8,128)(2,1)}, bf16[4096,128]{1,0:T(8,128)(2,1)}) fusion(f32[4096,128]{1,0:T(8,128)S(1)} %convolution_add_fusion, pred[128]{0:T(512)(128)(4,1)S(1)} %iota_compare_fusion.18, bf16[64,64]{1,0:T(8,128)(2,1)S(1)} %copy-done.3, bf16[64,64]{1,0:T(8,128)(2,1)S(1)} %copy-done.2, bf16[64,128]{1,0:T(8,128)(2,1)S(1)} %concatenate.43, ...), kind=kOutput, calls=%fused_computation.15 | convolution fusion | flops 137461760 | bytes 6324352 | tf_op jit(solution)/shard_map/dot_general | solution.py:78
  53.7 0.0 copy-start.1
  53.7 0.0 copy-start.4
  53.7 3.8 %all-to-all-start.1 = ((bf16[32,128,128]{2,1,0:T(8,128)(2,1)}), bf16[32,128,128]{2,1,0:T(8,128)(2,1)S(1)}, u32[]{:S(2)}, u32[]{:S(2)}) async-start(bf16[32,128,128]{2,1,0:T(8,128)(2,1)} %bitcast.8), calls=%async_computation.1 | async-start | bytes 2097152 | tf_op jit(solution)/shard_map/all_to_all | solution.py:83
  57.5 0.0 copy-done.1
  57.5 0.0 copy-done.4
  57.5 0.3 fusion.6
  57.8 8.2 %fusion.7 = bf16[2048,64]{0,1:T(8,128)(2,1)S(1)} fusion(s32[4096]{0:T(1024)S(1)} %bitcast.23, bf16[4096,128]{1,0:T(8,128)(2,1)} %get-tuple-element.15), kind=kOutput, calls=%fused_computation.13 | convolution fusion | flops 1082261504 | bytes 1327104 | tf_op jit(solution)/shard_map/dot_general | solution.py:86
  66.0 0.3 copy.14
  66.3 1.0 %reshape.58 = bf16[4,256,128]{2,1,0:T(8,128)(2,1)} reshape(bf16[2048,64]{1,0:T(8,128)(2,1)S(1)} %copy.14) | data formatting | bytes 524288 | tf_op jit(solution)/shard_map/reshape | solution.py:88
  67.2 16.3 %all-to-all-done.1 = bf16[32,128,128]{2,1,0:T(8,128)(2,1)S(1)} async-done(((bf16[32,128,128]{2,1,0:T(8,128)(2,1)}), bf16[32,128,128]{2,1,0:T(8,128)(2,1)S(1)}, u32[]{:S(2)}, u32[]{:S(2)}) %all-to-all-start.1) | async-done | bytes 1048608 | tf_op jit(solution)/shard_map/all_to_all | solution.py:83
  83.5 3.4 %all-to-all-start.2 = ((bf16[4,256,128]{2,1,0:T(8,128)(2,1)}), bf16[4,256,128]{2,1,0:T(8,128)(2,1)S(1)}, u32[]{:S(2)}, u32[]{:S(2)}) async-start(bf16[4,256,128]{2,1,0:T(8,128)(2,1)} %reshape.58), calls=%async_computation.2 | async-start | bytes 524288 | tf_op jit(solution)/shard_map/all_to_all | solution.py:92
  87.0 4.3 %gather_fusion = bf16[1024,128]{1,0:T(8,128)(2,1)} fusion(bf16[4096,128]{1,0:T(8,128)(2,1)S(1)} %bitcast.18, s32[1024]{0:T(1024)S(1)} %broadcast_clamp_fusion), kind=kCustom, calls=%fused_computation | custom fusion | bytes 528384 | tf_op jit(solution)/shard_map/gather | solution.py:90
  91.3 1.6 %all-to-all-done.2 = bf16[4,256,128]{2,1,0:T(8,128)(2,1)S(1)} async-done(((bf16[4,256,128]{2,1,0:T(8,128)(2,1)}), bf16[4,256,128]{2,1,0:T(8,128)(2,1)S(1)}, u32[]{:S(2)}, u32[]{:S(2)}) %all-to-all-start.2) | async-done | bytes 262176 | tf_op jit(solution)/shard_map/all_to_all | solution.py:92
  92.9 0.2 convert_element_type.94
  93.2 1.0 %add_convert_fusion = bf16[2048,128]{1,0:T(8,128)(2,1)} fusion(f32[2048,128]{1,0:T(8,128)S(1)} %fusion.6, bf16[2048,64]{1,0:T(8,128)(2,1)S(1)} %convert_element_type.94), kind=kLoop, calls=%fused_computation.22 | loop fusion | flops 1048576 | bytes 1835008 | tf_op jit(solution)/shard_map/convert_element_type | solution.py:104
  (11 shorter events, 0.1 us)
Async XLA Ops:
  0.6 43.5 %copy-start = (bf16[2048,128]{1,0:T(8,128)(2,1)S(1)}, bf16[2048,128]{1,0:T(8,128)(2,1)}, u32[]{:S(2)}) copy-start(bf16[2048,128]{1,0:T(8,128)(2,1)} %param.11) | copy-start | bytes 1572868
  0.6 3.4 %copy-start.5 = (s32[1024,1]{0,1:T(1,128)S(1)}, s32[1024,1]{0,1:T(1,128)}, u32[]{:S(2)}) copy-start(s32[1024,1]{0,1:T(1,128)} %param.9) | copy-start | bytes 12292
  8.0 8.5 %copy-start.2 = (bf16[64,64]{1,0:T(8,128)(2,1)S(1)}, bf16[64,64]{1,0:T(8,128)(2,1)}, u32[]{:S(2)}) copy-start(bf16[64,64]{1,0:T(8,128)(2,1)} %param.12) | copy-start | bytes 24580
  8.0 8.6 %copy-start.3 = (bf16[64,64]{1,0:T(8,128)(2,1)S(1)}, bf16[64,64]{1,0:T(8,128)(2,1)}, u32[]{:S(2)}) copy-start(bf16[64,64]{1,0:T(8,128)(2,1)} %param.13) | copy-start | bytes 24580
  9.1 34.9 %all-to-all-start = ((bf16[32,130,128]{2,1,0:T(8,128)(2,1)}), bf16[32,130,128]{2,1,0:T(8,128)(2,1)S(1)}, u32[]{:S(2)}, u32[]{:S(2)}) async-start(bf16[32,130,128]{2,1,0:T(8,128)(2,1)} %pad_maximum_fusion), calls=%async_computation | async-start | bytes 2228224 | tf_op jit(solution)/shard_map/all_to_all | solution.py:60
  53.7 3.8 %copy-start.1 = (bf16[2048,128]{1,0:T(8,128)(2,1)S(1)}, bf16[2048,128]{1,0:T(8,128)(2,1)}, u32[]{:S(2)}) copy-start(bf16[2048,128]{1,0:T(8,128)(2,1)} %param.15) | copy-start | bytes 1572868
  53.7 3.8 %copy-start.4 = (bf16[128,128]{1,0:T(8,128)(2,1)S(1)}, bf16[128,128]{1,0:T(8,128)(2,1)}, u32[]{:S(2)}) copy-start(bf16[128,128]{1,0:T(8,128)(2,1)} %param.14) | copy-start | bytes 98308
  53.7 29.8 %all-to-all-start.1 = ((bf16[32,128,128]{2,1,0:T(8,128)(2,1)}), bf16[32,128,128]{2,1,0:T(8,128)(2,1)S(1)}, u32[]{:S(2)}, u32[]{:S(2)}) async-start(bf16[32,128,128]{2,1,0:T(8,128)(2,1)} %bitcast.8), calls=%async_computation.1 | async-start | bytes 2097152 | tf_op jit(solution)/shard_map/all_to_all | solution.py:83
  83.5 9.4 %all-to-all-start.2 = ((bf16[4,256,128]{2,1,0:T(8,128)(2,1)}), bf16[4,256,128]{2,1,0:T(8,128)(2,1)S(1)}, u32[]{:S(2)}, u32[]{:S(2)}) async-start(bf16[4,256,128]{2,1,0:T(8,128)(2,1)} %reshape.58), calls=%async_computation.2 | async-start | bytes 524288 | tf_op jit(solution)/shard_map/all_to_all | solution.py:92

commit v19 on v13

--- a/solution.py
+++ b/solution.py
@@ -37,9 +37,8 @@
     hits = (target[:, None] == jnp.arange(devices, dtype=jnp.int32)[None, :]).astype(bf16)
     row_i = lax.broadcasted_iota(jnp.int32, (seg_rows, seg_rows), 0)
     row_j = lax.broadcasted_iota(jnp.int32, (seg_rows, seg_rows), 1)
-    earlier = (row_j < row_i).astype(bf16)
-    before = jnp.dot(earlier, hits, preferred_element_type=f32)
-    position = jnp.sum(before * hits.astype(f32), axis=1).astype(jnp.int32)
+    same = (row_j < row_i) & (target[None, :] == target[:, None])
+    position = jnp.sum(same.astype(jnp.int32), axis=1)
     slot_index = target * capacity + position
 
     code = face_id + 1

time: 94.6 us -> 95.5 us (level)
  other arithmetic: 3.31 us -> 5.27 us
  matrix products: 20 us -> 18.9 us
    dot_general x1 -> x0, matrix products: 1.32 us -> none  [local(): before = jnp.dot(earlier, hits, preferred_element_type=f32)]
    reduce_sum x0 -> x1, other arithmetic: none -> 1.28 us  [local(): position = jnp.sum(same.astype(jnp.int32), axis=1)]
where the time goes in v19:
time: 95.5 us; the launch traced here: 95 us
  waiting for transfers between devices  45.3 us (47%)
  matrix products  18.9 us (20%)
  starting transfers between devices  14.5 us (15%)
  local copies, waits for them, and re-layouts  10.1 us (11%)
  other arithmetic  5.27 us (6%)
    all_to_all x1, waiting for transfers between devices, local(): got = lax.all_to_all(send, axes, 0, 0, tiled=True)  27.4 us
    all_to_all x1, waiting for transfers between devices, local(): lax.all_to_all(answers.reshape(devices, capacity, row_width), axes, 0, 0,...  16.3 us
    dot_general x1, matrix products, local(): lax.dot_general(selector, gained, contract0, preferred_element_type=f32)  8.16 us
    all_to_all x1, starting transfers between devices, local(): got = lax.all_to_all(send, axes, 0, 0, tiled=True)  7.33 us
    dot_general x1, matrix products, local(): jnp.dot(selector, mold_faces, preferred_element_type=f32).astype(bf16)  6.44 us
    gather x1, local copies, waits for them, and re-layouts, local(): casting_out = jnp.take(returned, slot_index, axis=0, mode='clip')  4.31 us
    scatter x1, local copies, waits for them, and re-layouts, local(): send_rows = jnp.zeros((slots, row_width), bf16).at[slot_index].set(casting)  3.89 us
    all_to_all x1, starting transfers between devices, local(): lax.all_to_all(answers.reshape(devices, capacity, row_width), axes, 0, 0,...  3.8 us
  transfers between devices with their start and end apart: 3, of which 3 were waited for; matrix products, arithmetic and copies ran while one was open for 15% of the time, Pallas kernels for 0%

profile of v19, /device:TPU:0, one launch (start us, length us, event | category | flops | bytes accessed | tf_op | source)
XLA Modules:
  0.0 95.0 jit_solution(6566878522147177752)
XLA Ops:
  0.6 0.0 copy-start
  0.6 1.3 %convert_reduce_fusion = s32[1024]{0:T(1024)S(1)} fusion(s32[1024]{0:T(1024)} %bitcast.26), kind=kLoop, calls=%fused_computation.9 | loop fusion | flops 5241856 | bytes 8192 | tf_op jit(solution)/shard_map/reduce_sum | solution.py:41
  1.9 0.7 fusion.35
  2.6 0.5 fusion.13
  3.1 1.1 %convolution_convert_fusion = bf16[32,256]{1,0:T(8,128)(2,1)S(1)} fusion(bf16[1024,128]{1,0:T(8,128)(2,1)S(1)} %get-tuple-element.13, bf16[1024,128]{1,0:T(8,128)(2,1)S(1)} %get-tuple-element.12, s32[1024]{0:T(1024)} %bitcast.27), kind=kOutput, calls=%fused_computation.19 | convolution fusion | flops 17866752 | bytes 544768 | tf_op jit(solution)/shard_map/dot_general | solution.py:51
  4.3 0.7 compare_select_fusion
  5.0 3.9 %scatter_custom_fusion = bf16[4096,128]{1,0:T(8,128)(2,1)S(1)} fusion(s32[1024]{0:T(1024)S(1)} %bitcast.28, bf16[1024,128]{1,0:T(8,128)(2,1)} %param.8, bf16[]{:T(256)} %constant.38.clone.1), kind=kCustom, calls=%fused_computation.29 | custom fusion | bytes 1049088 | tf_op jit(solution)/shard_map/scatter | solution.py:55
  8.9 0.0 copy-start.2
  8.9 0.0 copy-start.3
  8.9 1.1 %pad_maximum_fusion = bf16[32,130,128]{2,1,0:T(8,128)(2,1)} fusion(bf16[32,2,128]{2,1,0:T(2,128)(2,1)S(1)} %convert_element_type.63, bf16[32,128,128]{2,1,0:T(8,128)(2,1)S(1)} %bitcast.20), kind=kLoop, calls=%fused_computation.18 | loop fusion | flops 2129920 | bytes 2129920 | tf_op jit(solution)/shard_map/concatenate | solution.py:56
  10.0 7.3 %all-to-all-start = ((bf16[32,130,128]{2,1,0:T(8,128)(2,1)}), bf16[32,130,128]{2,1,0:T(8,128)(2,1)S(1)}, u32[]{:S(2)}, u32[]{:S(2)}) async-start(bf16[32,130,128]{2,1,0:T(8,128)(2,1)} %pad_maximum_fusion), calls=%async_computation | async-start | bytes 2228224 | tf_op jit(solution)/shard_map/all_to_all | solution.py:59
  17.3 0.0 copy-done.2
  17.3 0.1 copy.15
  17.4 0.0 copy-done.3
  17.5 0.1 copy.16
  17.6 27.4 %all-to-all-done = bf16[32,130,128]{2,1,0:T(8,128)(2,1)S(1)} async-done(((bf16[32,130,128]{2,1,0:T(8,128)(2,1)}), bf16[32,130,128]{2,1,0:T(8,128)(2,1)S(1)}, u32[]{:S(2)}, u32[]{:S(2)}) %all-to-all-start) | async-done | bytes 1064992 | tf_op jit(solution)/shard_map/all_to_all | solution.py:59
  45.0 0.0 copy-done
  45.0 6.4 %fusion.4 = bf16[4096,128]{1,0:T(8,128)(2,1)S(1)} fusion(bf16[2048,128]{1,0:T(8,128)(2,1)S(1)} %copy-done, s32[4096]{0:T(1024)S(1)} %bitcast.23), kind=kOutput, calls=%fused_computation.8 | convolution fusion | flops 2156396544 | bytes 1589248 | tf_op jit(solution)/shard_map/dot_general | solution.py:67
  51.4 0.1 slice.26
  51.6 0.5 fusion.19
  52.1 0.5 convolution_add_fusion
  52.6 2.0 %select_convert_fusion = (bf16[4096,128]{1,0:T(8,128)(2,1)}, bf16[4096,128]{1,0:T(8,128)(2,1)}) fusion(f32[4096,128]{1,0:T(8,128)S(1)} %convolution_add_fusion, pred[128]{0:T(512)(128)(4,1)S(1)} %iota_compare_fusion.12, bf16[64,64]{1,0:T(8,128)(2,1)S(1)} %copy-done.3, bf16[64,64]{1,0:T(8,128)(2,1)S(1)} %copy-done.2, bf16[64,128]{1,0:T(8,128)(2,1)S(1)} %concatenate.43, ...), kind=kOutput, calls=%fused_computation.16 | convolution fusion | flops 137461760 | bytes 6324352 | tf_op jit(solution)/shard_map/dot_general | solution.py:77
  54.6 0.0 copy-start.1
  54.6 0.0 copy-start.4
  54.6 3.8 %all-to-all-start.1 = ((bf16[32,128,128]{2,1,0:T(8,128)(2,1)}), bf16[32,128,128]{2,1,0:T(8,128)(2,1)S(1)}, u32[]{:S(2)}, u32[]{:S(2)}) async-start(bf16[32,128,128]{2,1,0:T(8,128)(2,1)} %bitcast.8), calls=%async_computation.1 | async-start | bytes 2097152 | tf_op jit(solution)/shard_map/all_to_all | solution.py:82
  58.4 0.0 copy-done.1
  58.4 0.0 copy-done.4
  58.4 0.3 fusion.6
  58.7 8.2 %fusion.7 = bf16[2048,64]{0,1:T(8,128)(2,1)S(1)} fusion(s32[4096]{0:T(1024)S(1)} %bitcast.24, bf16[4096,128]{1,0:T(8,128)(2,1)} %get-tuple-element.17), kind=kOutput, calls=%fused_computation.14 | convolution fusion | flops 1082261504 | bytes 1327104 | tf_op jit(solution)/shard_map/dot_general | solution.py:85
  66.8 0.3 copy.17
  67.1 1.0 %reshape.53 = bf16[4,256,128]{2,1,0:T(8,128)(2,1)} reshape(bf16[2048,64]{1,0:T(8,128)(2,1)S(1)} %copy.17) | data formatting | bytes 524288 | tf_op jit(solution)/shard_map/reshape | solution.py:87
  68.1 16.3 %all-to-all-done.1 = bf16[32,128,128]{2,1,0:T(8,128)(2,1)S(1)} async-done(((bf16[32,128,128]{2,1,0:T(8,128)(2,1)}), bf16[32,128,128]{2,1,0:T(8,128)(2,1)S(1)}, u32[]{:S(2)}, u32[]{:S(2)}) %all-to-all-start.1) | async-done | bytes 1048608 | tf_op jit(solution)/shard_map/all_to_all | solution.py:82
  84.4 3.4 %all-to-all-start.2 = ((bf16[4,256,128]{2,1,0:T(8,128)(2,1)}), bf16[4,256,128]{2,1,0:T(8,128)(2,1)S(1)}, u32[]{:S(2)}, u32[]{:S(2)}) async-start(bf16[4,256,128]{2,1,0:T(8,128)(2,1)} %reshape.53), calls=%async_computation.2 | async-start | bytes 524288 | tf_op jit(solution)/shard_map/all_to_all | solution.py:91
  87.8 4.3 %gather_fusion = bf16[1024,128]{1,0:T(8,128)(2,1)} fusion(bf16[4096,128]{1,0:T(8,128)(2,1)S(1)} %bitcast.19, s32[1024]{0:T(1024)S(1)} %broadcast_clamp_fusion), kind=kCustom, calls=%fused_computation | custom fusion | bytes 528384 | tf_op jit(solution)/shard_map/jit(_take)/gather | solution.py:89
  92.1 1.6 %all-to-all-done.2 = bf16[4,256,128]{2,1,0:T(8,128)(2,1)S(1)} async-done(((bf16[4,256,128]{2,1,0:T(8,128)(2,1)}), bf16[4,256,128]{2,1,0:T(8,128)(2,1)S(1)}, u32[]{:S(2)}, u32[]{:S(2)}) %all-to-all-start.2) | async-done | bytes 262176 | tf_op jit(solution)/shard_map/all_to_all | solution.py:91
  93.8 0.2 convert_element_type.73
  94.0 1.0 %add_convert_fusion = bf16[2048,128]{1,0:T(8,128)(2,1)} fusion(f32[2048,128]{1,0:T(8,128)S(1)} %fusion.6, bf16[2048,64]{1,0:T(8,128)(2,1)S(1)} %convert_element_type.73), kind=kLoop, calls=%fused_computation.21 | loop fusion | flops 1048576 | bytes 1835008 | tf_op jit(solution)/shard_map/convert_element_type | solution.py:103
  (9 shorter events, 0.1 us)
Async XLA Ops:
  0.6 44.4 %copy-start = (bf16[2048,128]{1,0:T(8,128)(2,1)S(1)}, bf16[2048,128]{1,0:T(8,128)(2,1)}, u32[]{:S(2)}) copy-start(bf16[2048,128]{1,0:T(8,128)(2,1)} %param.11) | copy-start | bytes 1572868
  8.9 8.5 %copy-start.2 = (bf16[64,64]{1,0:T(8,128)(2,1)S(1)}, bf16[64,64]{1,0:T(8,128)(2,1)}, u32[]{:S(2)}) copy-start(bf16[64,64]{1,0:T(8,128)(2,1)} %param.12) | copy-start | bytes 24580
  8.9 8.6 %copy-start.3 = (bf16[64,64]{1,0:T(8,128)(2,1)S(1)}, bf16[64,64]{1,0:T(8,128)(2,1)}, u32[]{:S(2)}) copy-start(bf16[64,64]{1,0:T(8,128)(2,1)} %param.13) | copy-start | bytes 24580
  10.0 34.9 %all-to-all-start = ((bf16[32,130,128]{2,1,0:T(8,128)(2,1)}), bf16[32,130,128]{2,1,0:T(8,128)(2,1)S(1)}, u32[]{:S(2)}, u32[]{:S(2)}) async-start(bf16[32,130,128]{2,1,0:T(8,128)(2,1)} %pad_maximum_fusion), calls=%async_computation | async-start | bytes 2228224 | tf_op jit(solution)/shard_map/all_to_all | solution.py:59
  54.6 3.8 %copy-start.1 = (bf16[2048,128]{1,0:T(8,128)(2,1)S(1)}, bf16[2048,128]{1,0:T(8,128)(2,1)}, u32[]{:S(2)}) copy-start(bf16[2048,128]{1,0:T(8,128)(2,1)} %param.15) | copy-start | bytes 1572868
  54.6 3.8 %copy-start.4 = (bf16[128,128]{1,0:T(8,128)(2,1)S(1)}, bf16[128,128]{1,0:T(8,128)(2,1)}, u32[]{:S(2)}) copy-start(bf16[128,128]{1,0:T(8,128)(2,1)} %param.14) | copy-start | bytes 98308
  54.6 29.8 %all-to-all-start.1 = ((bf16[32,128,128]{2,1,0:T(8,128)(2,1)}), bf16[32,128,128]{2,1,0:T(8,128)(2,1)S(1)}, u32[]{:S(2)}, u32[]{:S(2)}) async-start(bf16[32,128,128]{2,1,0:T(8,128)(2,1)} %bitcast.8), calls=%async_computation.1 | async-start | bytes 2097152 | tf_op jit(solution)/shard_map/all_to_all | solution.py:82
  84.4 9.4 %all-to-all-start.2 = ((bf16[4,256,128]{2,1,0:T(8,128)(2,1)}), bf16[4,256,128]{2,1,0:T(8,128)(2,1)S(1)}, u32[]{:S(2)}, u32[]{:S(2)}) async-start(bf16[4,256,128]{2,1,0:T(8,128)(2,1)} %reshape.53), calls=%async_computation.2 | async-start | bytes 524288 | tf_op jit(solution)/shard_map/all_to_all | solution.py:91
